TPU v7x, 32 devices: a whole 2x2x4 slice. The times are simulated.
32 devices in a mesh: grp: 2 (over y), blk: 8 (over z, x), tch: 2 (over core).
Axes of the slice: x: 2, y: 2, z: 4, core: 2. Of those that a mesh axis runs over, the one named last changes fastest.
Arguments:
- samples: bfloat16 [4, 32, 65536], P('grp', 'blk', 'tch'), parts along dimension 0, may hold values from -6 to 6
- history: bfloat16 [4, 32, 15360], P('grp', 'blk'), parts along dimension 0, may hold values from -6 to 6
- coefficients: float32 [16, 1024], replicated, may hold values from -1.5 to 1.5
- station_of_slot: int32 [32], P('grp'), parts along dimension 0, may hold values from 0 to 15, each once
- station_ok: int32 [32], P('grp'), parts along dimension 0, may hold values from 0 to 1, as said below
Outputs:
- visibilities: bfloat16 [4, 1024, 32, 32], P('grp', ('blk', 'tch')), parts along dimension 0
There are 2 independent parts, one for each index of `grp`. A program takes and returns all parts, laid end to end along the dimension named above; an argument that names none is the same for every part. Nothing has to cross between parts.
Inputs may be any that keep to these rules, and one draw needn't show every extreme that they name: `station_of_slot`: each station stands in exactly one slot. `station_ok`: 2 or 3 stations are flagged.
All inputs are finite; a program needn't handle non-finite values.
Results may differ from a plain program's by a relative error of at most 0.0074.
Values may be sent and summed in bfloat16 or wider, within the bound.
No kernel may reach another device: no remote copies, remote signals or barrier semaphores. Data moves between devices by JAX's collectives and lax.ppermute only.
A program may use at most 64 MiB of HBM per device.

v0:
```python
import math

import jax
import jax.numpy as jnp
from jax import lax
from jax.sharding import PartitionSpec as P

POLS = 2


def shifted(block, axis, distance):
    devices = range(lax.axis_size(axis))
    route = [(i - distance, i) for i in devices if i - distance in devices]
    return lax.ppermute(block, axis, route)


def dft_table(fft_len):
    row_index = lax.broadcasted_iota(jnp.int32, (fft_len, fft_len), 0)
    col_index = lax.broadcasted_iota(jnp.int32, (fft_len, fft_len), 1)
    phase_step = row_index * col_index % fft_len
    angles = phase_step.astype(jnp.float32) * (2.0 * math.pi / fft_len)
    norm_scale = 1.0 / math.sqrt(fft_len)
    cosine = jnp.cos(angles) * norm_scale
    sine_part = jnp.sin(angles) * norm_scale
    upper_half = jnp.concatenate([cosine, -sine_part], axis=1)
    lower_half = jnp.concatenate([sine_part, cosine], axis=1)
    return jnp.concatenate([upper_half, lower_half], axis=0).astype(jnp.bfloat16)


def filter_bank(extended, coefficients, spec_count):
    tap_count, fft_len = coefficients.shape
    blocks = extended.reshape(extended.shape[0], extended.shape[1], -1, fft_len)
    running = jnp.zeros((extended.shape[0], extended.shape[1], spec_count, fft_len), jnp.float32)
    for tap_index in range(tap_count):
        running = running + coefficients[tap_index] * blocks[
            :, :, tap_index : tap_index + spec_count, :
        ].astype(jnp.float32)
    return running.astype(jnp.bfloat16)


def channel_major(filtered, dft_matrix):
    row_count, spec_count, fft_len = (filtered.shape[1], filtered.shape[2], filtered.shape[3])
    flat_rows = jnp.transpose(filtered, (1, 2, 0, 3)).reshape(row_count * spec_count, 2 * fft_len)
    product = jnp.dot(flat_rows, dft_matrix, preferred_element_type=jnp.float32).astype(
        jnp.bfloat16
    )
    product = product.reshape(row_count, spec_count, 2, fft_len)
    return jnp.transpose(product, (3, 0, 2, 1)).reshape(fft_len, row_count * 2 * spec_count)


def reorder_inputs(values, station_of_slot, station_ok):
    station_count = station_of_slot.shape[0]
    input_count = values.shape[1]
    slot_index = (
        jnp.zeros((station_count,), jnp.int32)
        .at[station_of_slot]
        .set(jnp.arange(station_count, dtype=jnp.int32))
    )
    position = jnp.arange(input_count, dtype=jnp.int32)
    source_rows = slot_index[position // POLS] * POLS + position % POLS
    keep_mask = station_ok[position // POLS].astype(values.dtype)
    return jnp.take(values, source_rows, axis=1) * keep_mask[None, :, None]


def rotate_parts(ordered):
    half_cols = ordered.shape[2] // 2
    return jnp.concatenate([-ordered[:, :, half_cols:], ordered[:, :, :half_cols]], axis=2)


def correlate_full(ordered, inverse_count):
    rotated = rotate_parts(ordered)
    real_vis = jnp.einsum("cak,cbk->cab", ordered, ordered, preferred_element_type=jnp.float32)
    imag_vis = jnp.einsum("cak,cbk->cab", ordered, rotated, preferred_element_type=jnp.float32)
    return (jnp.stack([real_vis, imag_vis], axis=0) * inverse_count).astype(jnp.bfloat16)


def local(samples, history, coefficients, station_of_slot, station_ok):
    tap_count, fft_len = coefficients.shape
    row_count = samples.shape[1]
    spec_local = samples.shape[2] // fft_len
    half_count = lax.axis_size("tch")
    block_count = lax.axis_size("blk")
    spec_total = spec_local * half_count
    dft_matrix = dft_table(fft_len)
    tail_block = jnp.concatenate([history, samples], axis=2)[:, :, -(tap_count - 1) * fft_len :]
    earlier = shifted(tail_block, "tch", 1)
    is_first = lax.axis_index("tch") == 0
    earlier = jnp.where(is_first, history, earlier)
    extended = jnp.concatenate([earlier, samples], axis=2)
    by_channel = channel_major(filter_bank(extended, coefficients, spec_local), dft_matrix)
    by_block = lax.all_to_all(by_channel, "blk", split_axis=0, concat_axis=1, tiled=True)
    turned = lax.all_to_all(by_block, "tch", split_axis=0, concat_axis=1, tiled=True)
    chan_local = turned.shape[0]
    layout = turned.reshape(chan_local, half_count, block_count, row_count, 2, spec_local)
    layout = jnp.transpose(layout, (0, 2, 3, 4, 1, 5))
    stacked = layout.reshape(chan_local, block_count * row_count, 2 * spec_total)
    ordered = reorder_inputs(stacked, station_of_slot, station_ok)
    inverse_count = 1.0 / spec_total
    return correlate_full(ordered, inverse_count)


def solution(mesh):
    return jax.shard_map(
        local,
        mesh=mesh,
        in_specs=(P("grp", "blk", "tch"), P("grp", "blk", None), P(), P("grp"), P("grp")),
        out_specs=P("grp", ("blk", "tch"), None, None),
        check_vma=False,
    )
```

profile of v0, /device:TPU:0, one launch (start us, length us, event | category | flops | bytes accessed | tf_op | source)
XLA Modules:
  0.0 76.3 jit_solution(1272274682949165277)
XLA Ops:
  0.0 0.0 copy-start
  0.0 1.0 %slice.106 = bf16[2,4,15360]{2,1,0:T(4,128)(2,1)S(1)} slice(bf16[2,4,32768]{2,1,0:T(4,128)(2,1)} %param.5), slice={[0:2], [0:4], [17408:32768]} | slice | bytes 491520 | tf_op jit(solution)/shard_map/slice | solution.py:85
  1.0 2.4 %collective-permute-start = (bf16[2,4,15360]{2,1,0:T(4,128)(2,1)S(1)}, bf16[2,4,15360]{2,1,0:T(4,128)(2,1)S(1)}, u32[]{:S(2)}, u32[]{:S(2)}) collective-permute-start(bf16[2,4,15360]{2,1,0:T(4,128)(2,1)S(1)} %slice.106), channel_id=1, source_target_pairs={{0,1},{2,3},{4,5},{6,7},{8,9},{10,11},{12,13},{14,15},{16,17},{18,... | collective-permute-start | bytes 737288 | tf_op jit(solution)/shard_map/ppermute | solution.py:14
  3.4 17.9 %negate_convert_fusion = (bf16[1024,1024]{1,0:T(8,128)(2,1)}, bf16[1024,1024]{1,0:T(8,128)(2,1)}) fusion(), kind=kLoop, calls=%fused_computation.18 | loop fusion | flops 19922944 | bytes 4194304 | tf_op jit(solution)/shard_map/convert.5
  21.4 0.0 copy-start.6
  21.4 0.0 copy-start.5
  21.4 0.0 copy-start.4
  21.4 16.6 %fusion.14 = bf16[1024,1024]{1,0:T(8,128)(2,1)} fusion(), kind=kLoop, calls=%fused_computation.24 | loop fusion | flops 16777216 | bytes 2097152 | tf_op jit(solution)/shard_map/convert.2
  37.9 0.0 copy-done.6
  38.0 0.0 collective-permute-done
  38.0 0.0 copy-done.5
  38.0 0.0 copy-done.4
  38.1 0.3 pad_maximum_fusion
  38.4 0.5 reshape.130
  38.9 0.0 copy-start.2
  38.9 0.0 copy-start.3
  38.9 2.2 %fusion.25 = bf16[4,32,2,1024]{3,1,0,2:T(8,128)(2,1)S(1)} fusion(bf16[2,4,47,1024]{3,2,1,0:T(8,128)(2,1)S(1)} %reshape.130, f32[1024]{0:T(1024)S(1)} %bitcast.78, f32[1024]{0:T(1024)S(1)} %bitcast.79, f32[1024]{0:T(1024)S(1)} %bitcast.65, f32[1024]{0:T(1024)S(1)} %bitcast.66, f32[1024]{0:T(1024)S(1)} %bitcast.67, f32[1024]{0:T(1024)S(1)} %bitcast.68, ...), kind=kLoop, calls=%fused_computation.38 | loop fusion | flops 12582912 | bytes 8978432 | tf_op jit(solution)/shard_map/transpose | solution.py:43
  41.2 0.0 copy-start.1
  41.2 0.5 copy.24
  41.7 0.1 copy.34
  41.8 0.0 copy-done.2
  41.8 0.0 copy-done.3
  41.9 0.9 %copy-done.1 = bf16[1024,1024]{1,0:T(8,128)(2,1)S(1)} copy-done((bf16[1024,1024]{1,0:T(8,128)(2,1)S(1)}, bf16[1024,1024]{1,0:T(8,128)(2,1)}, u32[]{:S(2)}) %copy-start.1) | copy-done | bytes 2097176
  42.7 1.3 %fusion.15 = bf16[128,2048]{1,0:T(8,128)(2,1)S(1)} fusion(bf16[128,2048]{1,0:T(8,128)(2,1)S(1)} %bitcast.61, bf16[1024,1024]{1,0:T(8,128)(2,1)S(1)} %copy-done.2, bf16[1024,1024]{1,0:T(8,128)(2,1)S(1)} %copy-done.3, bf16[1024,1024]{1,0:T(8,128)(2,1)S(1)} %copy-done.1), kind=kOutput, calls=%fused_computation.25 | convolution fusion | flops 1107558400 | bytes 7340032 | tf_op jit(solution)/shard_map/dot_general | solution.py:44
  44.0 0.4 reshape.132
  44.4 0.0 copy-start.7
  44.4 0.1 copy.25
  44.5 0.1 copy.35
  44.6 0.9 %copy.26 = bf16[8,128,256]{1,2,0:T(8,128)(2,1)} copy(bf16[8,128,256]{1,0,2:T(8,128)(2,1)S(1)} %bitcast.59) | data formatting | bytes 1048576 | tf_op jit(solution)/shard_map/all_to_all | solution.py:91
  45.5 6.6 %all-to-all-start = ((bf16[8,128,256]{1,2,0:T(8,128)(2,1)}), bf16[8,128,256]{1,2,0:T(8,128)(2,1)S(1)}, u32[]{:S(2)}, u32[]{:S(2)}) async-start(bf16[8,128,256]{1,2,0:T(8,128)(2,1)} %copy.26), calls=%async_computation | async-start | bytes 1048576 | tf_op jit(solution)/shard_map/all_to_all | solution.py:91
  52.1 0.0 copy-done.7
  52.2 0.6 scatter_custom_fusion
  52.8 0.7 gather_fusion
  53.5 0.0 copy-done
  53.5 0.7 gather_fusion.2
  54.3 11.9 %all-to-all-done = bf16[8,128,256]{1,2,0:T(8,128)(2,1)S(1)} async-done(((bf16[8,128,256]{1,2,0:T(8,128)(2,1)}), bf16[8,128,256]{1,2,0:T(8,128)(2,1)S(1)}, u32[]{:S(2)}, u32[]{:S(2)}) %all-to-all-start) | async-done | bytes 524320 | tf_op jit(solution)/shard_map/all_to_all | solution.py:91
  66.2 0.4 copy.27
  66.6 0.2 all_to_all.27
  66.9 4.2 %all_to_all.32 = bf16[2,64,2048]{2,1,0:T(8,128)(2,1)S(1)} all-to-all(bf16[2,64,2048]{2,1,0:T(8,128)(2,1)S(1)} %all_to_all.27), channel_id=1, replica_groups=mesh['grp'=2,'blk'=8,'tch'=2] {'tch'}, dimensions={0} | all-to-all | bytes 1048576 | tf_op jit(solution)/shard_map/all_to_all | solution.py:92
  71.0 0.5 copy.28
  71.5 0.1 copy.29
  71.7 0.4 copy.30
  72.1 0.7 gather_fusion.1
  72.8 0.3 fusion.24
  73.1 0.2 slice_negate_fusion
  73.4 0.4 fusion.35
  73.7 0.5 fusion.19
  74.2 0.6 copy.33
  74.8 0.6 copy.32
  75.4 0.9 %fusion.18 = bf16[2,64,32,32]{1,3,2,0:T(8,128)(2,1)} fusion(f32[1,64,32,32]{1,3,2,0:T(8,128)S(1)} %bitcast.53, f32[1,64,32,32]{1,3,2,0:T(8,128)S(1)} %bitcast.54), kind=kLoop, calls=%fused_computation.27 | loop fusion | flops 393216 | bytes 786432 | tf_op jit(solution)/shard_map/convert_element_type | solution.py:74
  (10 shorter events, 0.1 us)
Async XLA Ops:
  0.0 53.5 %copy-start = (s32[16]{0:T(128)S(1)}, s32[16]{0:T(128)}, u32[]{:S(2)}) copy-start(s32[16]{0:T(128)} %param.9) | copy-start | bytes 196
  1.0 36.9 %collective-permute-start = (bf16[2,4,15360]{2,1,0:T(4,128)(2,1)S(1)}, bf16[2,4,15360]{2,1,0:T(4,128)(2,1)S(1)}, u32[]{:S(2)}, u32[]{:S(2)}) collective-permute-start(bf16[2,4,15360]{2,1,0:T(4,128)(2,1)S(1)} %slice.106), channel_id=1, source_target_pairs={{0,1},{2,3},{4,5},{6,7},{8,9},{10,11},{12,13},{14,15},{16,17},{18,... | collective-permute-start | bytes 737288 | tf_op jit(solution)/shard_map/ppermute | solution.py:14
  21.4 16.6 %copy-start.6 = (f32[16,1024]{1,0:T(8,128)S(1)}, f32[16,1024]{1,0:T(8,128)}, u32[]{:S(2)}) copy-start(f32[16,1024]{1,0:T(8,128)} %param.7) | copy-start | bytes 196612
  21.4 16.6 %copy-start.5 = (bf16[2,4,15360]{2,1,0:T(4,128)(2,1)S(1)}, bf16[2,4,15360]{2,1,0:T(4,128)(2,1)}, u32[]{:S(2)}) copy-start(bf16[2,4,15360]{2,1,0:T(4,128)(2,1)} %param.6) | copy-start | bytes 737284
  21.4 16.7 %copy-start.4 = (bf16[2,4,32768]{2,1,0:T(4,128)(2,1)S(1)}, bf16[2,4,32768]{2,1,0:T(4,128)(2,1)}, u32[]{:S(2)}) copy-start(bf16[2,4,32768]{2,1,0:T(4,128)(2,1)} %param.5) | copy-start | bytes 1572868
  38.9 2.9 %copy-start.2 = (bf16[1024,1024]{1,0:T(8,128)(2,1)S(1)}, bf16[1024,1024]{1,0:T(8,128)(2,1)}, u32[]{:S(2)}) copy-start(bf16[1024,1024]{1,0:T(8,128)(2,1)} %get-tuple-element.24) | copy-start | bytes 6291460
  38.9 2.9 %copy-start.3 = (bf16[1024,1024]{1,0:T(8,128)(2,1)S(1)}, bf16[1024,1024]{1,0:T(8,128)(2,1)}, u32[]{:S(2)}) copy-start(bf16[1024,1024]{1,0:T(8,128)(2,1)} %fusion.14) | copy-start | bytes 6291460
  41.2 1.6 %copy-start.1 = (bf16[1024,1024]{1,0:T(8,128)(2,1)S(1)}, bf16[1024,1024]{1,0:T(8,128)(2,1)}, u32[]{:S(2)}) copy-start(bf16[1024,1024]{1,0:T(8,128)(2,1)} %get-tuple-element.23) | copy-start | bytes 6291460
  44.4 7.8 %copy-start.7 = (s32[16]{0:T(128)S(1)}, s32[16]{0:T(128)}, u32[]{:S(2)}) copy-start(s32[16]{0:T(128)} %param.8) | copy-start | bytes 196
  45.5 20.7 %all-to-all-start = ((bf16[8,128,256]{1,2,0:T(8,128)(2,1)}), bf16[8,128,256]{1,2,0:T(8,128)(2,1)S(1)}, u32[]{:S(2)}, u32[]{:S(2)}) async-start(bf16[8,128,256]{1,2,0:T(8,128)(2,1)} %copy.26), calls=%async_computation | async-start | bytes 1048576 | tf_op jit(solution)/shard_map/all_to_all | solution.py:91
where the time goes:
time: 76.6 us; the launch traced here: 76.3 us
  other arithmetic  38.6 us (50%)
  waiting for transfers between devices  11.9 us (16%)
  local copies, waits for them, and re-layouts  10.2 us (13%)
  starting transfers between devices  9 us (12%)
  blocking collectives  4.15 us (5%)
  matrix products  2.12 us (3%)
    another operation x2, other arithmetic  34.5 us
    all_to_all x1, waiting for transfers between devices, local(): lax.all_to_all(by_channel, 'blk', split_axis=0, concat_axis=1, tiled=True)  11.9 us
    all_to_all x1, starting transfers between devices, local(): lax.all_to_all(by_channel, 'blk', split_axis=0, concat_axis=1, tiled=True)  6.63 us
    all_to_all x1, blocking collectives, local(): lax.all_to_all(by_block, 'tch', split_axis=0, concat_axis=1, tiled=True)  4.15 us
    ppermute x1, starting transfers between devices, shifted(): return lax.ppermute(block, axis, route)  2.37 us
    transpose x1, other arithmetic, channel_major(): jnp.transpose(filtered, (1, 2, 0, 3))  2.23 us
  transfers between devices with their start and end apart: 2, of which 1 were waited for; matrix products, arithmetic and copies ran while one was open for 48% of the time, Pallas kernels for 0%

commit v1 on v0

--- a/solution.py
+++ b/solution.py
@@ -1,4 +1,6 @@
 import math
+
+import numpy as np
 
 import jax
 import jax.numpy as jnp
@@ -6,6 +8,7 @@
 from jax.sharding import PartitionSpec as P
 
 POLS = 2
+RADIX = 4
 
 
 def shifted(block, axis, distance):
@@ -14,17 +17,21 @@
     return lax.ppermute(block, axis, route)
 
 
-def dft_table(fft_len):
-    row_index = lax.broadcasted_iota(jnp.int32, (fft_len, fft_len), 0)
-    col_index = lax.broadcasted_iota(jnp.int32, (fft_len, fft_len), 1)
-    phase_step = row_index * col_index % fft_len
-    angles = phase_step.astype(jnp.float32) * (2.0 * math.pi / fft_len)
-    norm_scale = 1.0 / math.sqrt(fft_len)
-    cosine = jnp.cos(angles) * norm_scale
-    sine_part = jnp.sin(angles) * norm_scale
-    upper_half = jnp.concatenate([cosine, -sine_part], axis=1)
-    lower_half = jnp.concatenate([sine_part, cosine], axis=1)
-    return jnp.concatenate([upper_half, lower_half], axis=0).astype(jnp.bfloat16)
+def dft_tables(fft_len):
+    inner = fft_len // RADIX
+    n2 = np.arange(inner)
+    k1 = np.arange(RADIX)
+    tw_angle = 2.0 * np.pi * np.outer(k1, n2) / fft_len
+    twiddle_re = np.cos(tw_angle).astype(np.float32)
+    twiddle_im = (-np.sin(tw_angle)).astype(np.float32)
+    angle = 2.0 * np.pi * (np.outer(n2, n2) % inner) / inner
+    scale = 1.0 / math.sqrt(fft_len)
+    cosine = np.cos(angle) * scale
+    sine_part = np.sin(angle) * scale
+    upper_half = np.concatenate([cosine, -sine_part], axis=1)
+    lower_half = np.concatenate([sine_part, cosine], axis=1)
+    inner_matrix = np.concatenate([upper_half, lower_half], axis=0).astype(np.float32)
+    return twiddle_re, twiddle_im, inner_matrix
 
 
 def filter_bank(extended, coefficients, spec_count):
@@ -38,14 +45,32 @@
     return running.astype(jnp.bfloat16)
 
 
-def channel_major(filtered, dft_matrix):
-    row_count, spec_count, fft_len = (filtered.shape[1], filtered.shape[2], filtered.shape[3])
-    flat_rows = jnp.transpose(filtered, (1, 2, 0, 3)).reshape(row_count * spec_count, 2 * fft_len)
-    product = jnp.dot(flat_rows, dft_matrix, preferred_element_type=jnp.float32).astype(
-        jnp.bfloat16
-    )
-    product = product.reshape(row_count, spec_count, 2, fft_len)
-    return jnp.transpose(product, (3, 0, 2, 1)).reshape(fft_len, row_count * 2 * spec_count)
+def channelize(filtered):
+    _, row_count, spec_count, fft_len = filtered.shape
+    inner = fft_len // RADIX
+    twiddle_re, twiddle_im, inner_matrix = dft_tables(fft_len)
+    x = filtered.astype(jnp.float32).reshape(2, row_count, spec_count, RADIX, inner)
+    xr = [x[0, :, :, j, :] for j in range(RADIX)]
+    xi = [x[1, :, :, j, :] for j in range(RADIX)]
+    ar, ai = xr[0] + xr[2], xi[0] + xi[2]
+    br, bi = xr[1] + xr[3], xi[1] + xi[3]
+    cr, ci = xr[0] - xr[2], xi[0] - xi[2]
+    dr, di = xr[1] - xr[3], xi[1] - xi[3]
+    yr = jnp.stack([ar + br, cr + di, ar - br, cr - di], axis=0)
+    yi = jnp.stack([ai + bi, ci - dr, ai - bi, ci + dr], axis=0)
+    tr = jnp.asarray(twiddle_re)[:, None, None, :]
+    ti = jnp.asarray(twiddle_im)[:, None, None, :]
+    zr = yr * tr - yi * ti
+    zi = yr * ti + yi * tr
+    z = jnp.concatenate([zr, zi], axis=-1)
+    product = jnp.einsum(
+        "kasn,nm->kasm",
+        z,
+        jnp.asarray(inner_matrix),
+        precision=lax.Precision.HIGH,
+        preferred_element_type=jnp.float32,
+    ).astype(jnp.bfloat16)
+    return product.reshape(RADIX, row_count, spec_count, 2, inner)
 
 
 def reorder_inputs(values, station_of_slot, station_ok):
@@ -80,20 +105,22 @@
     spec_local = samples.shape[2] // fft_len
     half_count = lax.axis_size("tch")
     block_count = lax.axis_size("blk")
+    dest_count = half_count * block_count
     spec_total = spec_local * half_count
-    dft_matrix = dft_table(fft_len)
+    inner = fft_len // RADIX
     tail_block = jnp.concatenate([history, samples], axis=2)[:, :, -(tap_count - 1) * fft_len :]
     earlier = shifted(tail_block, "tch", 1)
     is_first = lax.axis_index("tch") == 0
     earlier = jnp.where(is_first, history, earlier)
     extended = jnp.concatenate([earlier, samples], axis=2)
-    by_channel = channel_major(filter_bank(extended, coefficients, spec_local), dft_matrix)
-    by_block = lax.all_to_all(by_channel, "blk", split_axis=0, concat_axis=1, tiled=True)
-    turned = lax.all_to_all(by_block, "tch", split_axis=0, concat_axis=1, tiled=True)
-    chan_local = turned.shape[0]
-    layout = turned.reshape(chan_local, half_count, block_count, row_count, 2, spec_local)
-    layout = jnp.transpose(layout, (0, 2, 3, 4, 1, 5))
-    stacked = layout.reshape(chan_local, block_count * row_count, 2 * spec_total)
+    spectra = channelize(filter_bank(extended, coefficients, spec_local))
+    kl_count = inner // dest_count
+    spectra = spectra.reshape(RADIX, row_count, spec_local, 2, dest_count, kl_count)
+    spectra = jnp.transpose(spectra, (4, 5, 0, 1, 3, 2))
+    turned = lax.all_to_all(spectra, ("blk", "tch"), split_axis=0, concat_axis=0, tiled=True)
+    layout = turned.reshape(block_count, half_count, kl_count, RADIX, row_count, 2, spec_local)
+    layout = jnp.transpose(layout, (2, 3, 0, 4, 5, 1, 6))
+    stacked = layout.reshape(kl_count * RADIX, block_count * row_count, 2 * spec_total)
     ordered = reorder_inputs(stacked, station_of_slot, station_ok)
     inverse_count = 1.0 / spec_total
     return correlate_full(ordered, inverse_count)

time: 76.6 us -> 56.7 us (0.74)
  other arithmetic: 38.6 us -> 6.42 us
  local copies, waits for them, and re-layouts: 10.2 us -> 26.3 us
  blocking collectives: 4.15 us -> 0 us
    another operation x2 -> x0, other arithmetic: 34.5 us -> none
    reshape x3 -> x4, local copies, waits for them, and re-layouts: 0.92 us -> 8.79 us  [the longest x2 4.79 us: local(): layout.reshape(kl_count * RADIX, block_count * row_count, 2 * spec_total)]
    unnamed x18 -> x12, local copies, waits for them, and re-layouts: 1.14 us -> 6.51 us
    all_to_all x1 -> x0, blocking collectives: 4.15 us -> none  [local(): lax.all_to_all(by_block, 'tch', split_axis=0, concat_axis=1, tiled=True)]
    transpose x1 -> x0, other arithmetic: 2.23 us -> none  [channel_major(): jnp.transpose(filtered, (1, 2, 0, 3))]
    reshape x0 -> x1, other arithmetic: none -> 2.21 us  [channelize(): filtered.astype(jnp.float32).reshape(2, row_count, spec_count, RADIX, inner)]
    all_to_all x4 -> x0, local copies, waits for them, and re-layouts: 2.03 us -> none  [the longest x2 1.28 us: local(): lax.all_to_all(by_channel, 'blk', split_axis=0, concat_axis=1, tiled=True)]
    transpose x2 -> x1, local copies, waits for them, and re-layouts: 0.67 us -> 1.94 us  [local(): spectra = jnp.transpose(spectra, (4, 5, 0, 1, 3, 2))]
  transfers between devices with their start and end apart: 2 -> 2, of which waited for: 1 -> 1; matrix products, arithmetic and copies ran while one was open for 48% -> 6% of each run, Pallas kernels for 0% -> 0%
where the time goes in v1:
time: 56.7 us; the launch traced here: 56.1 us
  local copies, waits for them, and re-layouts  26.3 us (46%)
  waiting for transfers between devices  12.1 us (21%)
  starting transfers between devices  9.11 us (16%)
  other arithmetic  6.42 us (11%)
  matrix products  1.91 us (3%)
    all_to_all x1, waiting for transfers between devices, local(): lax.all_to_all(spectra, ('blk', 'tch'), split_axis=0, concat_axis=0, tile...  12.1 us
    all_to_all x1, starting transfers between devices, local(): lax.all_to_all(spectra, ('blk', 'tch'), split_axis=0, concat_axis=0, tile...  6.74 us
    unnamed x12, local copies, waits for them, and re-layouts  6.51 us
    reshape x2, local copies, waits for them, and re-layouts, local(): layout.reshape(kl_count * RADIX, block_count * row_count, 2 * spec_total)  4.79 us
    reshape x1, local copies, waits for them, and re-layouts, local(): turned.reshape(block_count, half_count, kl_count, RADIX, row_count, 2, sp...  3.5 us
    ppermute x1, starting transfers between devices, shifted(): return lax.ppermute(block, axis, route)  2.37 us
    reshape x1, other arithmetic, channelize(): filtered.astype(jnp.float32).reshape(2, row_count, spec_count, RADIX, inner)  2.21 us
    transpose x1, local copies, waits for them, and re-layouts, local(): spectra = jnp.transpose(spectra, (4, 5, 0, 1, 3, 2))  1.94 us
  transfers between devices with their start and end apart: 2, of which 1 were waited for; matrix products, arithmetic and copies ran while one was open for 6% of the time, Pallas kernels for 0%

profile of v1, /device:TPU:0, one launch (start us, length us, event | category | flops | bytes accessed | tf_op | source)
XLA Modules:
  0.0 56.1 jit_solution(950478586566634360)
XLA Ops:
  0.0 0.0 copy-start
  0.0 1.0 %slice.130 = bf16[2,4,15360]{2,1,0:T(4,128)(2,1)S(1)} slice(bf16[2,4,32768]{2,1,0:T(4,128)(2,1)} %param.8), slice={[0:2], [0:4], [17408:32768]} | slice | bytes 491520 | tf_op jit(solution)/shard_map/slice | solution.py:111
  1.0 2.4 %collective-permute-start = (bf16[2,4,15360]{2,1,0:T(4,128)(2,1)S(1)}, bf16[2,4,15360]{2,1,0:T(4,128)(2,1)S(1)}, u32[]{:S(2)}, u32[]{:S(2)}) collective-permute-start(bf16[2,4,15360]{2,1,0:T(4,128)(2,1)S(1)} %slice.130), channel_id=1, source_target_pairs={{0,1},{2,3},{4,5},{6,7},{8,9},{10,11},{12,13},{14,15},{16,17},{18,... | collective-permute-start | bytes 737288 | tf_op jit(solution)/shard_map/ppermute | solution.py:17
  3.4 1.3 %fusion.20 = (f32[1,1024]{1,0:T(1,128)S(1)}, f32[1,1024]{1,0:T(1,128)S(1)}, f32[1,1024]{1,0:T(1,128)S(1)}, f32[1,1024]{1,0:T(1,128)S(1)}, f32[1,1024]{1,0:T(1,12...) fusion(f32[16,1024]{1,0:T(8,128)} %param.10), kind=kLoop, calls=%fused_computation.65 | loop fusion | bytes 131072 | tf_op jit(solution)/shard_map/slice | solution.py:42
  4.7 0.0 collective-permute-done
  4.7 1.0 %broadcast_select_fusion = bf16[1,8,15360]{2,1,0:T(8,128)(2,1)S(1)} fusion(bf16[1,8,15360]{2,1,0:T(8,128)(2,1)} %bitcast.72, bf16[1,8,15360]{2,1,0:T(8,128)(2,1)S(1)} %bitcast.73, pred[]{:T(512)S(6)} %eq.5), kind=kLoop, calls=%fused_computation.26 | loop fusion | flops 122880 | bytes 737281 | tf_op jit(solution)/shard_map/jit(_where)/select_n | solution.py:114
  5.7 1.4 %pad_maximum_fusion = bf16[2,4,48128]{2,1,0:T(4,128)(2,1)S(1)} fusion(bf16[2,4,32768]{2,1,0:T(4,128)(2,1)} %param.8, bf16[2,4,15360]{2,1,0:T(4,128)(2,1)S(1)} %bitcast.71), kind=kLoop, calls=%fused_computation.12 | loop fusion | flops 1540096 | bytes 1540096 | tf_op jit(solution)/shard_map/concatenate | solution.py:115
  7.1 0.5 reshape.362
  7.6 2.2 %fusion.10 = f32[2,4,32,1024]{3,2,1,0:T(8,128)S(1)} fusion(bf16[2,4,47,1024]{3,2,1,0:T(8,128)(2,1)S(1)} %reshape.362, f32[1024]{0:T(1024)S(1)} %bitcast.88, f32[1024]{0:T(1024)S(1)} %bitcast.89, f32[1024]{0:T(1024)S(1)} %bitcast.75, f32[1024]{0:T(1024)S(1)} %bitcast.76, f32[1024]{0:T(1024)S(1)} %bitcast.77, f32[1024]{0:T(1024)S(1)} %bitcast.78, ...), kind=kLoop, calls=%fused_computation.25 | loop fusion | flops 12845056 | bytes 9502720 | tf_op jit(solution)/shard_map/reshape | solution.py:52
  9.9 0.5 reshape.368
  10.4 0.0 copy-start.2
  10.4 0.0 copy-start.3
  10.4 0.9 %fusion.19 = (f32[1,4,32,1,256]{4,3,2,1,0:T(1,128)S(1)}, f32[1,4,32,1,256]{4,3,2,1,0:T(1,128)S(1)}, f32[1,4,32,1,256]{4,3,2,1,0:T(1,128)S(1)}, f32[1,4,32,1,256]...) fusion(f32[2,4,32,4,256]{4,3,2,1,0:T(4,128)S(1)} %reshape.368), kind=kLoop, calls=%fused_computation.64 | loop fusion | bytes 2097152 | tf_op jit(solution)/shard_map/slice | solution.py:53
  11.3 0.0 copy-start.1
  11.3 0.1 add_bitcast_fusion.3
  11.5 0.0 copy-done.2
  11.5 0.0 copy-done.3
  11.5 0.1 multiply_subtract_fusion
  11.7 0.9 %copy-done.1 = f32[512,512,1,1]{1,0,3,2:T(8,128)S(1)} copy-done((f32[512,512,1,1]{1,0,3,2:T(8,128)S(1)}, f32[512,512,1,1]{1,0,3,2:T(8,128)}, u32[]{:S(2)}) %copy-start.1) | copy-done | bytes 1048600
  12.6 1.0 %convolution_convert_fusion = bf16[4,4,32,512]{3,2,1,0:T(8,128)(2,1)S(1)} fusion(f32[512,512,1,1]{1,0,3,2:T(8,128)S(1)} %copy-done.1, f32[4,4,32,256]{3,2,1,0:T(8,128)S(1)} %get-tuple-element.6, f32[4,4,32,256]{3,2,1,0:T(8,128)S(1)} %get-tuple-element.5), kind=kOutput, calls=%fused_computation.5 | convolution fusion | flops 805830656 | bytes 2621440 | tf_op jit(solution)/shard_map/kasn,nm->kasm/dot_general | solution.py:66
  13.6 1.0 %copy.45 = bf16[4,4,32,512]{2,3,1,0:T(8,128)(2,1)S(1)} copy(bf16[4,4,32,512]{3,2,1,0:T(8,128)(2,1)S(1)} %convolution_convert_fusion) | data formatting | bytes 1048576 | tf_op jit(solution)/shard_map/convert_element_type | solution.py:72
  14.7 1.9 %copy.149 = bf16[16,16,4,4,2,32]{5,1,4,3,2,0:T(8,128)(2,1)} copy(bf16[16,16,4,4,2,32]{5,1,0,4,3,2:T(8,128)(2,1)S(1)} %bitcast.65) | data formatting | bytes 1048576 | tf_op jit(solution)/shard_map/transpose | solution.py:119
  16.6 0.0 copy-start.4
  16.6 4.5 %reshape.406 = bf16[16,2,8192]{2,1,0:T(2,128)(2,1)} reshape(bf16[16,4,4,2,16,32]{5,4,3,2,1,0:T(8,128)(2,1)} %bitcast.66) | data formatting | bytes 1048576
  21.1 6.7 %all-to-all-start = ((bf16[16,2,8192]{2,1,0:T(2,128)(2,1)}), bf16[16,2,8192]{2,1,0:T(2,128)(2,1)S(1)}, u32[]{:S(2)}, u32[]{:S(2)}) async-start(bf16[16,2,8192]{2,1,0:T(2,128)(2,1)} %reshape.406), calls=%async_computation | async-start | bytes 1048576 | tf_op jit(solution)/shard_map/all_to_all | solution.py:120
  27.9 0.0 copy-done.4
  27.9 0.8 %scatter_custom_fusion = s32[16]{0:T(128)S(1)} fusion(s32[16]{0:T(128)S(1)} %compare_select_fusion.3, s32[16]{0:T(128)S(1)} %iota.14, s32[]{:T(128)} %constant.58.clone.1), kind=kCustom, calls=%fused_computation.60 | custom fusion | bytes 68 | tf_op jit(solution)/shard_map/scatter | solution.py:82
  28.8 0.7 %gather_fusion = s32[32]{0:T(128)S(1)} fusion(s32[16]{0:T(128)S(1)} %scatter_custom_fusion, s32[1024]{0:T(1024)S(1)} %pad_clamp_fusion.1), kind=kCustom, calls=%fused_computation | custom fusion | bytes 384 | tf_op jit(solution)/shard_map/gather | solution.py:85
  29.5 0.0 copy-done
  29.5 0.7 %gather_fusion.2 = s32[32]{0:T(128)S(1)} fusion(s32[16]{0:T(128)S(1)} %copy-done, s32[1024]{0:T(1024)S(1)} %pad_clamp_fusion.1), kind=kCustom, calls=%fused_computation.2 | custom fusion | bytes 384 | tf_op jit(solution)/shard_map/gather | solution.py:86
  30.2 12.1 %all-to-all-done = bf16[16,2,8192]{2,1,0:T(2,128)(2,1)S(1)} async-done(((bf16[16,2,8192]{2,1,0:T(2,128)(2,1)}), bf16[16,2,8192]{2,1,0:T(2,128)(2,1)S(1)}, u32[]{:S(2)}, u32[]{:S(2)}) %all-to-all-start) | async-done | bytes 524320 | tf_op jit(solution)/shard_map/all_to_all | solution.py:120
  42.4 1.0 %reshape.407 = bf16[16,4,4,2,16,32]{5,4,3,2,1,0:T(8,128)(2,1)S(1)} reshape(bf16[16,2,8192]{2,1,0:T(2,128)(2,1)S(1)} %all-to-all-done) | data formatting | bytes 1048576
  43.4 3.5 %copy.148 = bf16[8,2,16,4,4,2,32]{6,1,5,4,0,3,2:T(2,128)(2,1)} copy(bf16[8,2,16,4,4,2,32]{6,2,5,4,3,1,0:T(8,128)(2,1)S(1)} %bitcast.67) | data formatting | bytes 1048576 | tf_op jit(solution)/shard_map/reshape | solution.py:121
  46.9 4.6 %reshape.366 = bf16[64,32,128]{2,1,0:T(8,128)(2,1)S(1)} reshape(bf16[16,4,8,4,2,2,32]{6,5,4,3,2,1,0:T(2,128)(2,1)} %bitcast.68) | data formatting | bytes 1048576 | tf_op jit(solution)/shard_map/reshape | solution.py:123
  51.5 0.2 copy.48
  51.7 0.6 %gather_fusion.1 = bf16[32,64,128]{2,1,0:T(8,128)(2,1)S(1)} fusion(bf16[64,32,128]{2,0,1:T(8,128)(2,1)S(1)} %copy.48, s32[1024]{0:T(1024)S(1)} %pad_clamp_fusion), kind=kCustom, calls=%fused_computation.1 | custom fusion | bytes 1048704 | tf_op jit(solution)/shard_map/jit(_take)/gather | solution.py:87
  52.4 0.3 fusion.9
  52.7 0.2 slice_negate_fusion
  53.0 0.4 fusion.21
  53.3 0.5 fusion.4
  53.8 0.7 %copy.51 = f32[64,32,32]{0,2,1:T(8,128)S(1)} copy(f32[64,32,32]{2,1,0:T(8,128)S(1)} %fusion.4) | data formatting | bytes 524288 | tf_op jit(solution)/shard_map/cak,cbk->cab/dot_general | solution.py:98
  54.5 0.7 %copy.50 = f32[64,32,32]{0,2,1:T(8,128)S(1)} copy(f32[64,32,32]{2,1,0:T(8,128)S(1)} %fusion.21) | data formatting | bytes 524288 | tf_op jit(solution)/shard_map/cak,cbk->cab/dot_general | solution.py:97
  55.2 0.9 %fusion.3 = bf16[2,64,32,32]{1,3,2,0:T(8,128)(2,1)} fusion(f32[1,64,32,32]{1,3,2,0:T(8,128)S(1)} %bitcast.69, f32[1,64,32,32]{1,3,2,0:T(8,128)S(1)} %bitcast.70), kind=kLoop, calls=%fused_computation.10 | loop fusion | flops 393216 | bytes 786432 | tf_op jit(solution)/shard_map/convert_element_type | solution.py:99
  (8 shorter events, 0.1 us)
Async XLA Ops:
  0.0 29.5 %copy-start = (s32[16]{0:T(128)S(1)}, s32[16]{0:T(128)}, u32[]{:S(2)}) copy-start(s32[16]{0:T(128)} %param.12) | copy-start | bytes 196
  1.0 3.7 %collective-permute-start = (bf16[2,4,15360]{2,1,0:T(4,128)(2,1)S(1)}, bf16[2,4,15360]{2,1,0:T(4,128)(2,1)S(1)}, u32[]{:S(2)}, u32[]{:S(2)}) collective-permute-start(bf16[2,4,15360]{2,1,0:T(4,128)(2,1)S(1)} %slice.130), channel_id=1, source_target_pairs={{0,1},{2,3},{4,5},{6,7},{8,9},{10,11},{12,13},{14,15},{16,17},{18,... | collective-permute-start | bytes 737288 | tf_op jit(solution)/shard_map/ppermute | solution.py:17
  10.4 1.1 %copy-start.2 = (f32[4,256]{1,0:T(4,128)S(1)}, f32[4,256]{1,0:T(4,128)}, u32[]{:S(2)}) copy-start(f32[4,256]{1,0:T(4,128)} %constant.68.clone) | copy-start | bytes 12292
  10.4 1.1 %copy-start.3 = (f32[4,256]{1,0:T(4,128)S(1)}, f32[4,256]{1,0:T(4,128)}, u32[]{:S(2)}) copy-start(f32[4,256]{1,0:T(4,128)} %constant.69.clone) | copy-start | bytes 12292
  11.3 1.2 %copy-start.1 = (f32[512,512,1,1]{1,0,3,2:T(8,128)S(1)}, f32[512,512,1,1]{1,0,3,2:T(8,128)}, u32[]{:S(2)}) copy-start(f32[512,512,1,1]{1,0,3,2:T(8,128)} %constant.73) | copy-start | bytes 3145732
  16.6 11.3 %copy-start.4 = (s32[16]{0:T(128)S(1)}, s32[16]{0:T(128)}, u32[]{:S(2)}) copy-start(s32[16]{0:T(128)} %param.11) | copy-start | bytes 196
  21.1 21.2 %all-to-all-start = ((bf16[16,2,8192]{2,1,0:T(2,128)(2,1)}), bf16[16,2,8192]{2,1,0:T(2,128)(2,1)S(1)}, u32[]{:S(2)}, u32[]{:S(2)}) async-start(bf16[16,2,8192]{2,1,0:T(2,128)(2,1)} %reshape.406), calls=%async_computation | async-start | bytes 1048576 | tf_op jit(solution)/shard_map/all_to_all | solution.py:120

commit v2 on v1

v2 whole, which is shorter than its diff:
```python
import math

import numpy as np

import jax
import jax.numpy as jnp
from jax import lax
from jax.sharding import PartitionSpec as P

POLS = 2
RADIX = 4


def dft_tables(fft_len):
    inner = fft_len // RADIX
    n2 = np.arange(inner)
    k1 = np.arange(RADIX)
    tw_angle = 2.0 * np.pi * np.outer(k1, n2) / fft_len
    twiddle_re = np.cos(tw_angle).astype(np.float32)
    twiddle_im = (-np.sin(tw_angle)).astype(np.float32)
    angle = 2.0 * np.pi * (np.outer(n2, n2) % inner) / inner
    scale = 1.0 / math.sqrt(fft_len)
    inner_matrix = np.concatenate([np.cos(angle) * scale, np.sin(angle) * scale], axis=0)
    return twiddle_re, twiddle_im, inner_matrix.astype(np.float32)


def filter_bank(extended, coefficients, spec_count):
    tap_count, fft_len = coefficients.shape
    blocks = extended.reshape(extended.shape[0], extended.shape[1], -1, fft_len)
    running = jnp.zeros((extended.shape[0], extended.shape[1], spec_count, fft_len), jnp.float32)
    for tap_index in range(tap_count):
        running = running + coefficients[tap_index] * blocks[
            :, :, tap_index : tap_index + spec_count, :
        ].astype(jnp.float32)
    return running.astype(jnp.bfloat16)


def channelize(filtered):
    _, pol_count, spec_count, fft_len = filtered.shape
    inner = fft_len // RADIX
    twiddle_re, twiddle_im, inner_matrix = dft_tables(fft_len)
    x = filtered.astype(jnp.float32)
    xr = [x[0, :, :, j * inner : (j + 1) * inner] for j in range(RADIX)]
    xi = [x[1, :, :, j * inner : (j + 1) * inner] for j in range(RADIX)]
    ar, ai = xr[0] + xr[2], xi[0] + xi[2]
    br, bi = xr[1] + xr[3], xi[1] + xi[3]
    cr, ci = xr[0] - xr[2], xi[0] - xi[2]
    dr, di = xr[1] - xr[3], xi[1] - xi[3]
    yr = jnp.stack([ar + br, cr + di, ar - br, cr - di], axis=0)
    yi = jnp.stack([ai + bi, ci - dr, ai - bi, ci + dr], axis=0)
    tr = jnp.asarray(twiddle_re)[:, None, None, :]
    ti = jnp.asarray(twiddle_im)[:, None, None, :]
    zr = yr * tr - yi * ti
    zi = yr * ti + yi * tr
    real_rows = jnp.concatenate([zr, zi], axis=-1)
    imag_rows = jnp.concatenate([zi, -zr], axis=-1)
    rows = jnp.stack([real_rows, imag_rows], axis=2).reshape(RADIX * pol_count * 2 * spec_count, 2 * inner)
    product = lax.dot_general(
        jnp.asarray(inner_matrix),
        rows,
        (((0,), (1,)), ((), ())),
        precision=lax.Precision.HIGH,
        preferred_element_type=jnp.float32,
    )
    return product.astype(jnp.bfloat16)


def rotate_parts(ordered):
    half_cols = ordered.shape[2] // 2
    return jnp.concatenate([-ordered[:, :, half_cols:], ordered[:, :, :half_cols]], axis=2)


def correlate_full(ordered, inverse_count):
    rotated = rotate_parts(ordered)
    real_vis = jnp.einsum("cak,cbk->cab", ordered, ordered, preferred_element_type=jnp.float32)
    imag_vis = jnp.einsum("cak,cbk->cab", ordered, rotated, preferred_element_type=jnp.float32)
    return (jnp.stack([real_vis, imag_vis], axis=0) * inverse_count).astype(jnp.bfloat16)


def local(samples, history, coefficients, station_of_slot, station_ok):
    tap_count, fft_len = coefficients.shape
    row_count = samples.shape[1]
    half_count = lax.axis_size("tch")
    block_count = lax.axis_size("blk")
    dest_count = half_count * block_count
    station_count = station_of_slot.shape[0]
    inner = fft_len // RADIX
    kl_count = inner // dest_count
    keep = row_count // half_count
    t = lax.axis_index("tch")
    own = lax.dynamic_slice_in_dim(samples, t * keep, keep, axis=1)
    other = lax.dynamic_slice_in_dim(samples, (1 - t) * keep, keep, axis=1)
    received = lax.ppermute(other, "tch", [(0, 1), (1, 0)])
    is_first = t == 0
    first = jnp.where(is_first, own, received)
    second = jnp.where(is_first, received, own)
    earlier = lax.dynamic_slice_in_dim(history, t * keep, keep, axis=1)
    extended = jnp.concatenate([earlier, first, second], axis=2)
    spec_total = (extended.shape[2] - (tap_count - 1) * fft_len) // fft_len
    spectra = channelize(filter_bank(extended, coefficients, spec_total))
    spectra = spectra.reshape(dest_count, kl_count, -1)
    turned = lax.all_to_all(spectra, ("blk", "tch"), split_axis=0, concat_axis=0, tiled=True)
    slot_index = (
        jnp.zeros((station_count,), jnp.int32)
        .at[station_of_slot]
        .set(jnp.arange(station_count, dtype=jnp.int32))
    )
    keep_mask = station_ok.astype(turned.dtype)
    gathered = jnp.take(turned, slot_index, axis=0) * keep_mask[:, None, None]
    gathered = gathered.reshape(station_count, kl_count, RADIX, POLS, 2 * spec_total)
    ordered = jnp.transpose(gathered, (1, 2, 0, 3, 4)).reshape(
        kl_count * RADIX, station_count * POLS, 2 * spec_total
    )
    return correlate_full(ordered, 1.0 / spec_total)


def solution(mesh):
    return jax.shard_map(
        local,
        mesh=mesh,
        in_specs=(P("grp", "blk", "tch"), P("grp", "blk", None), P(), P("grp"), P("grp")),
        out_specs=P("grp", ("blk", "tch"), None, None),
        check_vma=False,
    )
```

time: 56.7 us -> 39.2 us (0.69)
  local copies, waits for them, and re-layouts: 26.3 us -> 7.54 us
  waiting for transfers between devices: 12.1 us -> 13.7 us
  starting transfers between devices: 9.11 us -> 7.55 us
  matrix products: 1.91 us -> 2.71 us
    reshape x4 -> x0, local copies, waits for them, and re-layouts: 8.79 us -> none  [the longest x2 4.79 us: local(): layout.reshape(kl_count * RADIX, block_count * row_count, 2 * spec_total)]
    unnamed x12, local copies, waits for them, and re-layouts: 6.51 us -> 1.35 us
    reshape x1 -> x0, other arithmetic: 2.21 us -> none  [channelize(): filtered.astype(jnp.float32).reshape(2, row_count, spec_count, RADIX, inner)]
    convert_element_type x1 -> x2, other arithmetic: 0.01 us -> 2.16 us  [the longest x1 2.16 us: channelize(): x = filtered.astype(jnp.float32)]
    slice x2 -> x0, local copies, waits for them, and re-layouts: 1.99 us -> none  [the longest x1 1.04 us: local(): jnp.concatenate([history, samples], axis=2)]
    transpose x1 -> x0, local copies, waits for them, and re-layouts: 1.94 us -> none  [local(): spectra = jnp.transpose(spectra, (4, 5, 0, 1, 3, 2))]
    ppermute x1, starting transfers between devices: 2.37 us -> 0.52 us  [local(): received = lax.ppermute(other, 'tch', [(0, 1), (1, 0)])]
    all_to_all x1, waiting for transfers between devices: 12.1 us -> 13.7 us  [local(): lax.all_to_all(spectra, ('blk', 'tch'), split_axis=0, concat_axis=0, tile...]
  transfers between devices with their start and end apart: 2 -> 2, of which waited for: 1 -> 1; matrix products, arithmetic and copies ran while one was open for 6% -> 5% of each run, Pallas kernels for 0% -> 0%
where the time goes in v2:
time: 39.2 us; the launch traced here: 38.7 us
  waiting for transfers between devices  13.7 us (35%)
  starting transfers between devices  7.55 us (19%)
  local copies, waits for them, and re-layouts  7.54 us (19%)
  other arithmetic  6.91 us (18%)
  matrix products  2.71 us (7%)
    all_to_all x1, waiting for transfers between devices, local(): lax.all_to_all(spectra, ('blk', 'tch'), split_axis=0, concat_axis=0, tile...  13.7 us
    all_to_all x1, starting transfers between devices, local(): lax.all_to_all(spectra, ('blk', 'tch'), split_axis=0, concat_axis=0, tile...  7.03 us
    convert_element_type x1, other arithmetic, channelize(): x = filtered.astype(jnp.float32)  2.16 us
    dot_general x1, matrix products, channelize(): lax.dot_general(jnp.asarray(inner_matrix), rows, (((0,), (1,)), ((), ()))...  1.84 us
    select_n x1, other arithmetic, local(): first = jnp.where(is_first, own, received)  1.61 us
    dynamic_slice x1, local copies, waits for them, and re-layouts, local(): other = lax.dynamic_slice_in_dim(samples, (1 - t) * keep, keep, axis=1)  1.36 us
    unnamed x12, local copies, waits for them, and re-layouts  1.35 us
    slice x1, local copies, waits for them, and re-layouts, filter_bank(): coefficients[tap_index]  1.29 us
  transfers between devices with their start and end apart: 2, of which 1 were waited for; matrix products, arithmetic and copies ran while one was open for 5% of the time, Pallas kernels for 0%

profile of v2, /device:TPU:0, one launch (start us, length us, event | category | flops | bytes accessed | tf_op | source)
XLA Modules:
  0.0 38.7 jit_solution(6238181405765674895)
XLA Ops:
  0.0 0.0 copy-start
  0.0 1.4 %constant_dynamic-slice_fusion = bf16[2,2,32768]{2,1,0:T(2,128)(2,1)S(1)} fusion(bf16[2,4,32768]{2,1,0:T(4,128)(2,1)} %param.8, s32[]{:T(128)S(6)} %select_n.36), kind=kLoop, calls=%fused_computation.44 | loop fusion | bytes 524292 | tf_op jit(solution)/shard_map/dynamic_slice | solution.py:92
  1.4 0.5 %collective-permute-start = (bf16[2,2,32768]{2,1,0:T(2,128)(2,1)S(1)}, bf16[2,2,32768]{2,1,0:T(2,128)(2,1)S(1)}, u32[]{:S(2)}, u32[]{:S(2)}) collective-permute-start(bf16[2,2,32768]{2,1,0:T(2,128)(2,1)S(1)} %constant_dynamic-slice_fusion), channel_id=1, source_target_pairs={{0,1},{1,0},{2,3},{3,2},{4,5},{5,4},{6,7},{7,6},{8,9},{9,8},{10,11... | collective-permute-start | bytes 786440 | tf_op jit(solution)/shard_map/ppermute | solution.py:93
  1.9 0.0 copy-done
  1.9 0.1 constant_dynamic-slice_fusion.1
  2.0 1.3 %fusion.19 = (f32[1,1024]{1,0:T(1,128)S(1)}, f32[1,1024]{1,0:T(1,128)S(1)}, f32[1,1024]{1,0:T(1,128)S(1)}, f32[1,1024]{1,0:T(1,128)S(1)}, f32[1,1024]{1,0:T(1,12...) fusion(f32[16,1024]{1,0:T(8,128)} %param.10), kind=kLoop, calls=%fused_computation.50 | loop fusion | bytes 131072 | tf_op jit(solution)/shard_map/slice | solution.py:32
  3.3 0.0 collective-permute-done
  3.3 1.6 %broadcast_select_fusion.2 = (bf16[2,2,32768]{2,1,0:T(2,128)(2,1)S(1)}, bf16[2,2,32768]{2,1,0:T(2,128)(2,1)S(1)}) fusion(bf16[2,2,32768]{2,1,0:T(2,128)(2,1)S(1)} %collective-permute-done, pred[]{:T(512)S(6)} %eq.3, bf16[2,4,32768]{2,1,0:T(4,128)(2,1)} %param.8, s32[]{:T(128)S(6)} %select_n.34), kind=kLoop, calls=%fused_computation.22 | loop fusion | flops 262144 | bytes 1048581 | tf_op jit(solution)/shard_map/jit(_where)/select_n | solution.py:95
  4.9 0.6 %pad_maximum_fusion.1 = bf16[2,2,80896]{2,1,0:T(2,128)(2,1)S(1)} fusion(bf16[2,2,32768]{2,1,0:T(2,128)(2,1)S(1)} %get-tuple-element.17, bf16[2,2,32768]{2,1,0:T(2,128)(2,1)S(1)} %get-tuple-element.16, bf16[2,2,15360]{2,1,0:T(2,128)(2,1)S(1)} %constant_dynamic-slice_fusion.1), kind=kLoop, calls=%fused_computation.10 | loop fusion | flops 1941504 | bytes 1294336 | tf_op jit(solution)/shard_map/concatenate | solution.py:98
  5.5 0.4 %reshape.38 = bf16[2,2,79,1024]{3,2,1,0:T(8,128)(2,1)S(1)} reshape(bf16[2,2,80896]{2,1,0:T(2,128)(2,1)S(1)} %pad_maximum_fusion.1) | data formatting | bytes 1294336 | tf_op jit(solution)/shard_map/reshape | solution.py:29
  5.9 2.2 %fusion.6 = f32[2,2,64,1024]{3,2,1,0:T(8,128)S(1)} fusion(bf16[2,2,79,1024]{3,2,1,0:T(8,128)(2,1)S(1)} %reshape.38, f32[1024]{0:T(1024)S(1)} %bitcast.54, f32[1024]{0:T(1024)S(1)} %bitcast.55, f32[1024]{0:T(1024)S(1)} %bitcast.41, f32[1024]{0:T(1024)S(1)} %bitcast.42, f32[1024]{0:T(1024)S(1)} %bitcast.43, f32[1024]{0:T(1024)S(1)} %bitcast.44, ...), kind=kLoop, calls=%fused_computation.23 | loop fusion | flops 12845056 | bytes 9502720 | tf_op jit(solution)/shard_map/convert_element_type | solution.py:42
  8.1 0.0 copy-start.2
  8.1 0.0 copy-start.3
  8.1 0.1 fusion.8
  8.2 0.1 fusion.10
  8.3 0.5 %copy-done.2 = f32[4,256]{1,0:T(4,128)S(1)} copy-done((f32[4,256]{1,0:T(4,128)S(1)}, f32[4,256]{1,0:T(4,128)}, u32[]{:S(2)}) %copy-start.2) | copy-done | bytes 4120
  8.8 0.0 copy-done.3
  8.8 0.2 fusion.18
  9.0 0.2 maximum_bitcast_fusion
  9.2 0.2 pad_maximum_fusion
  9.5 0.0 copy-start.1
  9.5 0.2 copy.14
  9.7 0.8 %copy-done.1 = f32[512,256]{1,0:T(8,128)S(1)} copy-done((f32[512,256]{1,0:T(8,128)S(1)}, f32[512,256]{1,0:T(8,128)}, u32[]{:S(2)}) %copy-start.1) | copy-done | bytes 524312
  10.5 0.0 copy-start.4
  10.5 0.0 copy-start.5
  10.5 1.8 %convolution_convert_fusion = bf16[1024,256]{0,1:T(8,128)(2,1)} fusion(f32[1024,512]{1,0:T(8,128)S(1)} %bitcast.37, f32[512,256]{1,0:T(8,128)S(1)} %copy-done.1), kind=kOutput, calls=%fused_computation.3 | convolution fusion | flops 805568512 | bytes 3145728 | tf_op jit(solution)/shard_map/dot_general | solution.py:58
  12.4 7.0 %all-to-all-start = ((bf16[16,16,1024]{2,1,0:T(8,128)(2,1)}), bf16[16,16,1024]{2,1,0:T(8,128)(2,1)S(1)}, u32[]{:S(2)}, u32[]{:S(2)}) async-start(bf16[16,16,1024]{2,1,0:T(8,128)(2,1)} %bitcast.20), calls=%async_computation | async-start | bytes 1048576 | tf_op jit(solution)/shard_map/all_to_all | solution.py:102
  19.4 0.0 copy-done.4
  19.4 0.0 copy-done.5
  19.5 0.6 %scatter_custom_fusion = s32[16]{0:T(128)S(1)} fusion(s32[16]{0:T(128)S(1)} %compare_select_fusion.1, s32[16]{0:T(128)S(1)} %iota.3, s32[]{:T(128)} %constant.12.clone.1), kind=kCustom, calls=%fused_computation.46 | custom fusion | bytes 68 | tf_op jit(solution)/shard_map/scatter | solution.py:106
  20.1 13.7 %all-to-all-done = bf16[16,16,1024]{2,1,0:T(8,128)(2,1)S(1)} async-done(((bf16[16,16,1024]{2,1,0:T(8,128)(2,1)}), bf16[16,16,1024]{2,1,0:T(8,128)(2,1)S(1)}, u32[]{:S(2)}, u32[]{:S(2)}) %all-to-all-start) | async-done | bytes 524320 | tf_op jit(solution)/shard_map/all_to_all | solution.py:102
  33.9 0.6 %gather_fusion = bf16[16,16,1024]{2,1,0:T(8,128)(2,1)S(1)} fusion(bf16[16,16,1024]{2,1,0:T(8,128)(2,1)S(1)} %all-to-all-done, s32[1024]{0:T(1024)S(1)} %pad_clamp_fusion), kind=kCustom, calls=%fused_computation | custom fusion | bytes 1048640 | tf_op jit(solution)/shard_map/jit(_take)/gather | solution.py:109
  34.5 0.4 gather.7
  34.8 0.6 %fusion.5 = bf16[16,16,4,2,128]{4,3,0,2,1:T(2,128)(2,1)S(1)} fusion(bf16[16,16,4,2,128]{4,3,2,1,0:T(2,128)(2,1)S(1)} %gather.7, pred[16]{0:T(512)(128)(4,1)S(1)} %compare_and_fusion, bf16[16]{0:T(256)(128)(2,1)S(1)} %convert_element_type.86), kind=kLoop, calls=%fused_computation.20 | loop fusion | flops 524288 | bytes 1048624 | tf_op jit(solution)/shard_map/mul | solution.py:109
  35.5 0.2 slice_negate_fusion
  35.7 0.4 %fusion.20 = f32[64,32,32]{2,1,0:T(8,128)S(1)} fusion(bf16[64,32,128]{2,1,0:T(8,128)(2,1)S(1)} %bitcast.35), kind=kOutput, calls=%fused_computation.51 | convolution fusion | flops 16777216 | bytes 786432 | tf_op jit(solution)/shard_map/cak,cbk->cab/dot_general | solution.py:75
  36.1 0.5 %fusion.1 = f32[64,32,32]{2,1,0:T(8,128)S(1)} fusion(bf16[64,32,128]{2,1,0:T(8,128)(2,1)S(1)} %bitcast.36, bf16[64,32,64]{2,1,0:T(8,128)(2,1)S(1)} %get-tuple-element.19, bf16[64,32,64]{2,1,0:T(8,128)(2,1)S(1)} %get-tuple-element.18), kind=kOutput, calls=%fused_computation.14 | convolution fusion | flops 17825792 | bytes 1310720 | tf_op jit(solution)/shard_map/cak,cbk->cab/dot_general | solution.py:76
  36.6 0.6 %copy.17 = f32[64,32,32]{0,2,1:T(8,128)S(1)} copy(f32[64,32,32]{2,1,0:T(8,128)S(1)} %fusion.1) | data formatting | bytes 524288 | tf_op jit(solution)/shard_map/cak,cbk->cab/dot_general | solution.py:76
  37.2 0.6 %copy.16 = f32[64,32,32]{0,2,1:T(8,128)S(1)} copy(f32[64,32,32]{2,1,0:T(8,128)S(1)} %fusion.20) | data formatting | bytes 524288 | tf_op jit(solution)/shard_map/cak,cbk->cab/dot_general | solution.py:75
  37.8 0.9 %fusion = bf16[2,64,32,32]{1,3,2,0:T(8,128)(2,1)} fusion(f32[1,64,32,32]{1,3,2,0:T(8,128)S(1)} %bitcast.38, f32[1,64,32,32]{1,3,2,0:T(8,128)S(1)} %bitcast.39), kind=kLoop, calls=%fused_computation.7 | loop fusion | flops 393216 | bytes 786432 | tf_op jit(solution)/shard_map/convert_element_type | solution.py:77
  (6 shorter events, 0.0 us)
Async XLA Ops:
  0.0 1.9 %copy-start = (bf16[2,4,15360]{2,1,0:T(4,128)(2,1)S(1)}, bf16[2,4,15360]{2,1,0:T(4,128)(2,1)}, u32[]{:S(2)}) copy-start(bf16[2,4,15360]{2,1,0:T(4,128)(2,1)} %param.9) | copy-start | bytes 737284
  1.4 2.0 %collective-permute-start = (bf16[2,2,32768]{2,1,0:T(2,128)(2,1)S(1)}, bf16[2,2,32768]{2,1,0:T(2,128)(2,1)S(1)}, u32[]{:S(2)}, u32[]{:S(2)}) collective-permute-start(bf16[2,2,32768]{2,1,0:T(2,128)(2,1)S(1)} %constant_dynamic-slice_fusion), channel_id=1, source_target_pairs={{0,1},{1,0},{2,3},{3,2},{4,5},{5,4},{6,7},{7,6},{8,9},{9,8},{10,11... | collective-permute-start | bytes 786440 | tf_op jit(solution)/shard_map/ppermute | solution.py:93
  8.1 0.7 %copy-start.2 = (f32[4,256]{1,0:T(4,128)S(1)}, f32[4,256]{1,0:T(4,128)}, u32[]{:S(2)}) copy-start(f32[4,256]{1,0:T(4,128)} %constant.37.clone) | copy-start | bytes 12292
  8.1 0.7 %copy-start.3 = (f32[4,256]{1,0:T(4,128)S(1)}, f32[4,256]{1,0:T(4,128)}, u32[]{:S(2)}) copy-start(f32[4,256]{1,0:T(4,128)} %constant.38.clone) | copy-start | bytes 12292
  9.5 1.0 %copy-start.1 = (f32[512,256]{1,0:T(8,128)S(1)}, f32[512,256]{1,0:T(8,128)}, u32[]{:S(2)}) copy-start(f32[512,256]{1,0:T(8,128)} %constant.39.clone) | copy-start | bytes 1572868
  10.5 8.9 %copy-start.4 = (s32[16]{0:T(128)S(1)}, s32[16]{0:T(128)}, u32[]{:S(2)}) copy-start(s32[16]{0:T(128)} %param.12) | copy-start | bytes 196
  10.5 8.9 %copy-start.5 = (s32[16]{0:T(128)S(1)}, s32[16]{0:T(128)}, u32[]{:S(2)}) copy-start(s32[16]{0:T(128)} %param.11) | copy-start | bytes 196
  12.4 21.5 %all-to-all-start = ((bf16[16,16,1024]{2,1,0:T(8,128)(2,1)}), bf16[16,16,1024]{2,1,0:T(8,128)(2,1)S(1)}, u32[]{:S(2)}, u32[]{:S(2)}) async-start(bf16[16,16,1024]{2,1,0:T(8,128)(2,1)} %bitcast.20), calls=%async_computation | async-start | bytes 1048576 | tf_op jit(solution)/shard_map/all_to_all | solution.py:102

commit v3 on v2

--- a/solution.py
+++ b/solution.py
@@ -97,19 +97,25 @@
     earlier = lax.dynamic_slice_in_dim(history, t * keep, keep, axis=1)
     extended = jnp.concatenate([earlier, first, second], axis=2)
     spec_total = (extended.shape[2] - (tap_count - 1) * fft_len) // fft_len
-    spectra = channelize(filter_bank(extended, coefficients, spec_total))
-    spectra = spectra.reshape(dest_count, kl_count, -1)
-    turned = lax.all_to_all(spectra, ("blk", "tch"), split_axis=0, concat_axis=0, tiled=True)
     slot_index = (
         jnp.zeros((station_count,), jnp.int32)
         .at[station_of_slot]
         .set(jnp.arange(station_count, dtype=jnp.int32))
     )
-    keep_mask = station_ok.astype(turned.dtype)
-    gathered = jnp.take(turned, slot_index, axis=0) * keep_mask[:, None, None]
-    gathered = gathered.reshape(station_count, kl_count, RADIX, POLS, 2 * spec_total)
-    ordered = jnp.transpose(gathered, (1, 2, 0, 3, 4)).reshape(
-        kl_count * RADIX, station_count * POLS, 2 * spec_total
+    keep_mask = station_ok.astype(jnp.bfloat16)
+    by_pol = []
+    pending = extended[:, 0:1]
+    for pol in range(keep):
+        spectra = channelize(filter_bank(pending, coefficients, spec_total))
+        spectra = spectra.reshape(dest_count, kl_count, -1)
+        if pol + 1 < keep:
+            spectra, pending = lax.optimization_barrier((spectra, extended[:, pol + 1 : pol + 2]))
+        turned = lax.all_to_all(spectra, ("blk", "tch"), split_axis=0, concat_axis=0, tiled=True)
+        gathered = jnp.take(turned, slot_index, axis=0) * keep_mask[:, None, None]
+        by_pol.append(gathered.reshape(station_count, kl_count, RADIX, 2 * spec_total))
+    gathered = jnp.stack(by_pol, axis=1)
+    ordered = jnp.transpose(gathered, (2, 3, 0, 1, 4)).reshape(
+        kl_count * RADIX, station_count * keep, 2 * spec_total
     )
     return correlate_full(ordered, 1.0 / spec_total)
 

time: 39.2 us -> 54.2 us (1.38)
  waiting for transfers between devices: 13.7 us -> 18.6 us
  local copies, waits for them, and re-layouts: 7.54 us -> 11.6 us
  starting transfers between devices: 7.55 us -> 11.3 us
  other arithmetic: 6.91 us -> 8.32 us
  matrix products: 2.71 us -> 3.55 us
    all_to_all x1 -> x2, waiting for transfers between devices: 13.7 us -> 18.6 us  [local(): lax.all_to_all(spectra, ('blk', 'tch'), split_axis=0, concat_axis=0, tile...]
    all_to_all x1 -> x2, starting transfers between devices: 7.03 us -> 10.7 us  [local(): lax.all_to_all(spectra, ('blk', 'tch'), split_axis=0, concat_axis=0, tile...]
    slice x0 -> x1, local copies, waits for them, and re-layouts: none -> 2.57 us  [local(): extended[:, pol + 1:pol + 2]]
    optimization_barrier x0 -> x1, other arithmetic: none -> 2.26 us  [local(): lax.optimization_barrier((spectra, extended[:, pol + 1:pol + 2]))]
    another operation x0 -> x1, other arithmetic: none -> 1.19 us  [local(): gathered = jnp.stack(by_pol, axis=1)]
    another operation x0 -> x4, local copies, waits for them, and re-layouts: none -> 1.16 us  [local(): gathered = jnp.stack(by_pol, axis=1)]
    select_n x1, other arithmetic: 1.61 us -> 0.56 us  [local(): first = jnp.where(is_first, own, received)]
    dot_general x1 -> x2, matrix products: 1.84 us -> 2.69 us  [channelize(): lax.dot_general(jnp.asarray(inner_matrix), rows, (((0,), (1,)), ((), ()))...]
  transfers between devices with their start and end apart: 2 -> 3, of which waited for: 1 -> 2; matrix products, arithmetic and copies ran while one was open for 5% -> 5% of each run, Pallas kernels for 0% -> 0%
where the time goes in v3:
time: 54.2 us; the launch traced here: 53.7 us
  waiting for transfers between devices  18.6 us (34%)
  local copies, waits for them, and re-layouts  11.6 us (21%)
  starting transfers between devices  11.3 us (21%)
  other arithmetic  8.32 us (15%)
  matrix products  3.55 us (7%)
    all_to_all x2, waiting for transfers between devices, local(): lax.all_to_all(spectra, ('blk', 'tch'), split_axis=0, concat_axis=0, tile...  18.6 us
    all_to_all x2, starting transfers between devices, local(): lax.all_to_all(spectra, ('blk', 'tch'), split_axis=0, concat_axis=0, tile...  10.7 us
    dot_general x2, matrix products, channelize(): lax.dot_general(jnp.asarray(inner_matrix), rows, (((0,), (1,)), ((), ()))...  2.69 us
    slice x1, local copies, waits for them, and re-layouts, local(): extended[:, pol + 1:pol + 2]  2.57 us
    optimization_barrier x1, other arithmetic, local(): lax.optimization_barrier((spectra, extended[:, pol + 1:pol + 2]))  2.26 us
    convert_element_type x2, other arithmetic, channelize(): x = filtered.astype(jnp.float32)  1.78 us
    unnamed x14, local copies, waits for them, and re-layouts  1.58 us
    dynamic_slice x1, local copies, waits for them, and re-layouts, local(): other = lax.dynamic_slice_in_dim(samples, (1 - t) * keep, keep, axis=1)  1.39 us
  transfers between devices with their start and end apart: 3, of which 2 were waited for; matrix products, arithmetic and copies ran while one was open for 5% of the time, Pallas kernels for 0%

profile of v3, /device:TPU:0, one launch (start us, length us, event | category | flops | bytes accessed | tf_op | source)
XLA Modules:
  0.0 53.7 jit_solution(4729465102108095315)
XLA Ops:
  0.0 0.0 copy-start
  0.0 0.0 copy-start.2
  0.0 1.4 %constant_dynamic-slice_fusion = bf16[2,2,32768]{2,1,0:T(2,128)(2,1)S(1)} fusion(bf16[2,4,32768]{2,1,0:T(4,128)(2,1)} %param.13, s32[]{:T(128)S(6)} %select_n.31), kind=kLoop, calls=%fused_computation.73 | loop fusion | bytes 524292 | tf_op jit(solution)/shard_map/dynamic_slice | solution.py:92
  1.4 0.5 collective-permute-start
  1.9 0.0 copy-done
  1.9 0.1 constant_dynamic-slice_fusion.1
  2.1 1.3 %fusion.29 = (f32[1,1024]{1,0:T(1,128)S(1)}, f32[1,1024]{1,0:T(1,128)S(1)}, f32[1,1024]{1,0:T(1,128)S(1)}, f32[1,1024]{1,0:T(1,128)S(1)}, f32[1,1024]{1,0:T(1,12...) fusion(f32[16,1024]{1,0:T(8,128)} %param.15), kind=kLoop, calls=%fused_computation.81 | loop fusion | bytes 131072 | tf_op jit(solution)/shard_map/slice | solution.py:32
  3.4 0.0 collective-permute-done
  3.4 0.0 copy-done.2
  3.4 0.6 %broadcast_select_fusion.1 = (bf16[2,2,32768]{2,1,0:T(2,128)(2,1)S(1)}, bf16[2,2,32768]{2,1,0:T(2,128)(2,1)S(1)}) fusion(bf16[2,2,32768]{2,1,0:T(2,128)(2,1)S(1)} %collective-permute-done, pred[]{:T(512)S(6)} %eq.3, bf16[2,4,32768]{2,1,0:T(4,128)(2,1)S(1)} %copy-done.2, s32[]{:T(128)S(6)} %select_n.29), kind=kLoop, calls=%fused_computation.24 | loop fusion | flops 262144 | bytes 1048581 | tf_op jit(solution)/shard_map/jit(_where)/select_n | solution.py:95
  4.0 0.6 %pad_maximum_fusion.2 = bf16[2,2,80896]{2,1,0:T(2,128)(2,1)S(1)} fusion(bf16[2,2,32768]{2,1,0:T(2,128)(2,1)S(1)} %get-tuple-element.15, bf16[2,2,32768]{2,1,0:T(2,128)(2,1)S(1)} %get-tuple-element.14, bf16[2,2,15360]{2,1,0:T(2,128)(2,1)S(1)} %constant_dynamic-slice_fusion.1), kind=kLoop, calls=%fused_computation.10 | loop fusion | flops 1941504 | bytes 1294336 | tf_op jit(solution)/shard_map/concatenate | solution.py:98
  4.5 2.6 %fusion.28 = (bf16[2,1,80896]{2,1,0:T(2,128)(2,1)S(1)}, bf16[2,80896]{1,0:T(2,128)(2,1)S(1)}) fusion(bf16[2,2,80896]{2,1,0:T(2,128)(2,1)S(1)} %pad_maximum_fusion.2), kind=kLoop, calls=%fused_computation.80 | loop fusion | bytes 1294336 | tf_op jit(solution)/shard_map/slice | solution.py:112
  7.1 0.2 reshape.783
  7.3 0.9 %fusion.5 = f32[2,1,64,1024]{3,2,0,1:T(8,128)S(1)} fusion(bf16[2,1,79,1024]{3,2,0,1:T(8,128)(2,1)S(1)} %reshape.783, f32[1024]{0:T(1024)S(1)} %bitcast.79, f32[1024]{0:T(1024)S(1)} %bitcast.81, f32[1024]{0:T(1024)S(1)} %bitcast.53, f32[1024]{0:T(1024)S(1)} %bitcast.55, f32[1024]{0:T(1024)S(1)} %bitcast.57, f32[1024]{0:T(1024)S(1)} %bitcast.59, ...), kind=kLoop, calls=%fused_computation.35 | loop fusion | flops 6422528 | bytes 4784128 | tf_op jit(solution)/shard_map/convert_element_type | solution.py:42
  8.2 0.0 copy-start.3
  8.2 0.0 copy-start.4
  8.3 0.6 %copy-done.3 = f32[4,256]{1,0:T(4,128)S(1)} copy-done((f32[4,256]{1,0:T(4,128)S(1)}, f32[4,256]{1,0:T(4,128)}, u32[]{:S(2)}) %copy-start.3) | copy-done | bytes 4120
  8.9 0.0 copy-done.4
  8.9 0.1 fusion.27
  9.0 0.1 maximum_bitcast_fusion
  9.1 0.1 pad_maximum_fusion
  9.2 0.0 copy-start.1
  9.2 0.1 copy.20
  9.3 1.0 %copy-done.1 = f32[512,256]{1,0:T(8,128)S(1)} copy-done((f32[512,256]{1,0:T(8,128)S(1)}, f32[512,256]{1,0:T(8,128)}, u32[]{:S(2)}) %copy-start.1) | copy-done | bytes 524312
  10.2 1.3 %convolution_convert_fusion.1 = bf16[512,256]{0,1:T(8,128)(2,1)} fusion(f32[512,512]{1,0:T(8,128)S(1)} %bitcast.48, f32[512,256]{1,0:T(8,128)S(1)} %copy-done.1), kind=kOutput, calls=%fused_computation.4 | convolution fusion | flops 402784256 | bytes 1835008 | tf_op jit(solution)/shard_map/dot_general | solution.py:58
  11.6 2.3 %reduce.1 = bf16[2,80896]{1,0:T(2,128)(2,1)S(1)} reduce(bf16[2,1,80896]{2,1,0:T(2,128)(2,1)S(1)} %get-tuple-element.9, bf16[]{:T(256)} %constant.38), dimensions={1}, to_apply=%get-tuple-element.9.reduce_sub_computation | reduce | bytes 647170 | tf_op jit(solution)/shard_map/optimization_barrier | solution.py:112
  13.8 0.2 reshape.786
  14.0 0.9 %fusion.6 = f32[2,1,64,1024]{3,2,0,1:T(8,128)S(1)} fusion(bf16[2,1,79,1024]{3,2,0,1:T(8,128)(2,1)S(1)} %reshape.786, f32[1024]{0:T(1024)S(1)} %bitcast.80, f32[1024]{0:T(1024)S(1)} %bitcast.82, f32[1024]{0:T(1024)S(1)} %bitcast.54, f32[1024]{0:T(1024)S(1)} %bitcast.56, f32[1024]{0:T(1024)S(1)} %bitcast.58, f32[1024]{0:T(1024)S(1)} %bitcast.60, ...), kind=kLoop, calls=%fused_computation.36 | loop fusion | flops 6422528 | bytes 4784128 | tf_op jit(solution)/shard_map/convert_element_type | solution.py:42
  15.0 0.1 fusion.26
  15.1 0.1 maximum_bitcast_fusion.2
  15.2 0.1 pad_maximum_fusion.1
  15.3 0.1 copy.21
  15.4 0.0 copy-start.5
  15.4 0.0 copy-start.6
  15.4 1.3 %convolution_convert_fusion = bf16[512,256]{0,1:T(8,128)(2,1)} fusion(f32[512,512]{1,0:T(8,128)S(1)} %bitcast.47, f32[512,256]{1,0:T(8,128)S(1)} %copy-done.1), kind=kOutput, calls=%fused_computation.3 | convolution fusion | flops 402784256 | bytes 1835008 | tf_op jit(solution)/shard_map/dot_general | solution.py:58
  16.7 7.0 %all-to-all-start.1 = ((bf16[16,16,512]{2,1,0:T(8,128)(2,1)}), bf16[16,16,512]{2,1,0:T(8,128)(2,1)S(1)}, u32[]{:S(2)}, u32[]{:S(2)}) async-start(bf16[16,16,512]{2,1,0:T(8,128)(2,1)} %bitcast.25), calls=%async_computation.1 | async-start | bytes 524288 | tf_op jit(solution)/shard_map/all_to_all | solution.py:113
  23.7 0.0 copy-done.5
  23.8 0.0 copy-done.6
  23.8 0.6 %scatter_custom_fusion = s32[16]{0:T(128)S(1)} fusion(s32[16]{0:T(128)S(1)} %compare_select_fusion.1, s32[16]{0:T(128)S(1)} %iota.3, s32[]{:T(128)} %constant.4.clone.1), kind=kCustom, calls=%fused_computation.75 | custom fusion | bytes 68 | tf_op jit(solution)/shard_map/scatter | solution.py:103
  24.4 9.4 %all-to-all-done.1 = bf16[16,16,512]{2,1,0:T(8,128)(2,1)S(1)} async-done(((bf16[16,16,512]{2,1,0:T(8,128)(2,1)}), bf16[16,16,512]{2,1,0:T(8,128)(2,1)S(1)}, u32[]{:S(2)}, u32[]{:S(2)}) %all-to-all-start.1) | async-done | bytes 262176 | tf_op jit(solution)/shard_map/all_to_all | solution.py:113
  33.8 3.7 %all-to-all-start = ((bf16[16,16,512]{2,1,0:T(8,128)(2,1)}), bf16[16,16,512]{2,1,0:T(8,128)(2,1)S(1)}, u32[]{:S(2)}, u32[]{:S(2)}) async-start(bf16[16,16,512]{2,1,0:T(8,128)(2,1)} %bitcast.20), calls=%async_computation | async-start | bytes 524288 | tf_op jit(solution)/shard_map/all_to_all | solution.py:113
  37.6 0.6 %gather_fusion.1 = bf16[16,16,512]{2,1,0:T(8,128)(2,1)S(1)} fusion(bf16[16,16,512]{2,1,0:T(8,128)(2,1)S(1)} %all-to-all-done.1, s32[1024]{0:T(1024)S(1)} %pad_clamp_fusion), kind=kCustom, calls=%fused_computation.1.clone | custom fusion | bytes 524352 | tf_op jit(solution)/shard_map/jit(_take)/gather | solution.py:114
  38.1 9.2 %all-to-all-done = bf16[16,16,512]{2,1,0:T(8,128)(2,1)S(1)} async-done(((bf16[16,16,512]{2,1,0:T(8,128)(2,1)}), bf16[16,16,512]{2,1,0:T(8,128)(2,1)S(1)}, u32[]{:S(2)}, u32[]{:S(2)}) %all-to-all-start) | async-done | bytes 262176 | tf_op jit(solution)/shard_map/all_to_all | solution.py:113
  47.3 0.6 %gather_fusion = bf16[16,16,512]{2,1,0:T(8,128)(2,1)S(1)} fusion(bf16[16,16,512]{2,1,0:T(8,128)(2,1)S(1)} %all-to-all-done, s32[1024]{0:T(1024)S(1)} %pad_clamp_fusion), kind=kCustom, calls=%fused_computation.clone | custom fusion | bytes 524352 | tf_op jit(solution)/shard_map/jit(_take)/gather | solution.py:114
  47.9 0.1 select_multiply_fusion.1
  48.1 0.1 stack_reshape.6
  48.1 0.5 copy.22
  48.6 0.1 stack_reshape.7
  48.7 0.5 copy.23
  49.2 1.2 %pad_maximum_fusion.3 = bf16[16,2,16,4,128]{4,1,0,3,2:T(2,128)(2,1)S(1)} fusion(bf16[16,1,16,4,128]{4,1,0,3,2:T(2,128)(2,1)S(1)} %copy.23, bf16[16,1,16,4,128]{4,1,0,3,2:T(2,128)(2,1)S(1)} %copy.22), kind=kLoop, calls=%fused_computation.16 | loop fusion | flops 1048576 | bytes 1048576 | tf_op jit(solution)/shard_map/stack | solution.py:116
  50.4 0.2 slice_negate_fusion
  50.7 0.4 fusion.30
  51.1 0.5 fusion.1
  51.5 0.6 %copy.25 = f32[64,32,32]{0,2,1:T(8,128)S(1)} copy(f32[64,32,32]{2,1,0:T(8,128)S(1)} %fusion.1) | data formatting | bytes 524288 | tf_op jit(solution)/shard_map/cak,cbk->cab/dot_general | solution.py:76
  52.1 0.6 %copy.24 = f32[64,32,32]{0,2,1:T(8,128)S(1)} copy(f32[64,32,32]{2,1,0:T(8,128)S(1)} %fusion.30) | data formatting | bytes 524288 | tf_op jit(solution)/shard_map/cak,cbk->cab/dot_general | solution.py:75
  52.7 0.9 %fusion = bf16[2,64,32,32]{1,3,2,0:T(8,128)(2,1)} fusion(f32[1,64,32,32]{1,3,2,0:T(8,128)S(1)} %bitcast.49, f32[1,64,32,32]{1,3,2,0:T(8,128)S(1)} %bitcast.50), kind=kLoop, calls=%fused_computation.8 | loop fusion | flops 393216 | bytes 786432 | tf_op jit(solution)/shard_map/convert_element_type | solution.py:77
  (10 shorter events, 0.2 us)
Async XLA Ops:
  0.0 1.9 %copy-start = (bf16[2,4,15360]{2,1,0:T(4,128)(2,1)S(1)}, bf16[2,4,15360]{2,1,0:T(4,128)(2,1)}, u32[]{:S(2)}) copy-start(bf16[2,4,15360]{2,1,0:T(4,128)(2,1)} %param.14) | copy-start | bytes 737284
  0.0 3.4 %copy-start.2 = (bf16[2,4,32768]{2,1,0:T(4,128)(2,1)S(1)}, bf16[2,4,32768]{2,1,0:T(4,128)(2,1)}, u32[]{:S(2)}) copy-start(bf16[2,4,32768]{2,1,0:T(4,128)(2,1)} %param.13) | copy-start | bytes 1572868
  1.4 2.0 %collective-permute-start = (bf16[2,2,32768]{2,1,0:T(2,128)(2,1)S(1)}, bf16[2,2,32768]{2,1,0:T(2,128)(2,1)S(1)}, u32[]{:S(2)}, u32[]{:S(2)}) collective-permute-start(bf16[2,2,32768]{2,1,0:T(2,128)(2,1)S(1)} %constant_dynamic-slice_fusion), channel_id=1, source_target_pairs={{0,1},{1,0},{2,3},{3,2},{4,5},{5,4},{6,7},{7,6},{8,9},{9,8},{10,11... | collective-permute-start | bytes 786440 | tf_op jit(solution)/shard_map/ppermute | solution.py:93
  8.2 0.7 %copy-start.3 = (f32[4,256]{1,0:T(4,128)S(1)}, f32[4,256]{1,0:T(4,128)}, u32[]{:S(2)}) copy-start(f32[4,256]{1,0:T(4,128)} %constant.11.clone) | copy-start | bytes 12292
  8.2 0.7 %copy-start.4 = (f32[4,256]{1,0:T(4,128)S(1)}, f32[4,256]{1,0:T(4,128)}, u32[]{:S(2)}) copy-start(f32[4,256]{1,0:T(4,128)} %constant.12.clone) | copy-start | bytes 12292
  9.2 1.0 %copy-start.1 = (f32[512,256]{1,0:T(8,128)S(1)}, f32[512,256]{1,0:T(8,128)}, u32[]{:S(2)}) copy-start(f32[512,256]{1,0:T(8,128)} %constant.17.clone) | copy-start | bytes 1572868
  15.4 8.4 %copy-start.5 = (s32[16]{0:T(128)S(1)}, s32[16]{0:T(128)}, u32[]{:S(2)}) copy-start(s32[16]{0:T(128)} %param.17) | copy-start | bytes 196
  15.4 8.4 %copy-start.6 = (s32[16]{0:T(128)S(1)}, s32[16]{0:T(128)}, u32[]{:S(2)}) copy-start(s32[16]{0:T(128)} %param.16) | copy-start | bytes 196
  16.7 17.1 %all-to-all-start.1 = ((bf16[16,16,512]{2,1,0:T(8,128)(2,1)}), bf16[16,16,512]{2,1,0:T(8,128)(2,1)S(1)}, u32[]{:S(2)}, u32[]{:S(2)}) async-start(bf16[16,16,512]{2,1,0:T(8,128)(2,1)} %bitcast.25), calls=%async_computation.1 | async-start | bytes 524288 | tf_op jit(solution)/shard_map/all_to_all | solution.py:113
  33.8 13.5 %all-to-all-start = ((bf16[16,16,512]{2,1,0:T(8,128)(2,1)}), bf16[16,16,512]{2,1,0:T(8,128)(2,1)S(1)}, u32[]{:S(2)}, u32[]{:S(2)}) async-start(bf16[16,16,512]{2,1,0:T(8,128)(2,1)} %bitcast.20), calls=%async_computation | async-start | bytes 524288 | tf_op jit(solution)/shard_map/all_to_all | solution.py:113

commit v4 on v2

--- a/solution.py
+++ b/solution.py
@@ -27,9 +27,10 @@
 def filter_bank(extended, coefficients, spec_count):
     tap_count, fft_len = coefficients.shape
     blocks = extended.reshape(extended.shape[0], extended.shape[1], -1, fft_len)
+    weights = coefficients.reshape(tap_count, 1, fft_len)
     running = jnp.zeros((extended.shape[0], extended.shape[1], spec_count, fft_len), jnp.float32)
     for tap_index in range(tap_count):
-        running = running + coefficients[tap_index] * blocks[
+        running = running + weights[tap_index] * blocks[
             :, :, tap_index : tap_index + spec_count, :
         ].astype(jnp.float32)
     return running.astype(jnp.bfloat16)
@@ -88,14 +89,16 @@
     kl_count = inner // dest_count
     keep = row_count // half_count
     t = lax.axis_index("tch")
-    own = lax.dynamic_slice_in_dim(samples, t * keep, keep, axis=1)
-    other = lax.dynamic_slice_in_dim(samples, (1 - t) * keep, keep, axis=1)
+    blocks = samples.reshape(2, row_count, -1, fft_len)
+    before = history.reshape(2, row_count, -1, fft_len)
+    own = lax.dynamic_slice_in_dim(blocks, t * keep, keep, axis=1)
+    other = lax.dynamic_slice_in_dim(blocks, (1 - t) * keep, keep, axis=1)
     received = lax.ppermute(other, "tch", [(0, 1), (1, 0)])
     is_first = t == 0
     first = jnp.where(is_first, own, received)
     second = jnp.where(is_first, received, own)
-    earlier = lax.dynamic_slice_in_dim(history, t * keep, keep, axis=1)
-    extended = jnp.concatenate([earlier, first, second], axis=2)
+    earlier = lax.dynamic_slice_in_dim(before, t * keep, keep, axis=1)
+    extended = jnp.concatenate([earlier, first, second], axis=2).reshape(2, keep, -1)
     spec_total = (extended.shape[2] - (tap_count - 1) * fft_len) // fft_len
     spectra = channelize(filter_bank(extended, coefficients, spec_total))
     spectra = spectra.reshape(dest_count, kl_count, -1)

time: 39.2 us -> 36.4 us (0.929)
  other arithmetic: 6.91 us -> 4.92 us
  local copies, waits for them, and re-layouts: 7.54 us -> 6.74 us
    reshape x1 -> x2, local copies, waits for them, and re-layouts: 0.43 us -> 2.54 us  [the longest x1 1.45 us: local(): blocks = samples.reshape(2, row_count, -1, fft_len)]
    select_n x1, other arithmetic: 1.61 us -> 0.05 us  [local(): first = jnp.where(is_first, own, received)]
    dynamic_slice x2, local copies, waits for them, and re-layouts: 1.49 us -> 0.05 us  [the longest x1 0.03 us: local(): other = lax.dynamic_slice_in_dim(blocks, (1 - t) * keep, keep, axis=1)]
    slice x1, local copies, waits for them, and re-layouts: 1.29 us -> 0.05 us  [filter_bank(): weights[tap_index]]
    concatenate x1, other arithmetic: 0.56 us -> 0.16 us  [local(): jnp.concatenate([earlier, first, second], axis=2).reshape(2, keep, -1)]
where the time goes in v4:
time: 36.4 us; the launch traced here: 36.1 us
  waiting for transfers between devices  13.7 us (38%)
  starting transfers between devices  7.74 us (21%)
  local copies, waits for them, and re-layouts  6.74 us (19%)
  other arithmetic  4.92 us (14%)
  matrix products  2.71 us (7%)
    all_to_all x1, waiting for transfers between devices, local(): lax.all_to_all(spectra, ('blk', 'tch'), split_axis=0, concat_axis=0, tile...  13.7 us
    all_to_all x1, starting transfers between devices, local(): lax.all_to_all(spectra, ('blk', 'tch'), split_axis=0, concat_axis=0, tile...  7.22 us
    convert_element_type x1, other arithmetic, channelize(): x = filtered.astype(jnp.float32)  2.12 us
    dot_general x1, matrix products, channelize(): lax.dot_general(jnp.asarray(inner_matrix), rows, (((0,), (1,)), ((), ()))...  1.84 us
    reshape x1, local copies, waits for them, and re-layouts, local(): blocks = samples.reshape(2, row_count, -1, fft_len)  1.45 us
    unnamed x12, local copies, waits for them, and re-layouts  1.35 us
    reshape x1, local copies, waits for them, and re-layouts, local(): before = history.reshape(2, row_count, -1, fft_len)  1.09 us
    gather x2, local copies, waits for them, and re-layouts, local(): gathered = jnp.take(turned, slot_index, axis=0) * keep_mask[:, None, None]  0.95 us
  transfers between devices with their start and end apart: 2, of which 1 were waited for; matrix products, arithmetic and copies ran while one was open for 5% of the time, Pallas kernels for 0%

profile of v4, /device:TPU:0, one launch (start us, length us, event | category | flops | bytes accessed | tf_op | source)
XLA Modules:
  0.0 36.1 jit_solution(14735896147218100802)
XLA Ops:
  0.0 0.0 copy-start.1
  0.0 1.4 %reshape.75 = bf16[2,4,32,1024]{3,2,1,0:T(8,128)(2,1)S(1)} reshape(bf16[2,4,32768]{2,1,0:T(4,128)(2,1)} %param.8) | data formatting | bytes 1048576 | tf_op jit(solution)/shard_map/reshape | solution.py:92
  1.5 0.5 %collective-permute-start = (bf16[2,2,32,1024]{3,2,1,0:T(8,128)(2,1)S(1)}, bf16[2,2,32,1024]{3,2,1,0:T(8,128)(2,1)S(1)}, u32[]{:S(2)}, u32[]{:S(2)}) collective-permute-start(bf16[2,2,32,1024]{3,2,1,0:T(8,128)(2,1)S(1)} %constant_dynamic-slice_fusion), channel_id=1, source_target_pairs={{0,1},{1,0},{2,3},{3,2},{4,5},{5,4},{6,7},{7,6},{8,9},{9,8},{10,11... | collective-permute-start | bytes 786440 | tf_op jit(solution)/shard_map/ppermute | solution.py:96
  2.0 1.1 %reshape.74 = bf16[2,4,15,1024]{3,2,1,0:T(8,128)(2,1)S(1)} reshape(bf16[2,4,15360]{2,1,0:T(4,128)(2,1)} %param.9) | data formatting | bytes 491520 | tf_op jit(solution)/shard_map/reshape | solution.py:93
  3.1 0.0 copy-done.1
  3.2 0.0 collective-permute-done
  3.3 0.2 pad_maximum_fusion.1
  3.4 2.1 %fusion.6 = f32[2,2,64,1024]{3,2,1,0:T(8,128)S(1)} fusion(bf16[2,2,32,1024]{3,2,1,0:T(8,128)(2,1)S(1)} %get-tuple-element.17, bf16[2,2,32,1024]{3,2,1,0:T(8,128)(2,1)S(1)} %get-tuple-element.16, f32[1024]{0:T(1024)S(1)} %bitcast.56, bf16[2,2,79,1024]{3,2,1,0:T(8,128)(2,1)S(1)} %pad_maximum_fusion.1, f32[1024]{0:T(1024)S(1)} %bitcast.57, ...), kind=kLoop, calls=%fused_computation.21 | loop fusion | flops 13631488 | bytes 9502720 | tf_op jit(solution)/shard_map/convert_element_type | solution.py:43
  5.6 0.0 copy-start.2
  5.6 0.0 copy-start.3
  5.6 0.1 fusion.8
  5.7 0.1 fusion.10
  5.7 0.5 %copy-done.2 = f32[4,256]{1,0:T(4,128)S(1)} copy-done((f32[4,256]{1,0:T(4,128)S(1)}, f32[4,256]{1,0:T(4,128)}, u32[]{:S(2)}) %copy-start.2) | copy-done | bytes 4120
  6.3 0.0 copy-done.3
  6.3 0.2 fusion.18
  6.5 0.2 maximum_bitcast_fusion
  6.7 0.0 copy-start
  6.7 0.2 pad_maximum_fusion
  7.0 0.8 %copy-done = f32[512,256]{1,0:T(8,128)S(1)} copy-done((f32[512,256]{1,0:T(8,128)S(1)}, f32[512,256]{1,0:T(8,128)}, u32[]{:S(2)}) %copy-start) | copy-done | bytes 524312
  7.8 0.0 copy-start.4
  7.8 0.0 copy-start.5
  7.8 1.8 %convolution_convert_fusion = bf16[1024,256]{0,1:T(8,128)(2,1)} fusion(f32[1024,512]{1,0:T(8,128)S(1)} %bitcast.39, f32[512,256]{1,0:T(8,128)S(1)} %copy-done), kind=kOutput, calls=%fused_computation.3 | convolution fusion | flops 805568512 | bytes 3145728 | tf_op jit(solution)/shard_map/dot_general | solution.py:59
  9.6 7.2 %all-to-all-start = ((bf16[16,16,1024]{2,1,0:T(8,128)(2,1)}), bf16[16,16,1024]{2,1,0:T(8,128)(2,1)S(1)}, u32[]{:S(2)}, u32[]{:S(2)}) async-start(bf16[16,16,1024]{2,1,0:T(8,128)(2,1)} %bitcast.21), calls=%async_computation | async-start | bytes 1048576 | tf_op jit(solution)/shard_map/all_to_all | solution.py:105
  16.8 0.0 copy-done.4
  16.9 0.0 copy-done.5
  16.9 0.6 %scatter_custom_fusion = s32[16]{0:T(128)S(1)} fusion(s32[16]{0:T(128)S(1)} %compare_select_fusion.1, s32[16]{0:T(128)S(1)} %iota.3, s32[]{:T(128)} %constant.12.clone.1), kind=kCustom, calls=%fused_computation.46 | custom fusion | bytes 68 | tf_op jit(solution)/shard_map/scatter | solution.py:109
  17.6 13.7 %all-to-all-done = bf16[16,16,1024]{2,1,0:T(8,128)(2,1)S(1)} async-done(((bf16[16,16,1024]{2,1,0:T(8,128)(2,1)}), bf16[16,16,1024]{2,1,0:T(8,128)(2,1)S(1)}, u32[]{:S(2)}, u32[]{:S(2)}) %all-to-all-start) | async-done | bytes 524320 | tf_op jit(solution)/shard_map/all_to_all | solution.py:105
  31.3 0.6 %gather_fusion = bf16[16,16,1024]{2,1,0:T(8,128)(2,1)S(1)} fusion(bf16[16,16,1024]{2,1,0:T(8,128)(2,1)S(1)} %all-to-all-done, s32[1024]{0:T(1024)S(1)} %pad_clamp_fusion), kind=kCustom, calls=%fused_computation | custom fusion | bytes 1048640 | tf_op jit(solution)/shard_map/jit(_take)/gather | solution.py:112
  31.9 0.4 %gather.7 = bf16[16,16,4,2,128]{4,3,2,1,0:T(2,128)(2,1)S(1)} reshape(bf16[16,16,1024]{2,1,0:T(8,128)(2,1)S(1)} %gather_fusion) | data formatting | bytes 1048576 | tf_op jit(solution)/shard_map/jit(_take)/gather | solution.py:112
  32.3 0.6 %fusion.5 = bf16[16,16,4,2,128]{4,3,0,2,1:T(2,128)(2,1)S(1)} fusion(bf16[16,16,4,2,128]{4,3,2,1,0:T(2,128)(2,1)S(1)} %gather.7, pred[16]{0:T(512)(128)(4,1)S(1)} %compare_and_fusion, bf16[16]{0:T(256)(128)(2,1)S(1)} %convert_element_type.86), kind=kLoop, calls=%fused_computation.20 | loop fusion | flops 524288 | bytes 1048624 | tf_op jit(solution)/shard_map/mul | solution.py:112
  32.9 0.2 slice_negate_fusion
  33.1 0.4 %fusion.20 = f32[64,32,32]{2,1,0:T(8,128)S(1)} fusion(bf16[64,32,128]{2,1,0:T(8,128)(2,1)S(1)} %bitcast.37), kind=kOutput, calls=%fused_computation.51 | convolution fusion | flops 16777216 | bytes 786432 | tf_op jit(solution)/shard_map/cak,cbk->cab/dot_general | solution.py:76
  33.5 0.5 %fusion.1 = f32[64,32,32]{2,1,0:T(8,128)S(1)} fusion(bf16[64,32,128]{2,1,0:T(8,128)(2,1)S(1)} %bitcast.38, bf16[64,32,64]{2,1,0:T(8,128)(2,1)S(1)} %get-tuple-element.19, bf16[64,32,64]{2,1,0:T(8,128)(2,1)S(1)} %get-tuple-element.18), kind=kOutput, calls=%fused_computation.14 | convolution fusion | flops 17825792 | bytes 1310720 | tf_op jit(solution)/shard_map/cak,cbk->cab/dot_general | solution.py:77
  34.0 0.6 %copy.17 = f32[64,32,32]{0,2,1:T(8,128)S(1)} copy(f32[64,32,32]{2,1,0:T(8,128)S(1)} %fusion.1) | data formatting | bytes 524288 | tf_op jit(solution)/shard_map/cak,cbk->cab/dot_general | solution.py:77
  34.6 0.6 %copy.16 = f32[64,32,32]{0,2,1:T(8,128)S(1)} copy(f32[64,32,32]{2,1,0:T(8,128)S(1)} %fusion.20) | data formatting | bytes 524288 | tf_op jit(solution)/shard_map/cak,cbk->cab/dot_general | solution.py:76
  35.2 0.9 %fusion = bf16[2,64,32,32]{1,3,2,0:T(8,128)(2,1)} fusion(f32[1,64,32,32]{1,3,2,0:T(8,128)S(1)} %bitcast.40, f32[1,64,32,32]{1,3,2,0:T(8,128)S(1)} %bitcast.41), kind=kLoop, calls=%fused_computation.7 | loop fusion | flops 393216 | bytes 786432 | tf_op jit(solution)/shard_map/convert_element_type | solution.py:78
  (10 shorter events, 0.2 us)
Async XLA Ops:
  0.0 3.1 %copy-start.1 = (f32[16,1024]{1,0:T(8,128)S(1)}, f32[16,1024]{1,0:T(8,128)}, u32[]{:S(2)}) copy-start(f32[16,1024]{1,0:T(8,128)} %param.10) | copy-start | bytes 196612
  1.5 1.7 %collective-permute-start = (bf16[2,2,32,1024]{3,2,1,0:T(8,128)(2,1)S(1)}, bf16[2,2,32,1024]{3,2,1,0:T(8,128)(2,1)S(1)}, u32[]{:S(2)}, u32[]{:S(2)}) collective-permute-start(bf16[2,2,32,1024]{3,2,1,0:T(8,128)(2,1)S(1)} %constant_dynamic-slice_fusion), channel_id=1, source_target_pairs={{0,1},{1,0},{2,3},{3,2},{4,5},{5,4},{6,7},{7,6},{8,9},{9,8},{10,11... | collective-permute-start | bytes 786440 | tf_op jit(solution)/shard_map/ppermute | solution.py:96
  5.6 0.7 %copy-start.2 = (f32[4,256]{1,0:T(4,128)S(1)}, f32[4,256]{1,0:T(4,128)}, u32[]{:S(2)}) copy-start(f32[4,256]{1,0:T(4,128)} %constant.37.clone) | copy-start | bytes 12292
  5.6 0.7 %copy-start.3 = (f32[4,256]{1,0:T(4,128)S(1)}, f32[4,256]{1,0:T(4,128)}, u32[]{:S(2)}) copy-start(f32[4,256]{1,0:T(4,128)} %constant.38.clone) | copy-start | bytes 12292
  6.7 1.0 %copy-start = (f32[512,256]{1,0:T(8,128)S(1)}, f32[512,256]{1,0:T(8,128)}, u32[]{:S(2)}) copy-start(f32[512,256]{1,0:T(8,128)} %constant.39.clone) | copy-start | bytes 1572868
  7.8 9.1 %copy-start.4 = (s32[16]{0:T(128)S(1)}, s32[16]{0:T(128)}, u32[]{:S(2)}) copy-start(s32[16]{0:T(128)} %param.12) | copy-start | bytes 196
  7.8 9.1 %copy-start.5 = (s32[16]{0:T(128)S(1)}, s32[16]{0:T(128)}, u32[]{:S(2)}) copy-start(s32[16]{0:T(128)} %param.11) | copy-start | bytes 196
  9.6 21.7 %all-to-all-start = ((bf16[16,16,1024]{2,1,0:T(8,128)(2,1)}), bf16[16,16,1024]{2,1,0:T(8,128)(2,1)S(1)}, u32[]{:S(2)}, u32[]{:S(2)}) async-start(bf16[16,16,1024]{2,1,0:T(8,128)(2,1)} %bitcast.21), calls=%async_computation | async-start | bytes 1048576 | tf_op jit(solution)/shard_map/all_to_all | solution.py:105

commit v5 on v4

--- a/solution.py
+++ b/solution.py
@@ -56,11 +56,13 @@
     real_rows = jnp.concatenate([zr, zi], axis=-1)
     imag_rows = jnp.concatenate([zi, -zr], axis=-1)
     rows = jnp.stack([real_rows, imag_rows], axis=2).reshape(RADIX * pol_count * 2 * spec_count, 2 * inner)
+    rows_high = rows.astype(jnp.bfloat16)
+    rows_rest = (rows - rows_high.astype(jnp.float32)).astype(jnp.bfloat16)
+    table = inner_matrix.astype(jnp.bfloat16)
     product = lax.dot_general(
-        jnp.asarray(inner_matrix),
-        rows,
+        jnp.concatenate([table, table], axis=0),
+        jnp.concatenate([rows_high, rows_rest], axis=1),
         (((0,), (1,)), ((), ())),
-        precision=lax.Precision.HIGH,
         preferred_element_type=jnp.float32,
     )
     return product.astype(jnp.bfloat16)
@@ -72,10 +74,11 @@
 
 
 def correlate_full(ordered, inverse_count):
-    rotated = rotate_parts(ordered)
-    real_vis = jnp.einsum("cak,cbk->cab", ordered, ordered, preferred_element_type=jnp.float32)
-    imag_vis = jnp.einsum("cak,cbk->cab", ordered, rotated, preferred_element_type=jnp.float32)
-    return (jnp.stack([real_vis, imag_vis], axis=0) * inverse_count).astype(jnp.bfloat16)
+    both = jnp.concatenate([ordered, rotate_parts(ordered)], axis=1)
+    vis = jnp.einsum("cak,cjk->caj", ordered, both, preferred_element_type=jnp.float32)
+    input_count = ordered.shape[1]
+    vis = jnp.stack([vis[:, :, :input_count], vis[:, :, input_count:]], axis=0)
+    return (vis * inverse_count).astype(jnp.bfloat16)
 
 
 def local(samples, history, coefficients, station_of_slot, station_ok):

time: 36.4 us -> 36.8 us (1.011)
    dot_general x2 -> x0, local copies, waits for them, and re-layouts: 1.19 us -> none  [the longest x1 0.6 us: correlate_full(): jnp.einsum('cak,cbk->cab', ordered, rotated, preferred_element_type=jnp.f...]
    unnamed x12 -> x14, local copies, waits for them, and re-layouts: 1.35 us -> 2.45 us
    slice x0 -> x1, local copies, waits for them, and re-layouts: none -> 0.37 us  [correlate_full(): vis = jnp.stack([vis[:, :, :input_count], vis[:, :, input_count:]], axis=0)]
    convert_element_type x1 -> x2, other arithmetic: 0.93 us -> 1.16 us  [the longest x1 0.93 us: correlate_full(): return (vis * inverse_count).astype(jnp.bfloat16)]
where the time goes in v5:
time: 36.8 us; the launch traced here: 36.5 us
  waiting for transfers between devices  13.7 us (37%)
  starting transfers between devices  7.74 us (21%)
  local copies, waits for them, and re-layouts  7.02 us (19%)
  other arithmetic  5.19 us (14%)
  matrix products  2.48 us (7%)
    all_to_all x1, waiting for transfers between devices, local(): lax.all_to_all(spectra, ('blk', 'tch'), split_axis=0, concat_axis=0, tile...  13.7 us
    all_to_all x1, starting transfers between devices, local(): lax.all_to_all(spectra, ('blk', 'tch'), split_axis=0, concat_axis=0, tile...  7.22 us
    unnamed x14, local copies, waits for them, and re-layouts  2.45 us
    convert_element_type x1, other arithmetic, channelize(): x = filtered.astype(jnp.float32)  2.12 us
    dot_general x2, matrix products, channelize(): lax.dot_general(jnp.concatenate([table, table], axis=0), jnp.concatenate(...  1.76 us
    reshape x1, local copies, waits for them, and re-layouts, local(): blocks = samples.reshape(2, row_count, -1, fft_len)  1.45 us
    reshape x1, local copies, waits for them, and re-layouts, local(): before = history.reshape(2, row_count, -1, fft_len)  1.09 us
    gather x2, local copies, waits for them, and re-layouts, local(): gathered = jnp.take(turned, slot_index, axis=0) * keep_mask[:, None, None]  0.95 us
  transfers between devices with their start and end apart: 2, of which 1 were waited for; matrix products, arithmetic and copies ran while one was open for 5% of the time, Pallas kernels for 0%

profile of v5, /device:TPU:0, one launch (start us, length us, event | category | flops | bytes accessed | tf_op | source)
XLA Modules:
  0.0 36.5 jit_solution(12364060535571524925)
XLA Ops:
  0.0 0.0 copy-start.1
  0.0 1.4 %reshape.75 = bf16[2,4,32,1024]{3,2,1,0:T(8,128)(2,1)S(1)} reshape(bf16[2,4,32768]{2,1,0:T(4,128)(2,1)} %param.9) | data formatting | bytes 1048576 | tf_op jit(solution)/shard_map/reshape | solution.py:95
  1.5 0.5 %collective-permute-start = (bf16[2,2,32,1024]{3,2,1,0:T(8,128)(2,1)S(1)}, bf16[2,2,32,1024]{3,2,1,0:T(8,128)(2,1)S(1)}, u32[]{:S(2)}, u32[]{:S(2)}) collective-permute-start(bf16[2,2,32,1024]{3,2,1,0:T(8,128)(2,1)S(1)} %constant_dynamic-slice_fusion), channel_id=1, source_target_pairs={{0,1},{1,0},{2,3},{3,2},{4,5},{5,4},{6,7},{7,6},{8,9},{9,8},{10,11... | collective-permute-start | bytes 786440 | tf_op jit(solution)/shard_map/ppermute | solution.py:99
  2.0 1.1 %reshape.74 = bf16[2,4,15,1024]{3,2,1,0:T(8,128)(2,1)S(1)} reshape(bf16[2,4,15360]{2,1,0:T(4,128)(2,1)} %param.10) | data formatting | bytes 491520 | tf_op jit(solution)/shard_map/reshape | solution.py:96
  3.1 0.0 copy-done.1
  3.2 0.0 collective-permute-done
  3.3 0.2 pad_maximum_fusion.1
  3.4 2.1 %fusion.10 = f32[2,2,64,1024]{3,2,1,0:T(8,128)S(1)} fusion(bf16[2,2,32,1024]{3,2,1,0:T(8,128)(2,1)S(1)} %get-tuple-element.21, bf16[2,2,32,1024]{3,2,1,0:T(8,128)(2,1)S(1)} %get-tuple-element.20, f32[1024]{0:T(1024)S(1)} %bitcast.57, bf16[2,2,79,1024]{3,2,1,0:T(8,128)(2,1)S(1)} %pad_maximum_fusion.1, f32[1024]{0:T(1024)S(1)} %bitcast.58, ...), kind=kLoop, calls=%fused_computation.27 | loop fusion | flops 13631488 | bytes 9502720 | tf_op jit(solution)/shard_map/convert_element_type | solution.py:43
  5.6 0.0 copy-start.2
  5.6 0.0 copy-start.3
  5.6 0.1 fusion.12
  5.7 0.1 fusion.14
  5.7 0.5 %copy-done.2 = f32[4,256]{1,0:T(4,128)S(1)} copy-done((f32[4,256]{1,0:T(4,128)S(1)}, f32[4,256]{1,0:T(4,128)}, u32[]{:S(2)}) %copy-start.2) | copy-done | bytes 4120
  6.3 0.0 copy-done.3
  6.3 0.2 fusion.22
  6.5 0.2 maximum_bitcast_fusion
  6.7 0.2 pad_maximum_fusion
  7.0 0.0 copy-start
  7.0 0.2 fusion
  7.2 0.7 %copy-done = bf16[512,256]{1,0:T(8,128)(2,1)S(1)} copy-done((bf16[512,256]{1,0:T(8,128)(2,1)S(1)}, bf16[512,256]{1,0:T(8,128)(2,1)}, u32[]{:S(2)}) %copy-start) | copy-done | bytes 262168
  7.9 0.5 %fusion.25 = f32[256,1024]{1,0:T(8,128)S(1)} fusion(bf16[512,256]{1,0:T(8,128)(2,1)S(1)} %copy-done, bf16[1024,512]{1,0:T(8,128)(2,1)S(1)} %get-tuple-element.6), kind=kOutput, calls=%fused_computation.58 | convolution fusion | flops 268435456 | bytes 2359296 | tf_op jit(solution)/shard_map/dot_general | solution.py:62
  8.4 0.0 copy-start.4
  8.4 0.0 copy-start.5
  8.4 1.3 %fusion.1 = bf16[256,1024]{1,0:T(8,128)(2,1)} fusion(f32[256,1024]{1,0:T(8,128)S(1)} %fusion.25, bf16[512,256]{1,0:T(8,128)(2,1)S(1)} %copy-done, bf16[1024,512]{1,0:T(8,128)(2,1)S(1)} %get-tuple-element.5), kind=kOutput, calls=%fused_computation.7 | convolution fusion | flops 268959744 | bytes 2883584 | tf_op jit(solution)/shard_map/dot_general | solution.py:62
  9.7 7.2 %all-to-all-start = ((bf16[16,16,1024]{2,1,0:T(8,128)(2,1)}), bf16[16,16,1024]{2,1,0:T(8,128)(2,1)S(1)}, u32[]{:S(2)}, u32[]{:S(2)}) async-start(bf16[16,16,1024]{2,1,0:T(8,128)(2,1)} %bitcast.20), calls=%async_computation | async-start | bytes 1048576 | tf_op jit(solution)/shard_map/all_to_all | solution.py:108
  17.0 0.0 copy-done.4
  17.0 0.0 copy-done.5
  17.0 0.6 %scatter_custom_fusion = s32[16]{0:T(128)S(1)} fusion(s32[16]{0:T(128)S(1)} %compare_select_fusion.1, s32[16]{0:T(128)S(1)} %iota.3, s32[]{:T(128)} %constant.12.clone.1), kind=kCustom, calls=%fused_computation.52 | custom fusion | bytes 68 | tf_op jit(solution)/shard_map/scatter | solution.py:112
  17.7 13.7 %all-to-all-done = bf16[16,16,1024]{2,1,0:T(8,128)(2,1)S(1)} async-done(((bf16[16,16,1024]{2,1,0:T(8,128)(2,1)}), bf16[16,16,1024]{2,1,0:T(8,128)(2,1)S(1)}, u32[]{:S(2)}, u32[]{:S(2)}) %all-to-all-start) | async-done | bytes 524320 | tf_op jit(solution)/shard_map/all_to_all | solution.py:108
  31.4 0.6 %gather_fusion = bf16[16,16,1024]{2,1,0:T(8,128)(2,1)S(1)} fusion(bf16[16,16,1024]{2,1,0:T(8,128)(2,1)S(1)} %all-to-all-done, s32[1024]{0:T(1024)S(1)} %pad_clamp_fusion), kind=kCustom, calls=%fused_computation | custom fusion | bytes 1048640 | tf_op jit(solution)/shard_map/jit(_take)/gather | solution.py:115
  32.0 0.4 %gather.7 = bf16[16,16,4,2,128]{4,3,2,1,0:T(2,128)(2,1)S(1)} reshape(bf16[16,16,1024]{2,1,0:T(8,128)(2,1)S(1)} %gather_fusion) | data formatting | bytes 1048576 | tf_op jit(solution)/shard_map/jit(_take)/gather | solution.py:115
  32.4 0.6 %fusion.9 = bf16[16,16,4,2,128]{4,3,0,2,1:T(2,128)(2,1)S(1)} fusion(bf16[16,16,4,2,128]{4,3,2,1,0:T(2,128)(2,1)S(1)} %gather.7, pred[16]{0:T(512)(128)(4,1)S(1)} %compare_and_fusion, bf16[16]{0:T(256)(128)(2,1)S(1)} %convert_element_type.94), kind=kLoop, calls=%fused_computation.26 | loop fusion | flops 524288 | bytes 1048624 | tf_op jit(solution)/shard_map/mul | solution.py:115
  33.0 0.2 slice_negate_fusion
  33.2 0.7 %fusion.2 = f32[64,32,64]{2,1,0:T(8,128)S(1)} fusion(bf16[64,32,128]{2,1,0:T(8,128)(2,1)S(1)} %bitcast.40, bf16[64,32,64]{2,1,0:T(8,128)(2,1)S(1)} %get-tuple-element.23, bf16[64,32,64]{2,1,0:T(8,128)(2,1)S(1)} %get-tuple-element.22), kind=kOutput, calls=%fused_computation.10 | convolution fusion | flops 36700160 | bytes 1572864 | tf_op jit(solution)/shard_map/cak,cjk->caj/dot_general | solution.py:78
  34.0 0.4 %fusion.23 = (f32[64,32,32]{2,1,0:T(8,128)S(1)}, f32[64,32,32]{2,1,0:T(8,128)S(1)}) fusion(f32[64,32,64]{2,1,0:T(8,128)S(1)} %fusion.2), kind=kLoop, calls=%fused_computation.56 | loop fusion | bytes 1048576 | tf_op jit(solution)/shard_map/slice | solution.py:80
  34.3 0.6 %copy.19 = f32[64,32,32]{0,2,1:T(8,128)S(1)} copy(f32[64,32,32]{2,1,0:T(8,128)S(1)} %get-tuple-element.10) | data formatting | bytes 524288
  34.9 0.6 %copy.20 = f32[64,32,32]{0,2,1:T(8,128)S(1)} copy(f32[64,32,32]{2,1,0:T(8,128)S(1)} %get-tuple-element.11) | data formatting | bytes 524288
  35.5 0.9 %fusion.8 = bf16[2,64,32,32]{1,3,2,0:T(8,128)(2,1)} fusion(f32[1,64,32,32]{1,3,2,0:T(8,128)S(1)} %bitcast.42, f32[1,64,32,32]{1,3,2,0:T(8,128)S(1)} %bitcast.41), kind=kLoop, calls=%fused_computation.17 | loop fusion | flops 393216 | bytes 786432 | tf_op jit(solution)/shard_map/convert_element_type | solution.py:81
  (10 shorter events, 0.2 us)
Async XLA Ops:
  0.0 3.1 %copy-start.1 = (f32[16,1024]{1,0:T(8,128)S(1)}, f32[16,1024]{1,0:T(8,128)}, u32[]{:S(2)}) copy-start(f32[16,1024]{1,0:T(8,128)} %param.11) | copy-start | bytes 196612
  1.5 1.7 %collective-permute-start = (bf16[2,2,32,1024]{3,2,1,0:T(8,128)(2,1)S(1)}, bf16[2,2,32,1024]{3,2,1,0:T(8,128)(2,1)S(1)}, u32[]{:S(2)}, u32[]{:S(2)}) collective-permute-start(bf16[2,2,32,1024]{3,2,1,0:T(8,128)(2,1)S(1)} %constant_dynamic-slice_fusion), channel_id=1, source_target_pairs={{0,1},{1,0},{2,3},{3,2},{4,5},{5,4},{6,7},{7,6},{8,9},{9,8},{10,11... | collective-permute-start | bytes 786440 | tf_op jit(solution)/shard_map/ppermute | solution.py:99
  5.6 0.7 %copy-start.2 = (f32[4,256]{1,0:T(4,128)S(1)}, f32[4,256]{1,0:T(4,128)}, u32[]{:S(2)}) copy-start(f32[4,256]{1,0:T(4,128)} %constant.37.clone) | copy-start | bytes 12292
  5.6 0.7 %copy-start.3 = (f32[4,256]{1,0:T(4,128)S(1)}, f32[4,256]{1,0:T(4,128)}, u32[]{:S(2)}) copy-start(f32[4,256]{1,0:T(4,128)} %constant.38.clone) | copy-start | bytes 12292
  7.0 1.0 %copy-start = (bf16[512,256]{1,0:T(8,128)(2,1)S(1)}, bf16[512,256]{1,0:T(8,128)(2,1)}, u32[]{:S(2)}) copy-start(bf16[512,256]{1,0:T(8,128)(2,1)} %constant.43) | copy-start | bytes 786436
  8.4 8.5 %copy-start.4 = (s32[16]{0:T(128)S(1)}, s32[16]{0:T(128)}, u32[]{:S(2)}) copy-start(s32[16]{0:T(128)} %param.13) | copy-start | bytes 196
  8.4 8.6 %copy-start.5 = (s32[16]{0:T(128)S(1)}, s32[16]{0:T(128)}, u32[]{:S(2)}) copy-start(s32[16]{0:T(128)} %param.12) | copy-start | bytes 196
  9.7 21.7 %all-to-all-start = ((bf16[16,16,1024]{2,1,0:T(8,128)(2,1)}), bf16[16,16,1024]{2,1,0:T(8,128)(2,1)S(1)}, u32[]{:S(2)}, u32[]{:S(2)}) async-start(bf16[16,16,1024]{2,1,0:T(8,128)(2,1)} %bitcast.20), calls=%async_computation | async-start | bytes 1048576 | tf_op jit(solution)/shard_map/all_to_all | solution.py:108

commit v6 on v4

--- a/solution.py
+++ b/solution.py
@@ -57,10 +57,9 @@
     imag_rows = jnp.concatenate([zi, -zr], axis=-1)
     rows = jnp.stack([real_rows, imag_rows], axis=2).reshape(RADIX * pol_count * 2 * spec_count, 2 * inner)
     product = lax.dot_general(
-        jnp.asarray(inner_matrix),
-        rows,
+        jnp.asarray(inner_matrix).astype(jnp.bfloat16),
+        rows.astype(jnp.bfloat16),
         (((0,), (1,)), ((), ())),
-        precision=lax.Precision.HIGH,
         preferred_element_type=jnp.float32,
     )
     return product.astype(jnp.bfloat16)

time: 36.4 us -> 35.7 us (0.981)
  waiting for transfers between devices: 13.7 us -> 14.6 us
  local copies, waits for them, and re-layouts: 6.74 us -> 5.93 us
  matrix products: 2.71 us -> 2.14 us
    reshape x1, local copies, waits for them, and re-layouts: 1.09 us -> 0.15 us  [local(): before = history.reshape(2, row_count, -1, fft_len)]
    ppermute x1, waiting for transfers between devices: 0.01 us -> 0.9 us  [local(): received = lax.ppermute(other, 'tch', [(0, 1), (1, 0)])]
    dot_general x1, matrix products: 1.84 us -> 1.28 us  [channelize(): lax.dot_general(jnp.asarray(inner_matrix).astype(jnp.bfloat16), rows.asty...]
    unnamed x12 -> x14, local copies, waits for them, and re-layouts: 1.35 us -> 1.46 us
  transfers between devices with their start and end apart: 2 -> 2, of which waited for: 1 -> 2; matrix products, arithmetic and copies ran while one was open for 5% -> 2% of each run, Pallas kernels for 0% -> 0%
where the time goes in v6:
time: 35.7 us; the launch traced here: 35.4 us
  waiting for transfers between devices  14.6 us (41%)
  starting transfers between devices  7.79 us (22%)
  local copies, waits for them, and re-layouts  5.93 us (17%)
  other arithmetic  4.64 us (13%)
  matrix products  2.14 us (6%)
    all_to_all x1, waiting for transfers between devices, local(): lax.all_to_all(spectra, ('blk', 'tch'), split_axis=0, concat_axis=0, tile...  13.7 us
    all_to_all x1, starting transfers between devices, local(): lax.all_to_all(spectra, ('blk', 'tch'), split_axis=0, concat_axis=0, tile...  7.28 us
    convert_element_type x1, other arithmetic, channelize(): x = filtered.astype(jnp.float32)  2.12 us
    unnamed x14, local copies, waits for them, and re-layouts  1.46 us
    reshape x1, local copies, waits for them, and re-layouts, local(): blocks = samples.reshape(2, row_count, -1, fft_len)  1.46 us
    dot_general x1, matrix products, channelize(): lax.dot_general(jnp.asarray(inner_matrix).astype(jnp.bfloat16), rows.asty...  1.28 us
    gather x2, local copies, waits for them, and re-layouts, local(): gathered = jnp.take(turned, slot_index, axis=0) * keep_mask[:, None, None]  0.95 us
    convert_element_type x1, other arithmetic, correlate_full(): (jnp.stack([real_vis, imag_vis], axis=0) * inverse_count).astype(jnp.bflo...  0.93 us
  transfers between devices with their start and end apart: 2, of which 2 were waited for; matrix products, arithmetic and copies ran while one was open for 2% of the time, Pallas kernels for 0%

profile of v6, /device:TPU:0, one launch (start us, length us, event | category | flops | bytes accessed | tf_op | source)
XLA Modules:
  0.0 35.4 jit_solution(1754362028928755386)
XLA Ops:
  0.0 0.0 copy-start.1
  0.0 0.0 copy-start.2
  0.0 1.5 %reshape.74 = bf16[2,4,32,1024]{3,2,1,0:T(8,128)(2,1)S(1)} reshape(bf16[2,4,32768]{2,1,0:T(4,128)(2,1)} %param.8) | data formatting | bytes 1048576 | tf_op jit(solution)/shard_map/reshape | solution.py:91
  1.5 0.5 %collective-permute-start = (bf16[2,2,32,1024]{3,2,1,0:T(8,128)(2,1)S(1)}, bf16[2,2,32,1024]{3,2,1,0:T(8,128)(2,1)S(1)}, u32[]{:S(2)}, u32[]{:S(2)}) collective-permute-start(bf16[2,2,32,1024]{3,2,1,0:T(8,128)(2,1)S(1)} %constant_dynamic-slice_fusion), channel_id=1, source_target_pairs={{0,1},{1,0},{2,3},{3,2},{4,5},{5,4},{6,7},{7,6},{8,9},{9,8},{10,11... | collective-permute-start | bytes 786440 | tf_op jit(solution)/shard_map/ppermute | solution.py:95
  2.0 0.0 copy-done.1
  2.0 0.1 reshape.73
  2.2 0.0 copy-done.2
  2.3 0.9 %collective-permute-done = bf16[2,2,32,1024]{3,2,1,0:T(8,128)(2,1)S(1)} collective-permute-done((bf16[2,2,32,1024]{3,2,1,0:T(8,128)(2,1)S(1)}, bf16[2,2,32,1024]{3,2,1,0:T(8,128)(2,1)S(1)}, u32[]{:S(2)}, u32[]{:S(2)}) %collective-permute-start) | collective-permute-done | bytes 262176 | tf_op jit(solution)/shard_map/ppermute | solution.py:95
  3.2 0.2 pad_maximum_fusion.1
  3.4 2.1 %fusion.6 = f32[2,2,64,1024]{3,2,1,0:T(8,128)S(1)} fusion(bf16[2,2,32,1024]{3,2,1,0:T(8,128)(2,1)S(1)} %get-tuple-element.17, bf16[2,2,32,1024]{3,2,1,0:T(8,128)(2,1)S(1)} %get-tuple-element.16, f32[1024]{0:T(1024)S(1)} %bitcast.56, bf16[2,2,79,1024]{3,2,1,0:T(8,128)(2,1)S(1)} %pad_maximum_fusion.1, f32[1024]{0:T(1024)S(1)} %bitcast.57, ...), kind=kLoop, calls=%fused_computation.22 | loop fusion | flops 13631488 | bytes 9502720 | tf_op jit(solution)/shard_map/convert_element_type | solution.py:43
  5.5 0.1 fusion.8
  5.6 0.0 copy-start.3
  5.6 0.0 copy-start.4
  5.6 0.1 fusion.10
  5.7 0.6 %copy-done.3 = f32[4,256]{1,0:T(4,128)S(1)} copy-done((f32[4,256]{1,0:T(4,128)S(1)}, f32[4,256]{1,0:T(4,128)}, u32[]{:S(2)}) %copy-start.3) | copy-done | bytes 4120
  6.3 0.0 copy-done.4
  6.3 0.1 fusion.18
  6.5 0.1 maximum_bitcast_fusion
  6.6 0.0 copy-start
  6.6 0.1 pad_maximum_fusion
  6.7 0.8 %copy-done = bf16[512,256]{1,0:T(8,128)(2,1)S(1)} copy-done((bf16[512,256]{1,0:T(8,128)(2,1)S(1)}, bf16[512,256]{1,0:T(8,128)(2,1)}, u32[]{:S(2)}) %copy-start) | copy-done | bytes 262168
  7.6 0.0 copy-start.5
  7.6 0.0 copy-start.6
  7.6 1.3 %convolution_convert_fusion = bf16[1024,256]{0,1:T(8,128)(2,1)} fusion(bf16[1024,512]{1,0:T(8,128)(2,1)S(1)} %bitcast.39, bf16[512,256]{1,0:T(8,128)(2,1)S(1)} %copy-done), kind=kOutput, calls=%fused_computation.2 | convolution fusion | flops 268697600 | bytes 1835008 | tf_op jit(solution)/shard_map/dot_general | solution.py:59
  8.8 7.3 %all-to-all-start = ((bf16[16,16,1024]{2,1,0:T(8,128)(2,1)}), bf16[16,16,1024]{2,1,0:T(8,128)(2,1)S(1)}, u32[]{:S(2)}, u32[]{:S(2)}) async-start(bf16[16,16,1024]{2,1,0:T(8,128)(2,1)} %bitcast.21), calls=%async_computation | async-start | bytes 1048576 | tf_op jit(solution)/shard_map/all_to_all | solution.py:104
  16.1 0.0 copy-done.5
  16.2 0.0 copy-done.6
  16.2 0.6 %scatter_custom_fusion = s32[16]{0:T(128)S(1)} fusion(s32[16]{0:T(128)S(1)} %compare_select_fusion.1, s32[16]{0:T(128)S(1)} %iota.3, s32[]{:T(128)} %constant.12.clone.1), kind=kCustom, calls=%fused_computation.47 | custom fusion | bytes 68 | tf_op jit(solution)/shard_map/scatter | solution.py:108
  16.9 13.7 %all-to-all-done = bf16[16,16,1024]{2,1,0:T(8,128)(2,1)S(1)} async-done(((bf16[16,16,1024]{2,1,0:T(8,128)(2,1)}), bf16[16,16,1024]{2,1,0:T(8,128)(2,1)S(1)}, u32[]{:S(2)}, u32[]{:S(2)}) %all-to-all-start) | async-done | bytes 524320 | tf_op jit(solution)/shard_map/all_to_all | solution.py:104
  30.6 0.6 %gather_fusion = bf16[16,16,1024]{2,1,0:T(8,128)(2,1)S(1)} fusion(bf16[16,16,1024]{2,1,0:T(8,128)(2,1)S(1)} %all-to-all-done, s32[1024]{0:T(1024)S(1)} %pad_clamp_fusion), kind=kCustom, calls=%fused_computation | custom fusion | bytes 1048640 | tf_op jit(solution)/shard_map/jit(_take)/gather | solution.py:111
  31.2 0.4 %gather.7 = bf16[16,16,4,2,128]{4,3,2,1,0:T(2,128)(2,1)S(1)} reshape(bf16[16,16,1024]{2,1,0:T(8,128)(2,1)S(1)} %gather_fusion) | data formatting | bytes 1048576 | tf_op jit(solution)/shard_map/jit(_take)/gather | solution.py:111
  31.6 0.6 %fusion.5 = bf16[16,16,4,2,128]{4,3,0,2,1:T(2,128)(2,1)S(1)} fusion(bf16[16,16,4,2,128]{4,3,2,1,0:T(2,128)(2,1)S(1)} %gather.7, pred[16]{0:T(512)(128)(4,1)S(1)} %compare_and_fusion, bf16[16]{0:T(256)(128)(2,1)S(1)} %convert_element_type.95), kind=kLoop, calls=%fused_computation.21 | loop fusion | flops 524288 | bytes 1048624 | tf_op jit(solution)/shard_map/mul | solution.py:111
  32.2 0.2 slice_negate_fusion
  32.4 0.4 %fusion.20 = f32[64,32,32]{2,1,0:T(8,128)S(1)} fusion(bf16[64,32,128]{2,1,0:T(8,128)(2,1)S(1)} %bitcast.37), kind=kOutput, calls=%fused_computation.52 | convolution fusion | flops 16777216 | bytes 786432 | tf_op jit(solution)/shard_map/cak,cbk->cab/dot_general | solution.py:75
  32.8 0.5 %fusion.1 = f32[64,32,32]{2,1,0:T(8,128)S(1)} fusion(bf16[64,32,128]{2,1,0:T(8,128)(2,1)S(1)} %bitcast.38, bf16[64,32,64]{2,1,0:T(8,128)(2,1)S(1)} %get-tuple-element.19, bf16[64,32,64]{2,1,0:T(8,128)(2,1)S(1)} %get-tuple-element.18), kind=kOutput, calls=%fused_computation.14 | convolution fusion | flops 17825792 | bytes 1310720 | tf_op jit(solution)/shard_map/cak,cbk->cab/dot_general | solution.py:76
  33.3 0.6 %copy.17 = f32[64,32,32]{0,2,1:T(8,128)S(1)} copy(f32[64,32,32]{2,1,0:T(8,128)S(1)} %fusion.1) | data formatting | bytes 524288 | tf_op jit(solution)/shard_map/cak,cbk->cab/dot_general | solution.py:76
  33.9 0.6 %copy.16 = f32[64,32,32]{0,2,1:T(8,128)S(1)} copy(f32[64,32,32]{2,1,0:T(8,128)S(1)} %fusion.20) | data formatting | bytes 524288 | tf_op jit(solution)/shard_map/cak,cbk->cab/dot_general | solution.py:75
  34.5 0.9 %fusion = bf16[2,64,32,32]{1,3,2,0:T(8,128)(2,1)} fusion(f32[1,64,32,32]{1,3,2,0:T(8,128)S(1)} %bitcast.40, f32[1,64,32,32]{1,3,2,0:T(8,128)S(1)} %bitcast.41), kind=kLoop, calls=%fused_computation.5 | loop fusion | flops 393216 | bytes 786432 | tf_op jit(solution)/shard_map/convert_element_type | solution.py:77
  (11 shorter events, 0.2 us)
Async XLA Ops:
  0.0 2.0 %copy-start.1 = (bf16[2,4,15360]{2,1,0:T(4,128)(2,1)S(1)}, bf16[2,4,15360]{2,1,0:T(4,128)(2,1)}, u32[]{:S(2)}) copy-start(bf16[2,4,15360]{2,1,0:T(4,128)(2,1)} %param.9) | copy-start | bytes 737284
  0.0 2.2 %copy-start.2 = (f32[16,1024]{1,0:T(8,128)S(1)}, f32[16,1024]{1,0:T(8,128)}, u32[]{:S(2)}) copy-start(f32[16,1024]{1,0:T(8,128)} %param.10) | copy-start | bytes 196612
  1.5 1.7 %collective-permute-start = (bf16[2,2,32,1024]{3,2,1,0:T(8,128)(2,1)S(1)}, bf16[2,2,32,1024]{3,2,1,0:T(8,128)(2,1)S(1)}, u32[]{:S(2)}, u32[]{:S(2)}) collective-permute-start(bf16[2,2,32,1024]{3,2,1,0:T(8,128)(2,1)S(1)} %constant_dynamic-slice_fusion), channel_id=1, source_target_pairs={{0,1},{1,0},{2,3},{3,2},{4,5},{5,4},{6,7},{7,6},{8,9},{9,8},{10,11... | collective-permute-start | bytes 786440 | tf_op jit(solution)/shard_map/ppermute | solution.py:95
  5.6 0.7 %copy-start.3 = (f32[4,256]{1,0:T(4,128)S(1)}, f32[4,256]{1,0:T(4,128)}, u32[]{:S(2)}) copy-start(f32[4,256]{1,0:T(4,128)} %constant.37.clone) | copy-start | bytes 12292
  5.6 0.7 %copy-start.4 = (f32[4,256]{1,0:T(4,128)S(1)}, f32[4,256]{1,0:T(4,128)}, u32[]{:S(2)}) copy-start(f32[4,256]{1,0:T(4,128)} %constant.38.clone) | copy-start | bytes 12292
  6.6 1.0 %copy-start = (bf16[512,256]{1,0:T(8,128)(2,1)S(1)}, bf16[512,256]{1,0:T(8,128)(2,1)}, u32[]{:S(2)}) copy-start(bf16[512,256]{1,0:T(8,128)(2,1)} %constant.42) | copy-start | bytes 786436
  7.6 8.6 %copy-start.5 = (s32[16]{0:T(128)S(1)}, s32[16]{0:T(128)}, u32[]{:S(2)}) copy-start(s32[16]{0:T(128)} %param.12) | copy-start | bytes 196
  7.6 8.6 %copy-start.6 = (s32[16]{0:T(128)S(1)}, s32[16]{0:T(128)}, u32[]{:S(2)}) copy-start(s32[16]{0:T(128)} %param.11) | copy-start | bytes 196
  8.8 21.8 %all-to-all-start = ((bf16[16,16,1024]{2,1,0:T(8,128)(2,1)}), bf16[16,16,1024]{2,1,0:T(8,128)(2,1)S(1)}, u32[]{:S(2)}, u32[]{:S(2)}) async-start(bf16[16,16,1024]{2,1,0:T(8,128)(2,1)} %bitcast.21), calls=%async_computation | async-start | bytes 1048576 | tf_op jit(solution)/shard_map/all_to_all | solution.py:104

commit v7 on v6

--- a/solution.py
+++ b/solution.py
@@ -5,6 +5,7 @@
 import jax
 import jax.numpy as jnp
 from jax import lax
+from jax.experimental.layout import Layout, with_layout_constraint
 from jax.sharding import PartitionSpec as P
 
 POLS = 2
@@ -113,7 +114,8 @@
     ordered = jnp.transpose(gathered, (1, 2, 0, 3, 4)).reshape(
         kl_count * RADIX, station_count * POLS, 2 * spec_total
     )
-    return correlate_full(ordered, 1.0 / spec_total)
+    vis = correlate_full(ordered, 1.0 / spec_total)
+    return with_layout_constraint(vis, Layout((0, 1, 2, 3)))
 
 
 def solution(mesh):

time: 35.7 us -> 35.7 us (level)
  local copies, waits for them, and re-layouts: 5.93 us -> 6.61 us
  other arithmetic: 4.64 us -> 3.98 us
    another operation x0 -> x1, local copies, waits for them, and re-layouts: none -> 1.87 us  [local(): return with_layout_constraint(vis, Layout((0, 1, 2, 3)))]
    dot_general x2 -> x0, local copies, waits for them, and re-layouts: 1.19 us -> none  [the longest x1 0.6 us: correlate_full(): jnp.einsum('cak,cbk->cab', ordered, rotated, preferred_element_type=jnp.f...]
    convert_element_type x1, other arithmetic: 0.93 us -> 0.27 us  [correlate_full(): (jnp.stack([real_vis, imag_vis], axis=0) * inverse_count).astype(jnp.bflo...]
where the time goes in v7:
time: 35.7 us; the launch traced here: 35.4 us
  waiting for transfers between devices  14.6 us (41%)
  starting transfers between devices  7.79 us (22%)
  local copies, waits for them, and re-layouts  6.61 us (19%)
  other arithmetic  3.98 us (11%)
  matrix products  2.14 us (6%)
    all_to_all x1, waiting for transfers between devices, local(): lax.all_to_all(spectra, ('blk', 'tch'), split_axis=0, concat_axis=0, tile...  13.7 us
    all_to_all x1, starting transfers between devices, local(): lax.all_to_all(spectra, ('blk', 'tch'), split_axis=0, concat_axis=0, tile...  7.28 us
    convert_element_type x1, other arithmetic, channelize(): x = filtered.astype(jnp.float32)  2.12 us
    another operation x1, local copies, waits for them, and re-layouts, local(): return with_layout_constraint(vis, Layout((0, 1, 2, 3)))  1.87 us
    unnamed x14, local copies, waits for them, and re-layouts  1.46 us
    reshape x1, local copies, waits for them, and re-layouts, local(): blocks = samples.reshape(2, row_count, -1, fft_len)  1.46 us
    dot_general x1, matrix products, channelize(): lax.dot_general(jnp.asarray(inner_matrix).astype(jnp.bfloat16), rows.asty...  1.28 us
    gather x2, local copies, waits for them, and re-layouts, local(): gathered = jnp.take(turned, slot_index, axis=0) * keep_mask[:, None, None]  0.95 us
  transfers between devices with their start and end apart: 2, of which 2 were waited for; matrix products, arithmetic and copies ran while one was open for 2% of the time, Pallas kernels for 0%

profile of v7, /device:TPU:0, one launch (start us, length us, event | category | flops | bytes accessed | tf_op | source)
XLA Modules:
  0.0 35.4 jit_solution(17760244630580928524)
XLA Ops:
  0.0 0.0 copy-start.1
  0.0 0.0 copy-start.2
  0.0 1.5 %reshape.74 = bf16[2,4,32,1024]{3,2,1,0:T(8,128)(2,1)S(1)} reshape(bf16[2,4,32768]{2,1,0:T(4,128)(2,1)} %param.8) | data formatting | bytes 1048576 | tf_op jit(solution)/shard_map/reshape | solution.py:92
  1.5 0.5 %collective-permute-start = (bf16[2,2,32,1024]{3,2,1,0:T(8,128)(2,1)S(1)}, bf16[2,2,32,1024]{3,2,1,0:T(8,128)(2,1)S(1)}, u32[]{:S(2)}, u32[]{:S(2)}) collective-permute-start(bf16[2,2,32,1024]{3,2,1,0:T(8,128)(2,1)S(1)} %constant_dynamic-slice_fusion), channel_id=1, source_target_pairs={{0,1},{1,0},{2,3},{3,2},{4,5},{5,4},{6,7},{7,6},{8,9},{9,8},{10,11... | collective-permute-start | bytes 786440 | tf_op jit(solution)/shard_map/ppermute | solution.py:96
  2.0 0.0 copy-done.1
  2.0 0.1 reshape.73
  2.2 0.0 copy-done.2
  2.3 0.9 %collective-permute-done = bf16[2,2,32,1024]{3,2,1,0:T(8,128)(2,1)S(1)} collective-permute-done((bf16[2,2,32,1024]{3,2,1,0:T(8,128)(2,1)S(1)}, bf16[2,2,32,1024]{3,2,1,0:T(8,128)(2,1)S(1)}, u32[]{:S(2)}, u32[]{:S(2)}) %collective-permute-start) | collective-permute-done | bytes 262176 | tf_op jit(solution)/shard_map/ppermute | solution.py:96
  3.2 0.2 pad_maximum_fusion.1
  3.4 2.1 %fusion.5 = f32[2,2,64,1024]{3,2,1,0:T(8,128)S(1)} fusion(bf16[2,2,32,1024]{3,2,1,0:T(8,128)(2,1)S(1)} %get-tuple-element.17, bf16[2,2,32,1024]{3,2,1,0:T(8,128)(2,1)S(1)} %get-tuple-element.16, f32[1024]{0:T(1024)S(1)} %bitcast.56, bf16[2,2,79,1024]{3,2,1,0:T(8,128)(2,1)S(1)} %pad_maximum_fusion.1, f32[1024]{0:T(1024)S(1)} %bitcast.57, ...), kind=kLoop, calls=%fused_computation.23 | loop fusion | flops 13631488 | bytes 9502720 | tf_op jit(solution)/shard_map/convert_element_type | solution.py:44
  5.5 0.1 fusion.7
  5.6 0.0 copy-start.3
  5.6 0.0 copy-start.4
  5.6 0.1 fusion.9
  5.7 0.6 %copy-done.3 = f32[4,256]{1,0:T(4,128)S(1)} copy-done((f32[4,256]{1,0:T(4,128)S(1)}, f32[4,256]{1,0:T(4,128)}, u32[]{:S(2)}) %copy-start.3) | copy-done | bytes 4120
  6.3 0.0 copy-done.4
  6.3 0.1 fusion.17
  6.5 0.1 maximum_bitcast_fusion
  6.6 0.0 copy-start
  6.6 0.1 pad_maximum_fusion
  6.7 0.8 %copy-done = bf16[512,256]{1,0:T(8,128)(2,1)S(1)} copy-done((bf16[512,256]{1,0:T(8,128)(2,1)S(1)}, bf16[512,256]{1,0:T(8,128)(2,1)}, u32[]{:S(2)}) %copy-start) | copy-done | bytes 262168
  7.6 0.0 copy-start.5
  7.6 0.0 copy-start.6
  7.6 1.3 %convolution_convert_fusion = bf16[1024,256]{0,1:T(8,128)(2,1)} fusion(bf16[1024,512]{1,0:T(8,128)(2,1)S(1)} %bitcast.41, bf16[512,256]{1,0:T(8,128)(2,1)S(1)} %copy-done), kind=kOutput, calls=%fused_computation.6 | convolution fusion | flops 268697600 | bytes 1835008 | tf_op jit(solution)/shard_map/dot_general | solution.py:60
  8.8 7.3 %all-to-all-start = ((bf16[16,16,1024]{2,1,0:T(8,128)(2,1)}), bf16[16,16,1024]{2,1,0:T(8,128)(2,1)S(1)}, u32[]{:S(2)}, u32[]{:S(2)}) async-start(bf16[16,16,1024]{2,1,0:T(8,128)(2,1)} %bitcast.21), calls=%async_computation | async-start | bytes 1048576 | tf_op jit(solution)/shard_map/all_to_all | solution.py:105
  16.1 0.0 copy-done.5
  16.2 0.0 copy-done.6
  16.2 0.6 %scatter_custom_fusion = s32[16]{0:T(128)S(1)} fusion(s32[16]{0:T(128)S(1)} %compare_select_fusion.1, s32[16]{0:T(128)S(1)} %iota.3, s32[]{:T(128)} %constant.12.clone.1), kind=kCustom, calls=%fused_computation.48 | custom fusion | bytes 68 | tf_op jit(solution)/shard_map/scatter | solution.py:109
  16.9 13.7 %all-to-all-done = bf16[16,16,1024]{2,1,0:T(8,128)(2,1)S(1)} async-done(((bf16[16,16,1024]{2,1,0:T(8,128)(2,1)}), bf16[16,16,1024]{2,1,0:T(8,128)(2,1)S(1)}, u32[]{:S(2)}, u32[]{:S(2)}) %all-to-all-start) | async-done | bytes 524320 | tf_op jit(solution)/shard_map/all_to_all | solution.py:105
  30.6 0.6 %gather_fusion = bf16[16,16,1024]{2,1,0:T(8,128)(2,1)S(1)} fusion(bf16[16,16,1024]{2,1,0:T(8,128)(2,1)S(1)} %all-to-all-done, s32[1024]{0:T(1024)S(1)} %pad_clamp_fusion), kind=kCustom, calls=%fused_computation | custom fusion | bytes 1048640 | tf_op jit(solution)/shard_map/jit(_take)/gather | solution.py:112
  31.2 0.4 %gather.7 = bf16[16,16,4,2,128]{4,3,2,1,0:T(2,128)(2,1)S(1)} reshape(bf16[16,16,1024]{2,1,0:T(8,128)(2,1)S(1)} %gather_fusion) | data formatting | bytes 1048576 | tf_op jit(solution)/shard_map/jit(_take)/gather | solution.py:112
  31.6 0.6 %fusion.4 = bf16[16,16,4,2,128]{4,3,0,2,1:T(2,128)(2,1)S(1)} fusion(bf16[16,16,4,2,128]{4,3,2,1,0:T(2,128)(2,1)S(1)} %gather.7, pred[16]{0:T(512)(128)(4,1)S(1)} %compare_and_fusion, bf16[16]{0:T(256)(128)(2,1)S(1)} %convert_element_type.95), kind=kLoop, calls=%fused_computation.22 | loop fusion | flops 524288 | bytes 1048624 | tf_op jit(solution)/shard_map/mul | solution.py:112
  32.2 0.2 slice_negate_fusion
  32.4 0.4 %convolution_bitcast_fusion.1 = f32[1,64,32,32]{3,2,1,0:T(8,128)S(1)} fusion(bf16[64,32,128]{2,1,0:T(8,128)(2,1)S(1)} %bitcast.39), kind=kOutput, calls=%fused_computation.5 | convolution fusion | flops 16777216 | bytes 786432 | tf_op jit(solution)/shard_map/cak,cbk->cab/dot_general | solution.py:76
  32.8 0.5 %convolution_bitcast_fusion = f32[1,64,32,32]{3,2,1,0:T(8,128)S(1)} fusion(bf16[64,32,128]{2,1,0:T(8,128)(2,1)S(1)} %bitcast.40, bf16[64,32,64]{2,1,0:T(8,128)(2,1)S(1)} %get-tuple-element.19, bf16[64,32,64]{2,1,0:T(8,128)(2,1)S(1)} %get-tuple-element.18), kind=kOutput, calls=%fused_computation.4 | convolution fusion | flops 17825792 | bytes 1310720 | tf_op jit(solution)/shard_map/cak,cbk->cab/dot_general | solution.py:77
  33.3 0.3 fusion
  33.5 1.9 %copy.13 = bf16[2,64,32,32]{1,3,2,0:T(8,128)(2,1)} copy(bf16[2,64,32,32]{3,2,1,0:T(8,128)(2,1)S(1)} %fusion) | data formatting | bytes 524288 | tf_op jit(solution)/shard_map/layout_constraint | solution.py:118
  (11 shorter events, 0.2 us)
Async XLA Ops:
  0.0 2.0 %copy-start.1 = (bf16[2,4,15360]{2,1,0:T(4,128)(2,1)S(1)}, bf16[2,4,15360]{2,1,0:T(4,128)(2,1)}, u32[]{:S(2)}) copy-start(bf16[2,4,15360]{2,1,0:T(4,128)(2,1)} %param.9) | copy-start | bytes 737284
  0.0 2.2 %copy-start.2 = (f32[16,1024]{1,0:T(8,128)S(1)}, f32[16,1024]{1,0:T(8,128)}, u32[]{:S(2)}) copy-start(f32[16,1024]{1,0:T(8,128)} %param.10) | copy-start | bytes 196612
  1.5 1.7 %collective-permute-start = (bf16[2,2,32,1024]{3,2,1,0:T(8,128)(2,1)S(1)}, bf16[2,2,32,1024]{3,2,1,0:T(8,128)(2,1)S(1)}, u32[]{:S(2)}, u32[]{:S(2)}) collective-permute-start(bf16[2,2,32,1024]{3,2,1,0:T(8,128)(2,1)S(1)} %constant_dynamic-slice_fusion), channel_id=1, source_target_pairs={{0,1},{1,0},{2,3},{3,2},{4,5},{5,4},{6,7},{7,6},{8,9},{9,8},{10,11... | collective-permute-start | bytes 786440 | tf_op jit(solution)/shard_map/ppermute | solution.py:96
  5.6 0.7 %copy-start.3 = (f32[4,256]{1,0:T(4,128)S(1)}, f32[4,256]{1,0:T(4,128)}, u32[]{:S(2)}) copy-start(f32[4,256]{1,0:T(4,128)} %constant.37.clone) | copy-start | bytes 12292
  5.6 0.7 %copy-start.4 = (f32[4,256]{1,0:T(4,128)S(1)}, f32[4,256]{1,0:T(4,128)}, u32[]{:S(2)}) copy-start(f32[4,256]{1,0:T(4,128)} %constant.38.clone) | copy-start | bytes 12292
  6.6 1.0 %copy-start = (bf16[512,256]{1,0:T(8,128)(2,1)S(1)}, bf16[512,256]{1,0:T(8,128)(2,1)}, u32[]{:S(2)}) copy-start(bf16[512,256]{1,0:T(8,128)(2,1)} %constant.42) | copy-start | bytes 786436
  7.6 8.6 %copy-start.5 = (s32[16]{0:T(128)S(1)}, s32[16]{0:T(128)}, u32[]{:S(2)}) copy-start(s32[16]{0:T(128)} %param.12) | copy-start | bytes 196
  7.6 8.6 %copy-start.6 = (s32[16]{0:T(128)S(1)}, s32[16]{0:T(128)}, u32[]{:S(2)}) copy-start(s32[16]{0:T(128)} %param.11) | copy-start | bytes 196
  8.8 21.8 %all-to-all-start = ((bf16[16,16,1024]{2,1,0:T(8,128)(2,1)}), bf16[16,16,1024]{2,1,0:T(8,128)(2,1)S(1)}, u32[]{:S(2)}, u32[]{:S(2)}) async-start(bf16[16,16,1024]{2,1,0:T(8,128)(2,1)} %bitcast.21), calls=%async_computation | async-start | bytes 1048576 | tf_op jit(solution)/shard_map/all_to_all | solution.py:105

commit v8 on v7

--- a/solution.py
+++ b/solution.py
@@ -89,11 +89,10 @@
     kl_count = inner // dest_count
     keep = row_count // half_count
     t = lax.axis_index("tch")
-    blocks = samples.reshape(2, row_count, -1, fft_len)
+    other = lax.dynamic_slice_in_dim(samples, (1 - t) * keep, keep, axis=1).reshape(2, keep, -1, fft_len)
+    received = lax.ppermute(other, "tch", [(0, 1), (1, 0)])
+    own = lax.dynamic_slice_in_dim(samples, t * keep, keep, axis=1).reshape(2, keep, -1, fft_len)
     before = history.reshape(2, row_count, -1, fft_len)
-    own = lax.dynamic_slice_in_dim(blocks, t * keep, keep, axis=1)
-    other = lax.dynamic_slice_in_dim(blocks, (1 - t) * keep, keep, axis=1)
-    received = lax.ppermute(other, "tch", [(0, 1), (1, 0)])
     is_first = t == 0
     first = jnp.where(is_first, own, received)
     second = jnp.where(is_first, received, own)

time: 35.7 us -> 36.2 us (1.014)
  local copies, waits for them, and re-layouts: 6.61 us -> 7.31 us
    dynamic_slice x1, local copies, waits for them, and re-layouts: 0.03 us -> 1.81 us  [local(): lax.dynamic_slice_in_dim(samples, t * keep, keep, axis=1)]
    reshape x1 -> x2, local copies, waits for them, and re-layouts: 1.46 us -> 0.37 us  [the longest x1 0.19 us: local(): lax.dynamic_slice_in_dim(samples, (1 - t) * keep, keep, axis=1)]
  transfers between devices with their start and end apart: 2 -> 2, of which waited for: 2 -> 2; matrix products, arithmetic and copies ran while one was open for 2% -> 3% of each run, Pallas kernels for 0% -> 0%
where the time goes in v8:
time: 36.2 us; the launch traced here: 35.9 us
  waiting for transfers between devices  14.5 us (40%)
  starting transfers between devices  7.8 us (22%)
  local copies, waits for them, and re-layouts  7.31 us (20%)
  other arithmetic  3.98 us (11%)
  matrix products  2.14 us (6%)
    all_to_all x1, waiting for transfers between devices, local(): lax.all_to_all(spectra, ('blk', 'tch'), split_axis=0, concat_axis=0, tile...  13.7 us
    all_to_all x1, starting transfers between devices, local(): lax.all_to_all(spectra, ('blk', 'tch'), split_axis=0, concat_axis=0, tile...  7.28 us
    convert_element_type x1, other arithmetic, channelize(): x = filtered.astype(jnp.float32)  2.12 us
    another operation x1, local copies, waits for them, and re-layouts, local(): return with_layout_constraint(vis, Layout((0, 1, 2, 3)))  1.87 us
    dynamic_slice x1, local copies, waits for them, and re-layouts, local(): lax.dynamic_slice_in_dim(samples, t * keep, keep, axis=1)  1.81 us
    unnamed x14, local copies, waits for them, and re-layouts  1.47 us
    dot_general x1, matrix products, channelize(): lax.dot_general(jnp.asarray(inner_matrix).astype(jnp.bfloat16), rows.asty...  1.28 us
    gather x2, local copies, waits for them, and re-layouts, local(): gathered = jnp.take(turned, slot_index, axis=0) * keep_mask[:, None, None]  0.95 us
  transfers between devices with their start and end apart: 2, of which 2 were waited for; matrix products, arithmetic and copies ran while one was open for 3% of the time, Pallas kernels for 0%

profile of v8, /device:TPU:0, one launch (start us, length us, event | category | flops | bytes accessed | tf_op | source)
XLA Modules:
  0.0 35.9 jit_solution(17687027376592250979)
XLA Ops:
  0.0 0.0 copy-start.1
  0.0 1.8 %constant_dynamic-slice_fusion.1 = (bf16[2,2,32768]{2,1,0:T(2,128)(2,1)S(1)}, bf16[2,2,32768]{2,1,0:T(2,128)(2,1)S(1)}) fusion(bf16[2,4,32768]{2,1,0:T(4,128)(2,1)} %param.8, s32[]{:T(128)S(6)} %select_n.34, s32[]{:T(128)S(6)} %select_n.36), kind=kLoop, calls=%fused_computation.47 | loop fusion | bytes 1048584 | tf_op jit(solution)/shard_map/dynamic_slice | solution.py:94
  1.8 0.0 copy-start.2
  1.8 0.2 reshape.78
  2.0 0.5 %collective-permute-start = (bf16[2,2,32,1024]{3,2,1,0:T(8,128)(2,1)S(1)}, bf16[2,2,32,1024]{3,2,1,0:T(8,128)(2,1)S(1)}, u32[]{:S(2)}, u32[]{:S(2)}) collective-permute-start(bf16[2,2,32,1024]{3,2,1,0:T(8,128)(2,1)S(1)} %reshape.78), channel_id=1, source_target_pairs={{0,1},{1,0},{2,3},{3,2},{4,5},{5,4},{6,7},{7,6},{8,9},{9,8},{10,11... | collective-permute-start | bytes 786440 | tf_op jit(solution)/shard_map/ppermute | solution.py:93
  2.5 0.0 copy-done.1
  2.5 0.1 reshape.76
  2.7 0.2 reshape.77
  2.9 0.0 copy-done.2
  3.0 0.7 %collective-permute-done = bf16[2,2,32,1024]{3,2,1,0:T(8,128)(2,1)S(1)} collective-permute-done((bf16[2,2,32,1024]{3,2,1,0:T(8,128)(2,1)S(1)}, bf16[2,2,32,1024]{3,2,1,0:T(8,128)(2,1)S(1)}, u32[]{:S(2)}, u32[]{:S(2)}) %collective-permute-start) | collective-permute-done | bytes 262176 | tf_op jit(solution)/shard_map/ppermute | solution.py:93
  3.7 0.2 pad_maximum_fusion.1
  3.9 2.1 %fusion.5 = f32[2,2,64,1024]{3,2,1,0:T(8,128)S(1)} fusion(bf16[2,2,32,1024]{3,2,1,0:T(8,128)(2,1)S(1)} %get-tuple-element.19, bf16[2,2,32,1024]{3,2,1,0:T(8,128)(2,1)S(1)} %get-tuple-element.18, f32[1024]{0:T(1024)S(1)} %bitcast.56, bf16[2,2,79,1024]{3,2,1,0:T(8,128)(2,1)S(1)} %pad_maximum_fusion.1, f32[1024]{0:T(1024)S(1)} %bitcast.57, ...), kind=kLoop, calls=%fused_computation.23 | loop fusion | flops 13631488 | bytes 9502720 | tf_op jit(solution)/shard_map/convert_element_type | solution.py:44
  6.0 0.1 fusion.7
  6.1 0.0 copy-start.3
  6.1 0.0 copy-start.4
  6.1 0.1 fusion.9
  6.2 0.6 %copy-done.3 = f32[4,256]{1,0:T(4,128)S(1)} copy-done((f32[4,256]{1,0:T(4,128)S(1)}, f32[4,256]{1,0:T(4,128)}, u32[]{:S(2)}) %copy-start.3) | copy-done | bytes 4120
  6.8 0.0 copy-done.4
  6.8 0.1 fusion.17
  7.0 0.1 maximum_bitcast_fusion
  7.1 0.0 copy-start
  7.1 0.1 pad_maximum_fusion
  7.2 0.8 %copy-done = bf16[512,256]{1,0:T(8,128)(2,1)S(1)} copy-done((bf16[512,256]{1,0:T(8,128)(2,1)S(1)}, bf16[512,256]{1,0:T(8,128)(2,1)}, u32[]{:S(2)}) %copy-start) | copy-done | bytes 262168
  8.1 0.0 copy-start.5
  8.1 0.0 copy-start.6
  8.1 1.3 %convolution_convert_fusion = bf16[1024,256]{0,1:T(8,128)(2,1)} fusion(bf16[1024,512]{1,0:T(8,128)(2,1)S(1)} %bitcast.41, bf16[512,256]{1,0:T(8,128)(2,1)S(1)} %copy-done), kind=kOutput, calls=%fused_computation.6 | convolution fusion | flops 268697600 | bytes 1835008 | tf_op jit(solution)/shard_map/dot_general | solution.py:60
  9.4 7.3 %all-to-all-start = ((bf16[16,16,1024]{2,1,0:T(8,128)(2,1)}), bf16[16,16,1024]{2,1,0:T(8,128)(2,1)S(1)}, u32[]{:S(2)}, u32[]{:S(2)}) async-start(bf16[16,16,1024]{2,1,0:T(8,128)(2,1)} %bitcast.21), calls=%async_computation | async-start | bytes 1048576 | tf_op jit(solution)/shard_map/all_to_all | solution.py:104
  16.6 0.0 copy-done.5
  16.7 0.0 copy-done.6
  16.7 0.6 %scatter_custom_fusion = s32[16]{0:T(128)S(1)} fusion(s32[16]{0:T(128)S(1)} %compare_select_fusion.1, s32[16]{0:T(128)S(1)} %iota.3, s32[]{:T(128)} %constant.12.clone.1), kind=kCustom, calls=%fused_computation.49 | custom fusion | bytes 68 | tf_op jit(solution)/shard_map/scatter | solution.py:108
  17.4 13.7 %all-to-all-done = bf16[16,16,1024]{2,1,0:T(8,128)(2,1)S(1)} async-done(((bf16[16,16,1024]{2,1,0:T(8,128)(2,1)}), bf16[16,16,1024]{2,1,0:T(8,128)(2,1)S(1)}, u32[]{:S(2)}, u32[]{:S(2)}) %all-to-all-start) | async-done | bytes 524320 | tf_op jit(solution)/shard_map/all_to_all | solution.py:104
  31.1 0.6 %gather_fusion = bf16[16,16,1024]{2,1,0:T(8,128)(2,1)S(1)} fusion(bf16[16,16,1024]{2,1,0:T(8,128)(2,1)S(1)} %all-to-all-done, s32[1024]{0:T(1024)S(1)} %pad_clamp_fusion), kind=kCustom, calls=%fused_computation | custom fusion | bytes 1048640 | tf_op jit(solution)/shard_map/jit(_take)/gather | solution.py:111
  31.7 0.4 %gather.7 = bf16[16,16,4,2,128]{4,3,2,1,0:T(2,128)(2,1)S(1)} reshape(bf16[16,16,1024]{2,1,0:T(8,128)(2,1)S(1)} %gather_fusion) | data formatting | bytes 1048576 | tf_op jit(solution)/shard_map/jit(_take)/gather | solution.py:111
  32.1 0.6 %fusion.4 = bf16[16,16,4,2,128]{4,3,0,2,1:T(2,128)(2,1)S(1)} fusion(bf16[16,16,4,2,128]{4,3,2,1,0:T(2,128)(2,1)S(1)} %gather.7, pred[16]{0:T(512)(128)(4,1)S(1)} %compare_and_fusion, bf16[16]{0:T(256)(128)(2,1)S(1)} %convert_element_type.95), kind=kLoop, calls=%fused_computation.22 | loop fusion | flops 524288 | bytes 1048624 | tf_op jit(solution)/shard_map/mul | solution.py:111
  32.7 0.2 slice_negate_fusion
  32.9 0.4 %convolution_bitcast_fusion.1 = f32[1,64,32,32]{3,2,1,0:T(8,128)S(1)} fusion(bf16[64,32,128]{2,1,0:T(8,128)(2,1)S(1)} %bitcast.39), kind=kOutput, calls=%fused_computation.5 | convolution fusion | flops 16777216 | bytes 786432 | tf_op jit(solution)/shard_map/cak,cbk->cab/dot_general | solution.py:76
  33.3 0.5 %convolution_bitcast_fusion = f32[1,64,32,32]{3,2,1,0:T(8,128)S(1)} fusion(bf16[64,32,128]{2,1,0:T(8,128)(2,1)S(1)} %bitcast.40, bf16[64,32,64]{2,1,0:T(8,128)(2,1)S(1)} %get-tuple-element.17, bf16[64,32,64]{2,1,0:T(8,128)(2,1)S(1)} %get-tuple-element.16), kind=kOutput, calls=%fused_computation.4 | convolution fusion | flops 17825792 | bytes 1310720 | tf_op jit(solution)/shard_map/cak,cbk->cab/dot_general | solution.py:77
  33.8 0.3 fusion
  34.1 1.9 %copy.13 = bf16[2,64,32,32]{1,3,2,0:T(8,128)(2,1)} copy(bf16[2,64,32,32]{3,2,1,0:T(8,128)(2,1)S(1)} %fusion) | data formatting | bytes 524288 | tf_op jit(solution)/shard_map/layout_constraint | solution.py:117
  (10 shorter events, 0.2 us)
Async XLA Ops:
  0.0 2.5 %copy-start.1 = (bf16[2,4,15360]{2,1,0:T(4,128)(2,1)S(1)}, bf16[2,4,15360]{2,1,0:T(4,128)(2,1)}, u32[]{:S(2)}) copy-start(bf16[2,4,15360]{2,1,0:T(4,128)(2,1)} %param.9) | copy-start | bytes 737284
  1.8 1.1 %copy-start.2 = (f32[16,1024]{1,0:T(8,128)S(1)}, f32[16,1024]{1,0:T(8,128)}, u32[]{:S(2)}) copy-start(f32[16,1024]{1,0:T(8,128)} %param.10) | copy-start | bytes 196612
  2.0 1.7 %collective-permute-start = (bf16[2,2,32,1024]{3,2,1,0:T(8,128)(2,1)S(1)}, bf16[2,2,32,1024]{3,2,1,0:T(8,128)(2,1)S(1)}, u32[]{:S(2)}, u32[]{:S(2)}) collective-permute-start(bf16[2,2,32,1024]{3,2,1,0:T(8,128)(2,1)S(1)} %reshape.78), channel_id=1, source_target_pairs={{0,1},{1,0},{2,3},{3,2},{4,5},{5,4},{6,7},{7,6},{8,9},{9,8},{10,11... | collective-permute-start | bytes 786440 | tf_op jit(solution)/shard_map/ppermute | solution.py:93
  6.1 0.7 %copy-start.3 = (f32[4,256]{1,0:T(4,128)S(1)}, f32[4,256]{1,0:T(4,128)}, u32[]{:S(2)}) copy-start(f32[4,256]{1,0:T(4,128)} %constant.37.clone) | copy-start | bytes 12292
  6.1 0.7 %copy-start.4 = (f32[4,256]{1,0:T(4,128)S(1)}, f32[4,256]{1,0:T(4,128)}, u32[]{:S(2)}) copy-start(f32[4,256]{1,0:T(4,128)} %constant.38.clone) | copy-start | bytes 12292
  7.1 1.0 %copy-start = (bf16[512,256]{1,0:T(8,128)(2,1)S(1)}, bf16[512,256]{1,0:T(8,128)(2,1)}, u32[]{:S(2)}) copy-start(bf16[512,256]{1,0:T(8,128)(2,1)} %constant.42) | copy-start | bytes 786436
  8.1 8.6 %copy-start.5 = (s32[16]{0:T(128)S(1)}, s32[16]{0:T(128)}, u32[]{:S(2)}) copy-start(s32[16]{0:T(128)} %param.12) | copy-start | bytes 196
  8.1 8.6 %copy-start.6 = (s32[16]{0:T(128)S(1)}, s32[16]{0:T(128)}, u32[]{:S(2)}) copy-start(s32[16]{0:T(128)} %param.11) | copy-start | bytes 196
  9.4 21.8 %all-to-all-start = ((bf16[16,16,1024]{2,1,0:T(8,128)(2,1)}), bf16[16,16,1024]{2,1,0:T(8,128)(2,1)S(1)}, u32[]{:S(2)}, u32[]{:S(2)}) async-start(bf16[16,16,1024]{2,1,0:T(8,128)(2,1)} %bitcast.21), calls=%async_computation | async-start | bytes 1048576 | tf_op jit(solution)/shard_map/all_to_all | solution.py:104

commit v9 on v7

--- a/solution.py
+++ b/solution.py
@@ -98,7 +98,7 @@
     first = jnp.where(is_first, own, received)
     second = jnp.where(is_first, received, own)
     earlier = lax.dynamic_slice_in_dim(before, t * keep, keep, axis=1)
-    extended = jnp.concatenate([earlier, first, second], axis=2).reshape(2, keep, -1)
+    extended = jnp.concatenate([earlier, first, second], axis=2).astype(jnp.float32).reshape(2, keep, -1)
     spec_total = (extended.shape[2] - (tap_count - 1) * fft_len) // fft_len
     spectra = channelize(filter_bank(extended, coefficients, spec_total))
     spectra = spectra.reshape(dest_count, kl_count, -1)

time: 35.7 us -> 35.6 us (level)
  no operation moved by 1% of the time
where the time goes in v9:
time: 35.6 us; the launch traced here: 35.3 us
  waiting for transfers between devices  14.6 us (41%)
  starting transfers between devices  7.79 us (22%)
  local copies, waits for them, and re-layouts  6.53 us (18%)
  other arithmetic  3.96 us (11%)
  matrix products  2.14 us (6%)
    all_to_all x1, waiting for transfers between devices, local(): lax.all_to_all(spectra, ('blk', 'tch'), split_axis=0, concat_axis=0, tile...  13.7 us
    all_to_all x1, starting transfers between devices, local(): lax.all_to_all(spectra, ('blk', 'tch'), split_axis=0, concat_axis=0, tile...  7.28 us
    convert_element_type x1, other arithmetic, channelize(): x = filtered.astype(jnp.float32)  2.08 us
    another operation x1, local copies, waits for them, and re-layouts, local(): return with_layout_constraint(vis, Layout((0, 1, 2, 3)))  1.87 us
    reshape x1, local copies, waits for them, and re-layouts, local(): blocks = samples.reshape(2, row_count, -1, fft_len)  1.46 us
    unnamed x14, local copies, waits for them, and re-layouts  1.39 us
    dot_general x1, matrix products, channelize(): lax.dot_general(jnp.asarray(inner_matrix).astype(jnp.bfloat16), rows.asty...  1.28 us
    gather x2, local copies, waits for them, and re-layouts, local(): gathered = jnp.take(turned, slot_index, axis=0) * keep_mask[:, None, None]  0.95 us
  transfers between devices with their start and end apart: 2, of which 2 were waited for; matrix products, arithmetic and copies ran while one was open for 2% of the time, Pallas kernels for 0%

profile of v9, /device:TPU:0, one launch (start us, length us, event | category | flops | bytes accessed | tf_op | source)
XLA Modules:
  0.0 35.3 jit_solution(660452248959872105)
XLA Ops:
  0.0 0.0 copy-start.1
  0.0 0.0 copy-start.2
  0.0 1.5 %reshape.74 = bf16[2,4,32,1024]{3,2,1,0:T(8,128)(2,1)S(1)} reshape(bf16[2,4,32768]{2,1,0:T(4,128)(2,1)} %param.8) | data formatting | bytes 1048576 | tf_op jit(solution)/shard_map/reshape | solution.py:92
  1.5 0.5 %collective-permute-start = (bf16[2,2,32,1024]{3,2,1,0:T(8,128)(2,1)S(1)}, bf16[2,2,32,1024]{3,2,1,0:T(8,128)(2,1)S(1)}, u32[]{:S(2)}, u32[]{:S(2)}) collective-permute-start(bf16[2,2,32,1024]{3,2,1,0:T(8,128)(2,1)S(1)} %constant_dynamic-slice_fusion), channel_id=1, source_target_pairs={{0,1},{1,0},{2,3},{3,2},{4,5},{5,4},{6,7},{7,6},{8,9},{9,8},{10,11... | collective-permute-start | bytes 786440 | tf_op jit(solution)/shard_map/ppermute | solution.py:96
  2.0 0.0 copy-done.1
  2.0 0.1 reshape.73
  2.2 0.0 copy-done.2
  2.3 0.9 %collective-permute-done = bf16[2,2,32,1024]{3,2,1,0:T(8,128)(2,1)S(1)} collective-permute-done((bf16[2,2,32,1024]{3,2,1,0:T(8,128)(2,1)S(1)}, bf16[2,2,32,1024]{3,2,1,0:T(8,128)(2,1)S(1)}, u32[]{:S(2)}, u32[]{:S(2)}) %collective-permute-start) | collective-permute-done | bytes 262176 | tf_op jit(solution)/shard_map/ppermute | solution.py:96
  3.2 0.2 maximum_convert_fusion
  3.4 2.1 %fusion.21 = f32[2,2,64,1024]{3,2,1,0:T(8,128)S(1)} fusion(f32[2,2,79,1024]{3,2,1,0:T(8,128)S(1)} %maximum_convert_fusion, f32[1024]{0:T(1024)S(1)} %bitcast.56, f32[1024]{0:T(1024)S(1)} %bitcast.57, f32[1024]{0:T(1024)S(1)} %bitcast.43, f32[1024]{0:T(1024)S(1)} %bitcast.44, f32[1024]{0:T(1024)S(1)} %bitcast.45, f32[1024]{0:T(1024)S(1)} %bitcast.46, ...), kind=kLoop, calls=%fused_computation.54 | loop fusion | flops 8650752 | bytes 17891328 | tf_op jit(solution)/shard_map/convert_element_type | solution.py:44
  5.5 0.0 copy-start.3
  5.5 0.0 copy-start.4
  5.5 0.1 fusion.23
  5.6 0.1 fusion.25
  5.7 0.5 %copy-done.3 = f32[4,256]{1,0:T(4,128)S(1)} copy-done((f32[4,256]{1,0:T(4,128)S(1)}, f32[4,256]{1,0:T(4,128)}, u32[]{:S(2)}) %copy-start.3) | copy-done | bytes 4120
  6.2 0.0 copy-done.4
  6.2 0.1 fusion.33
  6.4 0.1 maximum_bitcast_fusion
  6.5 0.0 copy-start
  6.5 0.1 pad_maximum_fusion
  6.6 0.8 %copy-done = bf16[512,256]{1,0:T(8,128)(2,1)S(1)} copy-done((bf16[512,256]{1,0:T(8,128)(2,1)S(1)}, bf16[512,256]{1,0:T(8,128)(2,1)}, u32[]{:S(2)}) %copy-start) | copy-done | bytes 262168
  7.5 0.0 copy-start.5
  7.5 0.0 copy-start.6
  7.5 1.3 %convolution_convert_fusion = bf16[1024,256]{0,1:T(8,128)(2,1)} fusion(bf16[1024,512]{1,0:T(8,128)(2,1)S(1)} %bitcast.41, bf16[512,256]{1,0:T(8,128)(2,1)S(1)} %copy-done), kind=kOutput, calls=%fused_computation.6 | convolution fusion | flops 268697600 | bytes 1835008 | tf_op jit(solution)/shard_map/dot_general | solution.py:60
  8.8 7.3 %all-to-all-start = ((bf16[16,16,1024]{2,1,0:T(8,128)(2,1)}), bf16[16,16,1024]{2,1,0:T(8,128)(2,1)S(1)}, u32[]{:S(2)}, u32[]{:S(2)}) async-start(bf16[16,16,1024]{2,1,0:T(8,128)(2,1)} %bitcast.21), calls=%async_computation | async-start | bytes 1048576 | tf_op jit(solution)/shard_map/all_to_all | solution.py:105
  16.0 0.0 copy-done.5
  16.1 0.0 copy-done.6
  16.1 0.6 %scatter_custom_fusion = s32[16]{0:T(128)S(1)} fusion(s32[16]{0:T(128)S(1)} %compare_select_fusion.1, s32[16]{0:T(128)S(1)} %iota.3, s32[]{:T(128)} %constant.12.clone.1), kind=kCustom, calls=%fused_computation.79 | custom fusion | bytes 68 | tf_op jit(solution)/shard_map/scatter | solution.py:109
  16.8 13.7 %all-to-all-done = bf16[16,16,1024]{2,1,0:T(8,128)(2,1)S(1)} async-done(((bf16[16,16,1024]{2,1,0:T(8,128)(2,1)}), bf16[16,16,1024]{2,1,0:T(8,128)(2,1)S(1)}, u32[]{:S(2)}, u32[]{:S(2)}) %all-to-all-start) | async-done | bytes 524320 | tf_op jit(solution)/shard_map/all_to_all | solution.py:105
  30.5 0.6 %gather_fusion = bf16[16,16,1024]{2,1,0:T(8,128)(2,1)S(1)} fusion(bf16[16,16,1024]{2,1,0:T(8,128)(2,1)S(1)} %all-to-all-done, s32[1024]{0:T(1024)S(1)} %pad_clamp_fusion), kind=kCustom, calls=%fused_computation | custom fusion | bytes 1048640 | tf_op jit(solution)/shard_map/jit(_take)/gather | solution.py:112
  31.1 0.4 %gather.7 = bf16[16,16,4,2,128]{4,3,2,1,0:T(2,128)(2,1)S(1)} reshape(bf16[16,16,1024]{2,1,0:T(8,128)(2,1)S(1)} %gather_fusion) | data formatting | bytes 1048576 | tf_op jit(solution)/shard_map/jit(_take)/gather | solution.py:112
  31.5 0.6 %fusion.20 = bf16[16,16,4,2,128]{4,3,0,2,1:T(2,128)(2,1)S(1)} fusion(bf16[16,16,4,2,128]{4,3,2,1,0:T(2,128)(2,1)S(1)} %gather.7, pred[16]{0:T(512)(128)(4,1)S(1)} %compare_and_fusion, bf16[16]{0:T(256)(128)(2,1)S(1)} %convert_element_type.35), kind=kLoop, calls=%fused_computation.53 | loop fusion | flops 524288 | bytes 1048624 | tf_op jit(solution)/shard_map/mul | solution.py:112
  32.1 0.2 slice_negate_fusion
  32.3 0.4 %convolution_bitcast_fusion.1 = f32[1,64,32,32]{3,2,1,0:T(8,128)S(1)} fusion(bf16[64,32,128]{2,1,0:T(8,128)(2,1)S(1)} %bitcast.39), kind=kOutput, calls=%fused_computation.5 | convolution fusion | flops 16777216 | bytes 786432 | tf_op jit(solution)/shard_map/cak,cbk->cab/dot_general | solution.py:76
  32.7 0.5 %convolution_bitcast_fusion = f32[1,64,32,32]{3,2,1,0:T(8,128)S(1)} fusion(bf16[64,32,128]{2,1,0:T(8,128)(2,1)S(1)} %bitcast.40, bf16[64,32,64]{2,1,0:T(8,128)(2,1)S(1)} %get-tuple-element.19, bf16[64,32,64]{2,1,0:T(8,128)(2,1)S(1)} %get-tuple-element.18), kind=kOutput, calls=%fused_computation.4 | convolution fusion | flops 17825792 | bytes 1310720 | tf_op jit(solution)/shard_map/cak,cbk->cab/dot_general | solution.py:77
  33.2 0.3 fusion
  33.5 1.9 %copy.13 = bf16[2,64,32,32]{1,3,2,0:T(8,128)(2,1)} copy(bf16[2,64,32,32]{3,2,1,0:T(8,128)(2,1)S(1)} %fusion) | data formatting | bytes 524288 | tf_op jit(solution)/shard_map/layout_constraint | solution.py:118
  (11 shorter events, 0.2 us)
Async XLA Ops:
  0.0 2.0 %copy-start.1 = (bf16[2,4,15360]{2,1,0:T(4,128)(2,1)S(1)}, bf16[2,4,15360]{2,1,0:T(4,128)(2,1)}, u32[]{:S(2)}) copy-start(bf16[2,4,15360]{2,1,0:T(4,128)(2,1)} %param.9) | copy-start | bytes 737284
  0.0 2.2 %copy-start.2 = (f32[16,1024]{1,0:T(8,128)S(1)}, f32[16,1024]{1,0:T(8,128)}, u32[]{:S(2)}) copy-start(f32[16,1024]{1,0:T(8,128)} %param.10) | copy-start | bytes 196612
  1.5 1.7 %collective-permute-start = (bf16[2,2,32,1024]{3,2,1,0:T(8,128)(2,1)S(1)}, bf16[2,2,32,1024]{3,2,1,0:T(8,128)(2,1)S(1)}, u32[]{:S(2)}, u32[]{:S(2)}) collective-permute-start(bf16[2,2,32,1024]{3,2,1,0:T(8,128)(2,1)S(1)} %constant_dynamic-slice_fusion), channel_id=1, source_target_pairs={{0,1},{1,0},{2,3},{3,2},{4,5},{5,4},{6,7},{7,6},{8,9},{9,8},{10,11... | collective-permute-start | bytes 786440 | tf_op jit(solution)/shard_map/ppermute | solution.py:96
  5.5 0.7 %copy-start.3 = (f32[4,256]{1,0:T(4,128)S(1)}, f32[4,256]{1,0:T(4,128)}, u32[]{:S(2)}) copy-start(f32[4,256]{1,0:T(4,128)} %constant.37.clone) | copy-start | bytes 12292
  5.5 0.7 %copy-start.4 = (f32[4,256]{1,0:T(4,128)S(1)}, f32[4,256]{1,0:T(4,128)}, u32[]{:S(2)}) copy-start(f32[4,256]{1,0:T(4,128)} %constant.38.clone) | copy-start | bytes 12292
  6.5 1.0 %copy-start = (bf16[512,256]{1,0:T(8,128)(2,1)S(1)}, bf16[512,256]{1,0:T(8,128)(2,1)}, u32[]{:S(2)}) copy-start(bf16[512,256]{1,0:T(8,128)(2,1)} %constant.42) | copy-start | bytes 786436
  7.5 8.6 %copy-start.5 = (s32[16]{0:T(128)S(1)}, s32[16]{0:T(128)}, u32[]{:S(2)}) copy-start(s32[16]{0:T(128)} %param.12) | copy-start | bytes 196
  7.5 8.6 %copy-start.6 = (s32[16]{0:T(128)S(1)}, s32[16]{0:T(128)}, u32[]{:S(2)}) copy-start(s32[16]{0:T(128)} %param.11) | copy-start | bytes 196
  8.8 21.8 %all-to-all-start = ((bf16[16,16,1024]{2,1,0:T(8,128)(2,1)}), bf16[16,16,1024]{2,1,0:T(8,128)(2,1)S(1)}, u32[]{:S(2)}, u32[]{:S(2)}) async-start(bf16[16,16,1024]{2,1,0:T(8,128)(2,1)} %bitcast.21), calls=%async_computation | async-start | bytes 1048576 | tf_op jit(solution)/shard_map/all_to_all | solution.py:105

commit v10 on v7

--- a/solution.py
+++ b/solution.py
@@ -37,7 +37,7 @@
     return running.astype(jnp.bfloat16)
 
 
-def channelize(filtered):
+def channelize(filtered, origin):
     _, pol_count, spec_count, fft_len = filtered.shape
     inner = fft_len // RADIX
     twiddle_re, twiddle_im, inner_matrix = dft_tables(fft_len)
@@ -50,15 +50,19 @@
     dr, di = xr[1] - xr[3], xi[1] - xi[3]
     yr = jnp.stack([ar + br, cr + di, ar - br, cr - di], axis=0)
     yi = jnp.stack([ai + bi, ci - dr, ai - bi, ci + dr], axis=0)
-    tr = jnp.asarray(twiddle_re)[:, None, None, :]
-    ti = jnp.asarray(twiddle_im)[:, None, None, :]
+    angle = jnp.asarray(2.0 * np.pi * np.outer(np.arange(RADIX), np.arange(inner)) / fft_len, jnp.float32) + origin
+    tr, ti, inner_matrix = lax.optimization_barrier(
+        (jnp.cos(angle), -jnp.sin(angle), (jnp.asarray(inner_matrix) + origin).astype(jnp.bfloat16))
+    )
+    tr = tr[:, None, None, :]
+    ti = ti[:, None, None, :]
     zr = yr * tr - yi * ti
     zi = yr * ti + yi * tr
     real_rows = jnp.concatenate([zr, zi], axis=-1)
     imag_rows = jnp.concatenate([zi, -zr], axis=-1)
     rows = jnp.stack([real_rows, imag_rows], axis=2).reshape(RADIX * pol_count * 2 * spec_count, 2 * inner)
     product = lax.dot_general(
-        jnp.asarray(inner_matrix).astype(jnp.bfloat16),
+        inner_matrix,
         rows.astype(jnp.bfloat16),
         (((0,), (1,)), ((), ())),
         preferred_element_type=jnp.float32,
@@ -100,7 +104,7 @@
     earlier = lax.dynamic_slice_in_dim(before, t * keep, keep, axis=1)
     extended = jnp.concatenate([earlier, first, second], axis=2).reshape(2, keep, -1)
     spec_total = (extended.shape[2] - (tap_count - 1) * fft_len) // fft_len
-    spectra = channelize(filter_bank(extended, coefficients, spec_total))
+    spectra = channelize(filter_bank(extended, coefficients, spec_total), 0.0 * coefficients[0, 0])
     spectra = spectra.reshape(dest_count, kl_count, -1)
     turned = lax.all_to_all(spectra, ("blk", "tch"), split_axis=0, concat_axis=0, tiled=True)
     slot_index = (

time: 35.7 us -> 34.4 us (0.964)
  waiting for transfers between devices: 14.6 us -> 13.7 us
  local copies, waits for them, and re-layouts: 6.61 us -> 5.72 us
  between operations: 0.25 us -> 0.93 us
    unnamed x14 -> x12, local copies, waits for them, and re-layouts: 1.46 us -> 0.03 us
    ppermute x1, waiting for transfers between devices: 0.9 us -> 0.01 us  [local(): received = lax.ppermute(other, 'tch', [(0, 1), (1, 0)])]
    slice x0 -> x1, local copies, waits for them, and re-layouts: none -> 0.51 us  [local(): coefficients[0, 0]]
  transfers between devices with their start and end apart: 2 -> 2, of which waited for: 2 -> 1; matrix products, arithmetic and copies ran while one was open for 2% -> 4% of each run, Pallas kernels for 0% -> 0%
where the time goes in v10:
time: 34.4 us; the launch traced here: 34.2 us
  waiting for transfers between devices  13.7 us (40%)
  starting transfers between devices  7.55 us (22%)
  local copies, waits for them, and re-layouts  5.72 us (17%)
  other arithmetic  4.08 us (12%)
  matrix products  2.15 us (6%)
  between operations  0.93 us (3%)
    all_to_all x1, waiting for transfers between devices, local(): lax.all_to_all(spectra, ('blk', 'tch'), split_axis=0, concat_axis=0, tile...  13.7 us
    all_to_all x1, starting transfers between devices, local(): lax.all_to_all(spectra, ('blk', 'tch'), split_axis=0, concat_axis=0, tile...  7.02 us
    convert_element_type x1, other arithmetic, channelize(): x = filtered.astype(jnp.float32)  2.12 us
    another operation x1, local copies, waits for them, and re-layouts, local(): return with_layout_constraint(vis, Layout((0, 1, 2, 3)))  1.87 us
    reshape x1, local copies, waits for them, and re-layouts, local(): blocks = samples.reshape(2, row_count, -1, fft_len)  1.49 us
    dot_general x1, matrix products, channelize(): lax.dot_general(inner_matrix, rows.astype(jnp.bfloat16), (((0,), (1,)), (...  1.29 us
    gather x2, local copies, waits for them, and re-layouts, local(): gathered = jnp.take(turned, slot_index, axis=0) * keep_mask[:, None, None]  0.95 us
  transfers between devices with their start and end apart: 2, of which 1 were waited for; matrix products, arithmetic and copies ran while one was open for 4% of the time, Pallas kernels for 0%

profile of v10, /device:TPU:0, one launch (start us, length us, event | category | flops | bytes accessed | tf_op | source)
XLA Modules:
  0.0 34.2 jit_solution(3022826322581731186)
XLA Ops:
  0.0 0.0 copy-start.1
  0.0 0.0 copy-start.2
  0.0 0.0 copy-start.3
  0.0 0.0 copy-start
  0.0 1.5 %reshape.76 = bf16[2,4,32,1024]{3,2,1,0:T(8,128)(2,1)S(1)} reshape(bf16[2,4,32768]{2,1,0:T(4,128)(2,1)} %param.7) | data formatting | bytes 1048576 | tf_op jit(solution)/shard_map/reshape | solution.py:96
  1.5 0.5 %collective-permute-start = (bf16[2,2,32,1024]{3,2,1,0:T(8,128)(2,1)S(1)}, bf16[2,2,32,1024]{3,2,1,0:T(8,128)(2,1)S(1)}, u32[]{:S(2)}, u32[]{:S(2)}) collective-permute-start(bf16[2,2,32,1024]{3,2,1,0:T(8,128)(2,1)S(1)} %constant_dynamic-slice_fusion), channel_id=1, source_target_pairs={{0,1},{1,0},{2,3},{3,2},{4,5},{5,4},{6,7},{7,6},{8,9},{9,8},{10,11... | collective-permute-start | bytes 786440 | tf_op jit(solution)/shard_map/ppermute | solution.py:100
  2.1 0.0 copy-done.1
  2.1 0.1 reshape.75
  2.2 0.0 copy-done.2
  2.2 0.5 %slice.144 = f32[1,1]{1,0:T(1,128)} slice(f32[16,1024]{1,0:T(8,128)S(1)} %copy-done.2), slice={[0:1], [0:1]} | slice | bytes 8 | tf_op jit(solution)/shard_map/slice | solution.py:107
  3.4 0.0 copy-done.3
  3.4 0.1 fusion.14
  3.5 0.0 copy-done
  3.6 0.0 collective-permute-done
  3.7 0.2 pad_maximum_fusion.1
  3.9 2.1 %fusion.5 = f32[2,2,64,1024]{3,2,1,0:T(8,128)S(1)} fusion(bf16[2,2,32,1024]{3,2,1,0:T(8,128)(2,1)S(1)} %get-tuple-element.23, bf16[2,2,32,1024]{3,2,1,0:T(8,128)(2,1)S(1)} %get-tuple-element.22, f32[1024]{0:T(1024)S(1)} %bitcast.55, bf16[2,2,79,1024]{3,2,1,0:T(8,128)(2,1)S(1)} %pad_maximum_fusion.1, f32[1024]{0:T(1024)S(1)} %bitcast.56, ...), kind=kLoop, calls=%fused_computation.24 | loop fusion | flops 13631488 | bytes 9502720 | tf_op jit(solution)/shard_map/convert_element_type | solution.py:44
  6.0 0.1 fusion.7
  6.1 0.1 fusion.9
  6.1 0.1 fusion.18
  6.3 0.1 maximum_bitcast_fusion
  6.4 0.1 pad_maximum_fusion
  6.6 0.0 copy-start.4
  6.6 0.0 copy-start.5
  6.6 1.3 %convolution_convert_fusion = bf16[256,1024]{1,0:T(8,128)(2,1)} fusion(bf16[512,256]{1,0:T(8,128)(2,1)S(1)} %add_convert_fusion.1, bf16[1024,512]{1,0:T(8,128)(2,1)S(1)} %bitcast.40), kind=kOutput, calls=%fused_computation.6 | convolution fusion | flops 268697600 | bytes 1835008 | tf_op jit(solution)/shard_map/dot_general | solution.py:64
  7.9 7.0 %all-to-all-start = ((bf16[16,16,1024]{2,1,0:T(8,128)(2,1)}), bf16[16,16,1024]{2,1,0:T(8,128)(2,1)S(1)}, u32[]{:S(2)}, u32[]{:S(2)}) async-start(bf16[16,16,1024]{2,1,0:T(8,128)(2,1)} %bitcast.21), calls=%async_computation | async-start | bytes 1048576 | tf_op jit(solution)/shard_map/all_to_all | solution.py:109
  14.9 0.0 copy-done.4
  14.9 0.0 copy-done.5
  14.9 0.6 %scatter_custom_fusion = s32[16]{0:T(128)S(1)} fusion(s32[16]{0:T(128)S(1)} %compare_select_fusion.1, s32[16]{0:T(128)S(1)} %iota.3, s32[]{:T(128)} %constant.12.clone.1), kind=kCustom, calls=%fused_computation.52 | custom fusion | bytes 68 | tf_op jit(solution)/shard_map/scatter | solution.py:113
  15.6 13.7 %all-to-all-done = bf16[16,16,1024]{2,1,0:T(8,128)(2,1)S(1)} async-done(((bf16[16,16,1024]{2,1,0:T(8,128)(2,1)}), bf16[16,16,1024]{2,1,0:T(8,128)(2,1)S(1)}, u32[]{:S(2)}, u32[]{:S(2)}) %all-to-all-start) | async-done | bytes 524320 | tf_op jit(solution)/shard_map/all_to_all | solution.py:109
  29.4 0.6 %gather_fusion = bf16[16,16,1024]{2,1,0:T(8,128)(2,1)S(1)} fusion(bf16[16,16,1024]{2,1,0:T(8,128)(2,1)S(1)} %all-to-all-done, s32[1024]{0:T(1024)S(1)} %pad_clamp_fusion), kind=kCustom, calls=%fused_computation | custom fusion | bytes 1048640 | tf_op jit(solution)/shard_map/jit(_take)/gather | solution.py:116
  29.9 0.4 %gather.7 = bf16[16,16,4,2,128]{4,3,2,1,0:T(2,128)(2,1)S(1)} reshape(bf16[16,16,1024]{2,1,0:T(8,128)(2,1)S(1)} %gather_fusion) | data formatting | bytes 1048576 | tf_op jit(solution)/shard_map/jit(_take)/gather | solution.py:116
  30.3 0.6 %fusion.4 = bf16[16,16,4,2,128]{4,3,0,2,1:T(2,128)(2,1)S(1)} fusion(bf16[16,16,4,2,128]{4,3,2,1,0:T(2,128)(2,1)S(1)} %gather.7, pred[16]{0:T(512)(128)(4,1)S(1)} %compare_and_fusion, bf16[16]{0:T(256)(128)(2,1)S(1)} %convert_element_type.91), kind=kLoop, calls=%fused_computation.23 | loop fusion | flops 524288 | bytes 1048624 | tf_op jit(solution)/shard_map/mul | solution.py:116
  30.9 0.2 slice_negate_fusion
  31.2 0.4 %convolution_bitcast_fusion.1 = f32[1,64,32,32]{3,2,1,0:T(8,128)S(1)} fusion(bf16[64,32,128]{2,1,0:T(8,128)(2,1)S(1)} %bitcast.38), kind=kOutput, calls=%fused_computation.5 | convolution fusion | flops 16777216 | bytes 786432 | tf_op jit(solution)/shard_map/cak,cbk->cab/dot_general | solution.py:80
  31.6 0.5 %convolution_bitcast_fusion = f32[1,64,32,32]{3,2,1,0:T(8,128)S(1)} fusion(bf16[64,32,128]{2,1,0:T(8,128)(2,1)S(1)} %bitcast.39, bf16[64,32,64]{2,1,0:T(8,128)(2,1)S(1)} %get-tuple-element.25, bf16[64,32,64]{2,1,0:T(8,128)(2,1)S(1)} %get-tuple-element.24), kind=kOutput, calls=%fused_computation.4 | convolution fusion | flops 17825792 | bytes 1310720 | tf_op jit(solution)/shard_map/cak,cbk->cab/dot_general | solution.py:81
  32.0 0.3 fusion
  32.3 1.9 %copy.12 = bf16[2,64,32,32]{1,3,2,0:T(8,128)(2,1)} copy(bf16[2,64,32,32]{3,2,1,0:T(8,128)(2,1)S(1)} %fusion) | data formatting | bytes 524288 | tf_op jit(solution)/shard_map/layout_constraint | solution.py:122
  (12 shorter events, 0.3 us)
Async XLA Ops:
  0.0 2.1 %copy-start.1 = (bf16[2,4,15360]{2,1,0:T(4,128)(2,1)S(1)}, bf16[2,4,15360]{2,1,0:T(4,128)(2,1)}, u32[]{:S(2)}) copy-start(bf16[2,4,15360]{2,1,0:T(4,128)(2,1)} %param.8) | copy-start | bytes 737284
  0.0 2.2 %copy-start.2 = (f32[16,1024]{1,0:T(8,128)S(1)}, f32[16,1024]{1,0:T(8,128)}, u32[]{:S(2)}) copy-start(f32[16,1024]{1,0:T(8,128)} %param.9) | copy-start | bytes 196612
  0.0 3.4 %copy-start.3 = (f32[4,256]{1,0:T(4,128)S(1)}, f32[4,256]{1,0:T(4,128)}, u32[]{:S(2)}) copy-start(f32[4,256]{1,0:T(4,128)} %constant.38.clone) | copy-start | bytes 12292
  0.0 3.5 %copy-start = (f32[512,256]{1,0:T(8,128)S(1)}, f32[512,256]{1,0:T(8,128)}, u32[]{:S(2)}) copy-start(f32[512,256]{1,0:T(8,128)} %constant.39.clone) | copy-start | bytes 1572868
  1.5 2.1 %collective-permute-start = (bf16[2,2,32,1024]{3,2,1,0:T(8,128)(2,1)S(1)}, bf16[2,2,32,1024]{3,2,1,0:T(8,128)(2,1)S(1)}, u32[]{:S(2)}, u32[]{:S(2)}) collective-permute-start(bf16[2,2,32,1024]{3,2,1,0:T(8,128)(2,1)S(1)} %constant_dynamic-slice_fusion), channel_id=1, source_target_pairs={{0,1},{1,0},{2,3},{3,2},{4,5},{5,4},{6,7},{7,6},{8,9},{9,8},{10,11... | collective-permute-start | bytes 786440 | tf_op jit(solution)/shard_map/ppermute | solution.py:100
  6.6 8.3 %copy-start.4 = (s32[16]{0:T(128)S(1)}, s32[16]{0:T(128)}, u32[]{:S(2)}) copy-start(s32[16]{0:T(128)} %param.11) | copy-start | bytes 196
  6.6 8.3 %copy-start.5 = (s32[16]{0:T(128)S(1)}, s32[16]{0:T(128)}, u32[]{:S(2)}) copy-start(s32[16]{0:T(128)} %param.10) | copy-start | bytes 196
  7.9 21.5 %all-to-all-start = ((bf16[16,16,1024]{2,1,0:T(8,128)(2,1)}), bf16[16,16,1024]{2,1,0:T(8,128)(2,1)S(1)}, u32[]{:S(2)}, u32[]{:S(2)}) async-start(bf16[16,16,1024]{2,1,0:T(8,128)(2,1)} %bitcast.21), calls=%async_computation | async-start | bytes 1048576 | tf_op jit(solution)/shard_map/all_to_all | solution.py:109

commit v11 on v10

--- a/solution.py
+++ b/solution.py
@@ -112,12 +112,18 @@
         .at[station_of_slot]
         .set(jnp.arange(station_count, dtype=jnp.int32))
     )
-    keep_mask = station_ok.astype(turned.dtype)
-    gathered = jnp.take(turned, slot_index, axis=0) * keep_mask[:, None, None]
-    gathered = gathered.reshape(station_count, kl_count, RADIX, POLS, 2 * spec_total)
-    ordered = jnp.transpose(gathered, (1, 2, 0, 3, 4)).reshape(
-        kl_count * RADIX, station_count * POLS, 2 * spec_total
-    )
+    chan_count = kl_count * RADIX
+    input_count = station_count * POLS
+    by_source = turned.reshape(station_count, kl_count, RADIX, POLS, 2 * spec_total)
+    by_source = jnp.transpose(by_source, (1, 2, 3, 0, 4)).reshape(chan_count, input_count, 2 * spec_total)
+    position = jnp.arange(input_count, dtype=jnp.int32)
+    wanted = slot_index[position // POLS] + (position % POLS) * station_count
+    select = (wanted[:, None] == position[None, :]).astype(turned.dtype)
+    select = select * station_ok[position // POLS].astype(turned.dtype)[:, None]
+    select = jnp.broadcast_to(select, (chan_count, input_count, input_count))
+    ordered = jnp.einsum(
+        "cij,cjk->cik", select, by_source, preferred_element_type=jnp.float32
+    ).astype(turned.dtype)
     vis = correlate_full(ordered, 1.0 / spec_total)
     return with_layout_constraint(vis, Layout((0, 1, 2, 3)))
 

time: 34.4 us -> 34.1 us (level)
  local copies, waits for them, and re-layouts: 5.72 us -> 7.16 us
  waiting for transfers between devices: 13.7 us -> 12.3 us
  other arithmetic: 4.08 us -> 3.55 us
    all_to_all x1, waiting for transfers between devices: 13.7 us -> 12.3 us  [local(): lax.all_to_all(spectra, ('blk', 'tch'), split_axis=0, concat_axis=0, tile...]
    reshape x0 -> x2, local copies, waits for them, and re-layouts: none -> 0.98 us  [local(): turned.reshape(station_count, kl_count, RADIX, POLS, 2 * spec_total)]
    mul x1, other arithmetic: 0.62 us -> 0.07 us  [local(): select = select * station_ok[position // POLS].astype(turned.dtype)[:, None]]
    gather x2, local copies, waits for them, and re-layouts: 0.95 us -> 1.4 us  [the longest x1 0.7 us: local(): select = select * station_ok[position // POLS].astype(turned.dtype)[:, None]]
  transfers between devices with their start and end apart: 2 -> 2, of which waited for: 1 -> 1; matrix products, arithmetic and copies ran while one was open for 4% -> 9% of each run, Pallas kernels for 0% -> 0%
where the time goes in v11:
time: 34.1 us; the launch traced here: 33.9 us
  waiting for transfers between devices  12.3 us (36%)
  starting transfers between devices  7.55 us (22%)
  local copies, waits for them, and re-layouts  7.16 us (21%)
  other arithmetic  3.55 us (10%)
  matrix products  2.42 us (7%)
  between operations  0.92 us (3%)
    all_to_all x1, waiting for transfers between devices, local(): lax.all_to_all(spectra, ('blk', 'tch'), split_axis=0, concat_axis=0, tile...  12.3 us
    all_to_all x1, starting transfers between devices, local(): lax.all_to_all(spectra, ('blk', 'tch'), split_axis=0, concat_axis=0, tile...  7.02 us
    convert_element_type x1, other arithmetic, channelize(): x = filtered.astype(jnp.float32)  2.12 us
    another operation x1, local copies, waits for them, and re-layouts, local(): return with_layout_constraint(vis, Layout((0, 1, 2, 3)))  1.88 us
    reshape x1, local copies, waits for them, and re-layouts, local(): blocks = samples.reshape(2, row_count, -1, fft_len)  1.49 us
    dot_general x1, matrix products, channelize(): lax.dot_general(inner_matrix, rows.astype(jnp.bfloat16), (((0,), (1,)), (...  1.28 us
    reshape x2, local copies, waits for them, and re-layouts, local(): turned.reshape(station_count, kl_count, RADIX, POLS, 2 * spec_total)  0.98 us
    gather x1, local copies, waits for them, and re-layouts, local(): select = select * station_ok[position // POLS].astype(turned.dtype)[:, None]  0.7 us
  transfers between devices with their start and end apart: 2, of which 1 were waited for; matrix products, arithmetic and copies ran while one was open for 9% of the time, Pallas kernels for 0%

profile of v11, /device:TPU:0, one launch (start us, length us, event | category | flops | bytes accessed | tf_op | source)
XLA Modules:
  0.0 33.9 jit_solution(3324481785602355242)
XLA Ops:
  0.0 0.0 copy-start
  0.0 0.0 copy-start.2
  0.0 0.0 copy-start.3
  0.0 0.0 copy-start.4
  0.0 0.0 copy-start.1
  0.0 1.5 %reshape.130 = bf16[2,4,32,1024]{3,2,1,0:T(8,128)(2,1)S(1)} reshape(bf16[2,4,32768]{2,1,0:T(4,128)(2,1)} %param.7) | data formatting | bytes 1048576 | tf_op jit(solution)/shard_map/reshape | solution.py:96
  1.6 0.5 %collective-permute-start = (bf16[2,2,32,1024]{3,2,1,0:T(8,128)(2,1)S(1)}, bf16[2,2,32,1024]{3,2,1,0:T(8,128)(2,1)S(1)}, u32[]{:S(2)}, u32[]{:S(2)}) collective-permute-start(bf16[2,2,32,1024]{3,2,1,0:T(8,128)(2,1)S(1)} %constant_dynamic-slice_fusion), channel_id=1, source_target_pairs={{0,1},{1,0},{2,3},{3,2},{4,5},{5,4},{6,7},{7,6},{8,9},{9,8},{10,11... | collective-permute-start | bytes 786440 | tf_op jit(solution)/shard_map/ppermute | solution.py:100
  2.1 0.0 copy-done.2
  2.1 0.1 reshape.129
  2.2 0.0 copy-done.3
  2.3 0.5 %slice.144 = f32[1,1]{1,0:T(1,128)} slice(f32[16,1024]{1,0:T(8,128)S(1)} %copy-done.3), slice={[0:1], [0:1]} | slice | bytes 8 | tf_op jit(solution)/shard_map/slice | solution.py:107
  3.4 0.0 copy-done.4
  3.4 0.1 fusion.15
  3.5 0.0 copy-done.1
  3.6 0.0 collective-permute-done
  3.7 0.2 pad_maximum_fusion.1
  3.9 2.1 %fusion.4 = f32[2,2,64,1024]{3,2,1,0:T(8,128)S(1)} fusion(bf16[2,2,32,1024]{3,2,1,0:T(8,128)(2,1)S(1)} %get-tuple-element.23, bf16[2,2,32,1024]{3,2,1,0:T(8,128)(2,1)S(1)} %get-tuple-element.22, f32[1024]{0:T(1024)S(1)} %bitcast.56, bf16[2,2,79,1024]{3,2,1,0:T(8,128)(2,1)S(1)} %pad_maximum_fusion.1, f32[1024]{0:T(1024)S(1)} %bitcast.57, ...), kind=kLoop, calls=%fused_computation.24 | loop fusion | flops 13631488 | bytes 9502720 | tf_op jit(solution)/shard_map/convert_element_type | solution.py:44
  6.0 0.1 fusion.7
  6.1 0.1 fusion.9
  6.2 0.2 fusion.22
  6.4 0.1 maximum_bitcast_fusion
  6.5 0.1 pad_maximum_fusion
  6.6 0.0 copy-start.5
  6.6 1.3 %convolution_convert_fusion.1 = bf16[256,1024]{1,0:T(8,128)(2,1)} fusion(bf16[512,256]{1,0:T(8,128)(2,1)S(1)} %add_convert_fusion.1, bf16[1024,512]{1,0:T(8,128)(2,1)S(1)} %bitcast.40), kind=kOutput, calls=%fused_computation.8 | convolution fusion | flops 268697600 | bytes 1835008 | tf_op jit(solution)/shard_map/dot_general | solution.py:64
  7.9 7.0 %all-to-all-start = ((bf16[16,16,1024]{2,1,0:T(8,128)(2,1)}), bf16[16,16,1024]{2,1,0:T(8,128)(2,1)S(1)}, u32[]{:S(2)}, u32[]{:S(2)}) async-start(bf16[16,16,1024]{2,1,0:T(8,128)(2,1)} %bitcast.22), calls=%async_computation | async-start | bytes 1048576 | tf_op jit(solution)/shard_map/all_to_all | solution.py:109
  14.9 0.0 copy-done.5
  14.9 0.6 %scatter_custom_fusion = s32[16]{0:T(128)S(1)} fusion(s32[16]{0:T(128)S(1)} %compare_select_fusion.1, s32[16]{0:T(128)S(1)} %iota.16, s32[]{:T(128)} %constant.45.clone.1), kind=kCustom, calls=%fused_computation.62 | custom fusion | bytes 68 | tf_op jit(solution)/shard_map/scatter | solution.py:113
  15.6 0.7 %gather_fusion = s32[32]{0:T(128)S(1)} fusion(s32[16]{0:T(128)S(1)} %scatter_custom_fusion, s32[1024]{0:T(1024)S(1)} %pad_clamp_fusion), kind=kCustom, calls=%fused_computation | custom fusion | bytes 384 | tf_op jit(solution)/shard_map/gather | solution.py:120
  16.3 0.0 copy-done
  16.3 0.7 %gather_fusion.1 = s32[32]{0:T(128)S(1)} fusion(s32[16]{0:T(128)S(1)} %copy-done, s32[1024]{0:T(1024)S(1)} %pad_clamp_fusion), kind=kCustom, calls=%fused_computation.1 | custom fusion | bytes 384 | tf_op jit(solution)/shard_map/gather | solution.py:122
  17.0 0.1 fusion.14
  17.1 12.3 %all-to-all-done = bf16[16,16,1024]{2,1,0:T(8,128)(2,1)S(1)} async-done(((bf16[16,16,1024]{2,1,0:T(8,128)(2,1)}), bf16[16,16,1024]{2,1,0:T(8,128)(2,1)S(1)}, u32[]{:S(2)}, u32[]{:S(2)}) %all-to-all-start) | async-done | bytes 524320 | tf_op jit(solution)/shard_map/all_to_all | solution.py:109
  29.4 0.4 %reshape.132 = bf16[16,16,4,2,128]{4,3,2,1,0:T(2,128)(2,1)S(1)} reshape(bf16[16,16,1024]{2,1,0:T(8,128)(2,1)S(1)} %all-to-all-done) | data formatting | bytes 1048576 | tf_op jit(solution)/shard_map/reshape | solution.py:117
  29.7 0.6 %copy.11 = bf16[16,16,4,2,128]{4,0,3,2,1:T(8,128)(2,1)S(1)} copy(bf16[16,16,4,2,128]{4,3,2,1,0:T(2,128)(2,1)S(1)} %reshape.132) | data formatting | bytes 1048576 | tf_op jit(solution)/shard_map/reshape | solution.py:117
  30.4 0.3 convolution_convert_fusion
  30.6 0.2 slice_negate_fusion
  30.9 0.4 %convolution_bitcast_fusion.1 = f32[1,64,32,32]{3,2,1,0:T(8,128)S(1)} fusion(bf16[64,32,128]{2,1,0:T(8,128)(2,1)S(1)} %convolution_convert_fusion), kind=kOutput, calls=%fused_computation.6 | convolution fusion | flops 16777216 | bytes 786432 | tf_op jit(solution)/shard_map/cak,cbk->cab/dot_general | solution.py:80
  31.3 0.5 %convolution_bitcast_fusion = f32[1,64,32,32]{3,2,1,0:T(8,128)S(1)} fusion(bf16[64,32,128]{2,1,0:T(8,128)(2,1)S(1)} %convolution_convert_fusion, bf16[64,32,64]{2,1,0:T(8,128)(2,1)S(1)} %get-tuple-element.25, bf16[64,32,64]{2,1,0:T(8,128)(2,1)S(1)} %get-tuple-element.24), kind=kOutput, calls=%fused_computation.5 | convolution fusion | flops 17825792 | bytes 1310720 | tf_op jit(solution)/shard_map/cak,cbk->cab/dot_general | solution.py:81
  31.7 0.3 fusion
  32.0 1.9 %copy.12 = bf16[2,64,32,32]{1,3,2,0:T(8,128)(2,1)} copy(bf16[2,64,32,32]{3,2,1,0:T(8,128)(2,1)S(1)} %fusion) | data formatting | bytes 524288 | tf_op jit(solution)/shard_map/layout_constraint | solution.py:128
  (12 shorter events, 0.3 us)
Async XLA Ops:
  0.0 16.3 %copy-start = (s32[16]{0:T(128)S(1)}, s32[16]{0:T(128)}, u32[]{:S(2)}) copy-start(s32[16]{0:T(128)} %param.11) | copy-start | bytes 196
  0.0 2.1 %copy-start.2 = (bf16[2,4,15360]{2,1,0:T(4,128)(2,1)S(1)}, bf16[2,4,15360]{2,1,0:T(4,128)(2,1)}, u32[]{:S(2)}) copy-start(bf16[2,4,15360]{2,1,0:T(4,128)(2,1)} %param.8) | copy-start | bytes 737284
  0.0 2.2 %copy-start.3 = (f32[16,1024]{1,0:T(8,128)S(1)}, f32[16,1024]{1,0:T(8,128)}, u32[]{:S(2)}) copy-start(f32[16,1024]{1,0:T(8,128)} %param.9) | copy-start | bytes 196612
  0.0 3.4 %copy-start.4 = (f32[4,256]{1,0:T(4,128)S(1)}, f32[4,256]{1,0:T(4,128)}, u32[]{:S(2)}) copy-start(f32[4,256]{1,0:T(4,128)} %constant.55.clone) | copy-start | bytes 12292
  0.0 3.5 %copy-start.1 = (f32[512,256]{1,0:T(8,128)S(1)}, f32[512,256]{1,0:T(8,128)}, u32[]{:S(2)}) copy-start(f32[512,256]{1,0:T(8,128)} %constant.56.clone) | copy-start | bytes 1572868
  1.6 2.1 %collective-permute-start = (bf16[2,2,32,1024]{3,2,1,0:T(8,128)(2,1)S(1)}, bf16[2,2,32,1024]{3,2,1,0:T(8,128)(2,1)S(1)}, u32[]{:S(2)}, u32[]{:S(2)}) collective-permute-start(bf16[2,2,32,1024]{3,2,1,0:T(8,128)(2,1)S(1)} %constant_dynamic-slice_fusion), channel_id=1, source_target_pairs={{0,1},{1,0},{2,3},{3,2},{4,5},{5,4},{6,7},{7,6},{8,9},{9,8},{10,11... | collective-permute-start | bytes 786440 | tf_op jit(solution)/shard_map/ppermute | solution.py:100
  6.6 8.3 %copy-start.5 = (s32[16]{0:T(128)S(1)}, s32[16]{0:T(128)}, u32[]{:S(2)}) copy-start(s32[16]{0:T(128)} %param.10) | copy-start | bytes 196
  7.9 21.5 %all-to-all-start = ((bf16[16,16,1024]{2,1,0:T(8,128)(2,1)}), bf16[16,16,1024]{2,1,0:T(8,128)(2,1)S(1)}, u32[]{:S(2)}, u32[]{:S(2)}) async-start(bf16[16,16,1024]{2,1,0:T(8,128)(2,1)} %bitcast.22), calls=%async_computation | async-start | bytes 1048576 | tf_op jit(solution)/shard_map/all_to_all | solution.py:109

commit v12 on v11

--- a/solution.py
+++ b/solution.py
@@ -114,8 +114,8 @@
     )
     chan_count = kl_count * RADIX
     input_count = station_count * POLS
-    by_source = turned.reshape(station_count, kl_count, RADIX, POLS, 2 * spec_total)
-    by_source = jnp.transpose(by_source, (1, 2, 3, 0, 4)).reshape(chan_count, input_count, 2 * spec_total)
+    by_source = turned.reshape(station_count, kl_count, RADIX * POLS, 2 * spec_total)
+    by_source = jnp.transpose(by_source, (1, 2, 0, 3)).reshape(chan_count, input_count, 2 * spec_total)
     position = jnp.arange(input_count, dtype=jnp.int32)
     wanted = slot_index[position // POLS] + (position % POLS) * station_count
     select = (wanted[:, None] == position[None, :]).astype(turned.dtype)

time: 34.1 us -> 33.6 us (0.985)
  local copies, waits for them, and re-layouts: 7.16 us -> 6.61 us
    reshape x2 -> x1, local copies, waits for them, and re-layouts: 0.98 us -> 0.34 us  [local(): turned.reshape(station_count, kl_count, RADIX * POLS, 2 * spec_total)]
where the time goes in v12:
time: 33.6 us; the launch traced here: 33.4 us
  waiting for transfers between devices  12.3 us (37%)
  starting transfers between devices  7.55 us (22%)
  local copies, waits for them, and re-layouts  6.61 us (20%)
  other arithmetic  3.55 us (11%)
  matrix products  2.43 us (7%)
  between operations  0.93 us (3%)
    all_to_all x1, waiting for transfers between devices, local(): lax.all_to_all(spectra, ('blk', 'tch'), split_axis=0, concat_axis=0, tile...  12.3 us
    all_to_all x1, starting transfers between devices, local(): lax.all_to_all(spectra, ('blk', 'tch'), split_axis=0, concat_axis=0, tile...  7.02 us
    convert_element_type x1, other arithmetic, channelize(): x = filtered.astype(jnp.float32)  2.12 us
    another operation x1, local copies, waits for them, and re-layouts, local(): return with_layout_constraint(vis, Layout((0, 1, 2, 3)))  1.88 us
    reshape x1, local copies, waits for them, and re-layouts, local(): blocks = samples.reshape(2, row_count, -1, fft_len)  1.49 us
    dot_general x1, matrix products, channelize(): lax.dot_general(inner_matrix, rows.astype(jnp.bfloat16), (((0,), (1,)), (...  1.28 us
    gather x1, local copies, waits for them, and re-layouts, local(): select = select * station_ok[position // POLS].astype(turned.dtype)[:, None]  0.7 us
    gather x1, local copies, waits for them, and re-layouts, local(): wanted = slot_index[position // POLS] + position % POLS * station_count  0.7 us
  transfers between devices with their start and end apart: 2, of which 1 were waited for; matrix products, arithmetic and copies ran while one was open for 9% of the time, Pallas kernels for 0%

profile of v12, /device:TPU:0, one launch (start us, length us, event | category | flops | bytes accessed | tf_op | source)
XLA Modules:
  0.0 33.4 jit_solution(11282202427813133303)
XLA Ops:
  0.0 0.0 copy-start
  0.0 0.0 copy-start.2
  0.0 0.0 copy-start.3
  0.0 0.0 copy-start.4
  0.0 0.0 copy-start.1
  0.0 1.5 %reshape.130 = bf16[2,4,32,1024]{3,2,1,0:T(8,128)(2,1)S(1)} reshape(bf16[2,4,32768]{2,1,0:T(4,128)(2,1)} %param.7) | data formatting | bytes 1048576 | tf_op jit(solution)/shard_map/reshape | solution.py:96
  1.6 0.5 %collective-permute-start = (bf16[2,2,32,1024]{3,2,1,0:T(8,128)(2,1)S(1)}, bf16[2,2,32,1024]{3,2,1,0:T(8,128)(2,1)S(1)}, u32[]{:S(2)}, u32[]{:S(2)}) collective-permute-start(bf16[2,2,32,1024]{3,2,1,0:T(8,128)(2,1)S(1)} %constant_dynamic-slice_fusion), channel_id=1, source_target_pairs={{0,1},{1,0},{2,3},{3,2},{4,5},{5,4},{6,7},{7,6},{8,9},{9,8},{10,11... | collective-permute-start | bytes 786440 | tf_op jit(solution)/shard_map/ppermute | solution.py:100
  2.1 0.0 copy-done.2
  2.1 0.1 reshape.129
  2.2 0.0 copy-done.3
  2.3 0.5 %slice.144 = f32[1,1]{1,0:T(1,128)} slice(f32[16,1024]{1,0:T(8,128)S(1)} %copy-done.3), slice={[0:1], [0:1]} | slice | bytes 8 | tf_op jit(solution)/shard_map/slice | solution.py:107
  3.4 0.0 copy-done.4
  3.4 0.1 fusion.15
  3.5 0.0 copy-done.1
  3.6 0.0 collective-permute-done
  3.7 0.2 pad_maximum_fusion.1
  3.9 2.1 %fusion.4 = f32[2,2,64,1024]{3,2,1,0:T(8,128)S(1)} fusion(bf16[2,2,32,1024]{3,2,1,0:T(8,128)(2,1)S(1)} %get-tuple-element.23, bf16[2,2,32,1024]{3,2,1,0:T(8,128)(2,1)S(1)} %get-tuple-element.22, f32[1024]{0:T(1024)S(1)} %bitcast.62, bf16[2,2,79,1024]{3,2,1,0:T(8,128)(2,1)S(1)} %pad_maximum_fusion.1, f32[1024]{0:T(1024)S(1)} %bitcast.63, ...), kind=kLoop, calls=%fused_computation.24 | loop fusion | flops 13631488 | bytes 9502720 | tf_op jit(solution)/shard_map/convert_element_type | solution.py:44
  6.0 0.1 fusion.7
  6.1 0.1 fusion.9
  6.2 0.2 fusion.22
  6.4 0.1 maximum_bitcast_fusion
  6.5 0.1 pad_maximum_fusion
  6.6 0.0 copy-start.5
  6.6 1.3 %convolution_convert_fusion.1 = bf16[256,1024]{1,0:T(8,128)(2,1)} fusion(bf16[512,256]{1,0:T(8,128)(2,1)S(1)} %add_convert_fusion.1, bf16[1024,512]{1,0:T(8,128)(2,1)S(1)} %bitcast.44), kind=kOutput, calls=%fused_computation.8 | convolution fusion | flops 268697600 | bytes 1835008 | tf_op jit(solution)/shard_map/dot_general | solution.py:64
  7.9 7.0 %all-to-all-start = ((bf16[16,16,1024]{2,1,0:T(8,128)(2,1)}), bf16[16,16,1024]{2,1,0:T(8,128)(2,1)S(1)}, u32[]{:S(2)}, u32[]{:S(2)}) async-start(bf16[16,16,1024]{2,1,0:T(8,128)(2,1)} %bitcast.22), calls=%async_computation | async-start | bytes 1048576 | tf_op jit(solution)/shard_map/all_to_all | solution.py:109
  14.9 0.0 copy-done.5
  14.9 0.6 %scatter_custom_fusion = s32[16]{0:T(128)S(1)} fusion(s32[16]{0:T(128)S(1)} %compare_select_fusion.1, s32[16]{0:T(128)S(1)} %iota.16, s32[]{:T(128)} %constant.45.clone.1), kind=kCustom, calls=%fused_computation.62 | custom fusion | bytes 68 | tf_op jit(solution)/shard_map/scatter | solution.py:113
  15.6 0.7 %gather_fusion = s32[32]{0:T(128)S(1)} fusion(s32[16]{0:T(128)S(1)} %scatter_custom_fusion, s32[1024]{0:T(1024)S(1)} %pad_clamp_fusion), kind=kCustom, calls=%fused_computation | custom fusion | bytes 384 | tf_op jit(solution)/shard_map/gather | solution.py:120
  16.3 0.0 copy-done
  16.3 0.7 %gather_fusion.1 = s32[32]{0:T(128)S(1)} fusion(s32[16]{0:T(128)S(1)} %copy-done, s32[1024]{0:T(1024)S(1)} %pad_clamp_fusion), kind=kCustom, calls=%fused_computation.1 | custom fusion | bytes 384 | tf_op jit(solution)/shard_map/gather | solution.py:122
  17.0 0.1 fusion.14
  17.1 12.3 %all-to-all-done = bf16[16,16,1024]{2,1,0:T(8,128)(2,1)S(1)} async-done(((bf16[16,16,1024]{2,1,0:T(8,128)(2,1)}), bf16[16,16,1024]{2,1,0:T(8,128)(2,1)S(1)}, u32[]{:S(2)}, u32[]{:S(2)}) %all-to-all-start) | async-done | bytes 524320 | tf_op jit(solution)/shard_map/all_to_all | solution.py:109
  29.4 0.1 copy.13
  29.5 0.3 %copy.11 = bf16[16,16,8,128]{3,0,2,1:T(8,128)(2,1)S(1)} copy(bf16[16,16,8,128]{3,2,1,0:T(8,128)(2,1)S(1)} %bitcast.47) | data formatting | bytes 1048576 | tf_op jit(solution)/shard_map/reshape | solution.py:117
  29.8 0.3 convolution_convert_fusion
  30.1 0.2 slice_negate_fusion
  30.3 0.4 %convolution_bitcast_fusion.1 = f32[1,64,32,32]{3,2,1,0:T(8,128)S(1)} fusion(bf16[64,32,128]{2,1,0:T(8,128)(2,1)S(1)} %convolution_convert_fusion), kind=kOutput, calls=%fused_computation.6 | convolution fusion | flops 16777216 | bytes 786432 | tf_op jit(solution)/shard_map/cak,cbk->cab/dot_general | solution.py:80
  30.7 0.5 %convolution_bitcast_fusion = f32[1,64,32,32]{3,2,1,0:T(8,128)S(1)} fusion(bf16[64,32,128]{2,1,0:T(8,128)(2,1)S(1)} %convolution_convert_fusion, bf16[64,32,64]{2,1,0:T(8,128)(2,1)S(1)} %get-tuple-element.25, bf16[64,32,64]{2,1,0:T(8,128)(2,1)S(1)} %get-tuple-element.24), kind=kOutput, calls=%fused_computation.5 | convolution fusion | flops 17825792 | bytes 1310720 | tf_op jit(solution)/shard_map/cak,cbk->cab/dot_general | solution.py:81
  31.2 0.3 fusion
  31.5 1.9 %copy.12 = bf16[2,64,32,32]{1,3,2,0:T(8,128)(2,1)} copy(bf16[2,64,32,32]{3,2,1,0:T(8,128)(2,1)S(1)} %fusion) | data formatting | bytes 524288 | tf_op jit(solution)/shard_map/layout_constraint | solution.py:128
  (12 shorter events, 0.3 us)
Async XLA Ops:
  0.0 16.3 %copy-start = (s32[16]{0:T(128)S(1)}, s32[16]{0:T(128)}, u32[]{:S(2)}) copy-start(s32[16]{0:T(128)} %param.11) | copy-start | bytes 196
  0.0 2.1 %copy-start.2 = (bf16[2,4,15360]{2,1,0:T(4,128)(2,1)S(1)}, bf16[2,4,15360]{2,1,0:T(4,128)(2,1)}, u32[]{:S(2)}) copy-start(bf16[2,4,15360]{2,1,0:T(4,128)(2,1)} %param.8) | copy-start | bytes 737284
  0.0 2.2 %copy-start.3 = (f32[16,1024]{1,0:T(8,128)S(1)}, f32[16,1024]{1,0:T(8,128)}, u32[]{:S(2)}) copy-start(f32[16,1024]{1,0:T(8,128)} %param.9) | copy-start | bytes 196612
  0.0 3.4 %copy-start.4 = (f32[4,256]{1,0:T(4,128)S(1)}, f32[4,256]{1,0:T(4,128)}, u32[]{:S(2)}) copy-start(f32[4,256]{1,0:T(4,128)} %constant.55.clone) | copy-start | bytes 12292
  0.0 3.5 %copy-start.1 = (f32[512,256]{1,0:T(8,128)S(1)}, f32[512,256]{1,0:T(8,128)}, u32[]{:S(2)}) copy-start(f32[512,256]{1,0:T(8,128)} %constant.56.clone) | copy-start | bytes 1572868
  1.6 2.1 %collective-permute-start = (bf16[2,2,32,1024]{3,2,1,0:T(8,128)(2,1)S(1)}, bf16[2,2,32,1024]{3,2,1,0:T(8,128)(2,1)S(1)}, u32[]{:S(2)}, u32[]{:S(2)}) collective-permute-start(bf16[2,2,32,1024]{3,2,1,0:T(8,128)(2,1)S(1)} %constant_dynamic-slice_fusion), channel_id=1, source_target_pairs={{0,1},{1,0},{2,3},{3,2},{4,5},{5,4},{6,7},{7,6},{8,9},{9,8},{10,11... | collective-permute-start | bytes 786440 | tf_op jit(solution)/shard_map/ppermute | solution.py:100
  6.6 8.3 %copy-start.5 = (s32[16]{0:T(128)S(1)}, s32[16]{0:T(128)}, u32[]{:S(2)}) copy-start(s32[16]{0:T(128)} %param.10) | copy-start | bytes 196
  7.9 21.5 %all-to-all-start = ((bf16[16,16,1024]{2,1,0:T(8,128)(2,1)}), bf16[16,16,1024]{2,1,0:T(8,128)(2,1)S(1)}, u32[]{:S(2)}, u32[]{:S(2)}) async-start(bf16[16,16,1024]{2,1,0:T(8,128)(2,1)} %bitcast.22), calls=%async_computation | async-start | bytes 1048576 | tf_op jit(solution)/shard_map/all_to_all | solution.py:109

commit v13 on v12

--- a/solution.py
+++ b/solution.py
@@ -97,7 +97,9 @@
     before = history.reshape(2, row_count, -1, fft_len)
     own = lax.dynamic_slice_in_dim(blocks, t * keep, keep, axis=1)
     other = lax.dynamic_slice_in_dim(blocks, (1 - t) * keep, keep, axis=1)
-    received = lax.ppermute(other, "tch", [(0, 1), (1, 0)])
+    received = jnp.concatenate(
+        [lax.ppermute(other[part : part + 1], "tch", [(0, 1), (1, 0)]) for part in range(2)], axis=0
+    )
     is_first = t == 0
     first = jnp.where(is_first, own, received)
     second = jnp.where(is_first, received, own)

time: 33.6 us -> 34 us (1.012)
  starting transfers between devices: 7.55 us -> 7.95 us
  transfers between devices with their start and end apart: 2 -> 3, of which waited for: 1 -> 1; matrix products, arithmetic and copies ran while one was open for 9% -> 9% of each run, Pallas kernels for 0% -> 0%
where the time goes in v13:
time: 34 us; the launch traced here: 33.8 us
  waiting for transfers between devices  12.3 us (36%)
  starting transfers between devices  7.95 us (23%)
  local copies, waits for them, and re-layouts  6.63 us (20%)
  other arithmetic  3.55 us (10%)
  matrix products  2.43 us (7%)
  between operations  0.95 us (3%)
    all_to_all x1, waiting for transfers between devices, local(): lax.all_to_all(spectra, ('blk', 'tch'), split_axis=0, concat_axis=0, tile...  12.3 us
    all_to_all x1, starting transfers between devices, local(): lax.all_to_all(spectra, ('blk', 'tch'), split_axis=0, concat_axis=0, tile...  7.34 us
    convert_element_type x1, other arithmetic, channelize(): x = filtered.astype(jnp.float32)  2.12 us
    another operation x1, local copies, waits for them, and re-layouts, local(): return with_layout_constraint(vis, Layout((0, 1, 2, 3)))  1.88 us
    reshape x1, local copies, waits for them, and re-layouts, local(): blocks = samples.reshape(2, row_count, -1, fft_len)  1.49 us
    dot_general x1, matrix products, channelize(): lax.dot_general(inner_matrix, rows.astype(jnp.bfloat16), (((0,), (1,)), (...  1.28 us
    gather x1, local copies, waits for them, and re-layouts, local(): select = select * station_ok[position // POLS].astype(turned.dtype)[:, None]  0.7 us
    gather x1, local copies, waits for them, and re-layouts, local(): wanted = slot_index[position // POLS] + position % POLS * station_count  0.7 us
  transfers between devices with their start and end apart: 3, of which 1 were waited for; matrix products, arithmetic and copies ran while one was open for 9% of the time, Pallas kernels for 0%

profile of v13, /device:TPU:0, one launch (start us, length us, event | category | flops | bytes accessed | tf_op | source)
XLA Modules:
  0.0 33.8 jit_solution(17561698366425532983)
XLA Ops:
  0.0 0.0 copy-start
  0.0 0.0 copy-start.1
  0.0 0.0 copy-start.3
  0.0 0.0 copy-start.4
  0.0 0.0 copy-start.2
  0.0 1.5 %reshape.130 = bf16[2,4,32,1024]{3,2,1,0:T(8,128)(2,1)S(1)} reshape(bf16[2,4,32768]{2,1,0:T(4,128)(2,1)} %param.7) | data formatting | bytes 1048576 | tf_op jit(solution)/shard_map/reshape | solution.py:96
  1.6 0.5 %collective-permute-start = (bf16[1,2,32,1024]{3,2,1,0:T(8,128)(2,1)S(1)}, bf16[1,2,32,1024]{3,2,1,0:T(8,128)(2,1)S(1)}, u32[]{:S(2)}, u32[]{:S(2)}) collective-permute-start(bf16[1,2,32,1024]{3,2,1,0:T(8,128)(2,1)S(1)} %get-tuple-element.27), channel_id=1, source_target_pairs={{0,1},{1,0},{2,3},{3,2},{4,5},{5,4},{6,7},{7,6},{8,9},{9,8},{10,11... | collective-permute-start | bytes 393224 | tf_op jit(solution)/shard_map/ppermute | solution.py:101
  2.1 0.1 collective-permute-start.1
  2.2 0.0 copy-done.3
  2.2 0.5 %slice.150 = f32[1,1]{1,0:T(1,128)} slice(f32[16,1024]{1,0:T(8,128)S(1)} %copy-done.3), slice={[0:1], [0:1]} | slice | bytes 8 | tf_op jit(solution)/shard_map/slice | solution.py:109
  3.4 0.0 copy-done.1
  3.4 0.0 copy-done.4
  3.5 0.1 fusion.15
  3.5 0.0 copy-done.2
  3.5 0.1 reshape.129
  3.7 0.0 collective-permute-done
  3.7 0.0 collective-permute-done.1
  3.8 0.2 pad_maximum_fusion.1
  4.0 2.1 %fusion.4 = f32[2,2,64,1024]{3,2,1,0:T(8,128)S(1)} fusion(bf16[2,2,32,1024]{3,2,1,0:T(8,128)(2,1)S(1)} %get-tuple-element.23, bf16[2,2,32,1024]{3,2,1,0:T(8,128)(2,1)S(1)} %get-tuple-element.22, f32[1024]{0:T(1024)S(1)} %bitcast.62, bf16[2,2,79,1024]{3,2,1,0:T(8,128)(2,1)S(1)} %pad_maximum_fusion.1, f32[1024]{0:T(1024)S(1)} %bitcast.63, ...), kind=kLoop, calls=%fused_computation.24 | loop fusion | flops 13631488 | bytes 9502720 | tf_op jit(solution)/shard_map/convert_element_type | solution.py:44
  6.1 0.1 fusion.7
  6.2 0.1 fusion.9
  6.3 0.2 fusion.22
  6.5 0.1 maximum_bitcast_fusion
  6.6 0.1 pad_maximum_fusion
  6.7 0.0 copy-start.5
  6.7 1.3 %convolution_convert_fusion.1 = bf16[256,1024]{1,0:T(8,128)(2,1)} fusion(bf16[512,256]{1,0:T(8,128)(2,1)S(1)} %add_convert_fusion.1, bf16[1024,512]{1,0:T(8,128)(2,1)S(1)} %bitcast.44), kind=kOutput, calls=%fused_computation.8 | convolution fusion | flops 268697600 | bytes 1835008 | tf_op jit(solution)/shard_map/dot_general | solution.py:64
  8.0 7.3 %all-to-all-start = ((bf16[16,16,1024]{2,1,0:T(8,128)(2,1)}), bf16[16,16,1024]{2,1,0:T(8,128)(2,1)S(1)}, u32[]{:S(2)}, u32[]{:S(2)}) async-start(bf16[16,16,1024]{2,1,0:T(8,128)(2,1)} %bitcast.22), calls=%async_computation | async-start | bytes 1048576 | tf_op jit(solution)/shard_map/all_to_all | solution.py:111
  15.3 0.0 copy-done.5
  15.4 0.6 %scatter_custom_fusion = s32[16]{0:T(128)S(1)} fusion(s32[16]{0:T(128)S(1)} %compare_select_fusion.1, s32[16]{0:T(128)S(1)} %iota.16, s32[]{:T(128)} %constant.45.clone.1), kind=kCustom, calls=%fused_computation.65 | custom fusion | bytes 68 | tf_op jit(solution)/shard_map/scatter | solution.py:115
  16.0 0.7 %gather_fusion = s32[32]{0:T(128)S(1)} fusion(s32[16]{0:T(128)S(1)} %scatter_custom_fusion, s32[1024]{0:T(1024)S(1)} %pad_clamp_fusion), kind=kCustom, calls=%fused_computation | custom fusion | bytes 384 | tf_op jit(solution)/shard_map/gather | solution.py:122
  16.7 0.0 copy-done
  16.7 0.7 %gather_fusion.1 = s32[32]{0:T(128)S(1)} fusion(s32[16]{0:T(128)S(1)} %copy-done, s32[1024]{0:T(1024)S(1)} %pad_clamp_fusion), kind=kCustom, calls=%fused_computation.1 | custom fusion | bytes 384 | tf_op jit(solution)/shard_map/gather | solution.py:124
  17.4 0.1 fusion.14
  17.5 12.3 %all-to-all-done = bf16[16,16,1024]{2,1,0:T(8,128)(2,1)S(1)} async-done(((bf16[16,16,1024]{2,1,0:T(8,128)(2,1)}), bf16[16,16,1024]{2,1,0:T(8,128)(2,1)S(1)}, u32[]{:S(2)}, u32[]{:S(2)}) %all-to-all-start) | async-done | bytes 524320 | tf_op jit(solution)/shard_map/all_to_all | solution.py:111
  29.8 0.1 copy.13
  29.9 0.3 %copy.11 = bf16[16,16,8,128]{3,0,2,1:T(8,128)(2,1)S(1)} copy(bf16[16,16,8,128]{3,2,1,0:T(8,128)(2,1)S(1)} %bitcast.47) | data formatting | bytes 1048576 | tf_op jit(solution)/shard_map/reshape | solution.py:119
  30.3 0.3 convolution_convert_fusion
  30.5 0.2 slice_negate_fusion
  30.8 0.4 %convolution_bitcast_fusion.1 = f32[1,64,32,32]{3,2,1,0:T(8,128)S(1)} fusion(bf16[64,32,128]{2,1,0:T(8,128)(2,1)S(1)} %convolution_convert_fusion), kind=kOutput, calls=%fused_computation.6 | convolution fusion | flops 16777216 | bytes 786432 | tf_op jit(solution)/shard_map/cak,cbk->cab/dot_general | solution.py:80
  31.2 0.5 %convolution_bitcast_fusion = f32[1,64,32,32]{3,2,1,0:T(8,128)S(1)} fusion(bf16[64,32,128]{2,1,0:T(8,128)(2,1)S(1)} %convolution_convert_fusion, bf16[64,32,64]{2,1,0:T(8,128)(2,1)S(1)} %get-tuple-element.25, bf16[64,32,64]{2,1,0:T(8,128)(2,1)S(1)} %get-tuple-element.24), kind=kOutput, calls=%fused_computation.5 | convolution fusion | flops 17825792 | bytes 1310720 | tf_op jit(solution)/shard_map/cak,cbk->cab/dot_general | solution.py:81
  31.6 0.3 fusion
  31.9 1.9 %copy.12 = bf16[2,64,32,32]{1,3,2,0:T(8,128)(2,1)} copy(bf16[2,64,32,32]{3,2,1,0:T(8,128)(2,1)S(1)} %fusion) | data formatting | bytes 524288 | tf_op jit(solution)/shard_map/layout_constraint | solution.py:130
  (14 shorter events, 0.3 us)
Async XLA Ops:
  0.0 16.7 %copy-start = (s32[16]{0:T(128)S(1)}, s32[16]{0:T(128)}, u32[]{:S(2)}) copy-start(s32[16]{0:T(128)} %param.11) | copy-start | bytes 196
  0.0 3.4 %copy-start.1 = (f32[512,256]{1,0:T(8,128)S(1)}, f32[512,256]{1,0:T(8,128)}, u32[]{:S(2)}) copy-start(f32[512,256]{1,0:T(8,128)} %constant.56.clone) | copy-start | bytes 1572868
  0.0 2.2 %copy-start.3 = (f32[16,1024]{1,0:T(8,128)S(1)}, f32[16,1024]{1,0:T(8,128)}, u32[]{:S(2)}) copy-start(f32[16,1024]{1,0:T(8,128)} %param.9) | copy-start | bytes 196612
  0.0 3.4 %copy-start.4 = (f32[4,256]{1,0:T(4,128)S(1)}, f32[4,256]{1,0:T(4,128)}, u32[]{:S(2)}) copy-start(f32[4,256]{1,0:T(4,128)} %constant.55.clone) | copy-start | bytes 12292
  0.0 3.5 %copy-start.2 = (bf16[2,4,15360]{2,1,0:T(4,128)(2,1)S(1)}, bf16[2,4,15360]{2,1,0:T(4,128)(2,1)}, u32[]{:S(2)}) copy-start(bf16[2,4,15360]{2,1,0:T(4,128)(2,1)} %param.8) | copy-start | bytes 737284
  1.6 2.2 %collective-permute-start = (bf16[1,2,32,1024]{3,2,1,0:T(8,128)(2,1)S(1)}, bf16[1,2,32,1024]{3,2,1,0:T(8,128)(2,1)S(1)}, u32[]{:S(2)}, u32[]{:S(2)}) collective-permute-start(bf16[1,2,32,1024]{3,2,1,0:T(8,128)(2,1)S(1)} %get-tuple-element.27), channel_id=1, source_target_pairs={{0,1},{1,0},{2,3},{3,2},{4,5},{5,4},{6,7},{7,6},{8,9},{9,8},{10,11... | collective-permute-start | bytes 393224 | tf_op jit(solution)/shard_map/ppermute | solution.py:101
  2.1 1.7 %collective-permute-start.1 = (bf16[1,2,32,1024]{3,2,1,0:T(8,128)(2,1)S(1)}, bf16[1,2,32,1024]{3,2,1,0:T(8,128)(2,1)S(1)}, u32[]{:S(2)}, u32[]{:S(2)}) collective-permute-start(bf16[1,2,32,1024]{3,2,1,0:T(8,128)(2,1)S(1)} %get-tuple-element.26), channel_id=1, source_target_pairs={{0,1},{1,0},{2,3},{3,2},{4,5},{5,4},{6,7},{7,6},{8,9},{9,8},{10,11... | collective-permute-start | bytes 393224 | tf_op jit(solution)/shard_map/ppermute | solution.py:101
  6.7 8.6 %copy-start.5 = (s32[16]{0:T(128)S(1)}, s32[16]{0:T(128)}, u32[]{:S(2)}) copy-start(s32[16]{0:T(128)} %param.10) | copy-start | bytes 196
  8.0 21.8 %all-to-all-start = ((bf16[16,16,1024]{2,1,0:T(8,128)(2,1)}), bf16[16,16,1024]{2,1,0:T(8,128)(2,1)S(1)}, u32[]{:S(2)}, u32[]{:S(2)}) async-start(bf16[16,16,1024]{2,1,0:T(8,128)(2,1)} %bitcast.22), calls=%async_computation | async-start | bytes 1048576 | tf_op jit(solution)/shard_map/all_to_all | solution.py:111

commit v14 on v12

--- a/solution.py
+++ b/solution.py
@@ -52,7 +52,7 @@
     yi = jnp.stack([ai + bi, ci - dr, ai - bi, ci + dr], axis=0)
     angle = jnp.asarray(2.0 * np.pi * np.outer(np.arange(RADIX), np.arange(inner)) / fft_len, jnp.float32) + origin
     tr, ti, inner_matrix = lax.optimization_barrier(
-        (jnp.cos(angle), -jnp.sin(angle), (jnp.asarray(inner_matrix) + origin).astype(jnp.bfloat16))
+        (jnp.cos(angle), -jnp.sin(angle), jnp.asarray(inner_matrix, jnp.bfloat16) + origin.astype(jnp.bfloat16))
     )
     tr = tr[:, None, None, :]
     ti = ti[:, None, None, :]

time: 33.6 us -> 33.6 us (level)
  no operation moved by 1% of the time
where the time goes in v14:
time: 33.6 us; the launch traced here: 33.3 us
  waiting for transfers between devices  12.3 us (37%)
  starting transfers between devices  7.55 us (22%)
  local copies, waits for them, and re-layouts  6.6 us (20%)
  other arithmetic  3.53 us (11%)
  matrix products  2.43 us (7%)
  between operations  0.93 us (3%)
    all_to_all x1, waiting for transfers between devices, local(): lax.all_to_all(spectra, ('blk', 'tch'), split_axis=0, concat_axis=0, tile...  12.3 us
    all_to_all x1, starting transfers between devices, local(): lax.all_to_all(spectra, ('blk', 'tch'), split_axis=0, concat_axis=0, tile...  7.02 us
    convert_element_type x1, other arithmetic, channelize(): x = filtered.astype(jnp.float32)  2.12 us
    another operation x1, local copies, waits for them, and re-layouts, local(): return with_layout_constraint(vis, Layout((0, 1, 2, 3)))  1.88 us
    reshape x1, local copies, waits for them, and re-layouts, local(): blocks = samples.reshape(2, row_count, -1, fft_len)  1.48 us
    dot_general x1, matrix products, channelize(): lax.dot_general(inner_matrix, rows.astype(jnp.bfloat16), (((0,), (1,)), (...  1.28 us
    gather x1, local copies, waits for them, and re-layouts, local(): select = select * station_ok[position // POLS].astype(turned.dtype)[:, None]  0.7 us
    gather x1, local copies, waits for them, and re-layouts, local(): wanted = slot_index[position // POLS] + position % POLS * station_count  0.7 us
  transfers between devices with their start and end apart: 2, of which 1 were waited for; matrix products, arithmetic and copies ran while one was open for 9% of the time, Pallas kernels for 0%

profile of v14, /device:TPU:0, one launch (start us, length us, event | category | flops | bytes accessed | tf_op | source)
XLA Modules:
  0.0 33.3 jit_solution(5129044393643032772)
XLA Ops:
  0.0 0.0 copy-start
  0.0 0.0 copy-start.2
  0.0 0.0 copy-start.3
  0.0 0.0 copy-start.4
  0.0 0.0 copy-start.1
  0.0 1.5 %reshape.130 = bf16[2,4,32,1024]{3,2,1,0:T(8,128)(2,1)S(1)} reshape(bf16[2,4,32768]{2,1,0:T(4,128)(2,1)} %param.7) | data formatting | bytes 1048576 | tf_op jit(solution)/shard_map/reshape | solution.py:96
  1.5 0.5 %collective-permute-start = (bf16[2,2,32,1024]{3,2,1,0:T(8,128)(2,1)S(1)}, bf16[2,2,32,1024]{3,2,1,0:T(8,128)(2,1)S(1)}, u32[]{:S(2)}, u32[]{:S(2)}) collective-permute-start(bf16[2,2,32,1024]{3,2,1,0:T(8,128)(2,1)S(1)} %constant_dynamic-slice_fusion), channel_id=1, source_target_pairs={{0,1},{1,0},{2,3},{3,2},{4,5},{5,4},{6,7},{7,6},{8,9},{9,8},{10,11... | collective-permute-start | bytes 786440 | tf_op jit(solution)/shard_map/ppermute | solution.py:100
  2.1 0.0 copy-done.2
  2.1 0.1 reshape.129
  2.2 0.0 copy-done.3
  2.2 0.5 %slice.144 = f32[1,1]{1,0:T(1,128)} slice(f32[16,1024]{1,0:T(8,128)S(1)} %copy-done.3), slice={[0:1], [0:1]} | slice | bytes 8 | tf_op jit(solution)/shard_map/slice | solution.py:107
  3.4 0.0 copy-done.4
  3.4 0.1 fusion.15
  3.5 0.0 copy-done.1
  3.6 0.0 collective-permute-done
  3.7 0.2 pad_maximum_fusion.1
  3.8 2.1 %fusion.4 = f32[2,2,64,1024]{3,2,1,0:T(8,128)S(1)} fusion(bf16[2,2,32,1024]{3,2,1,0:T(8,128)(2,1)S(1)} %get-tuple-element.23, bf16[2,2,32,1024]{3,2,1,0:T(8,128)(2,1)S(1)} %get-tuple-element.22, f32[1024]{0:T(1024)S(1)} %bitcast.62, bf16[2,2,79,1024]{3,2,1,0:T(8,128)(2,1)S(1)} %pad_maximum_fusion.1, f32[1024]{0:T(1024)S(1)} %bitcast.63, ...), kind=kLoop, calls=%fused_computation.23 | loop fusion | flops 13631488 | bytes 9502720 | tf_op jit(solution)/shard_map/convert_element_type | solution.py:44
  6.0 0.1 fusion.7
  6.0 0.1 fusion.9
  6.1 0.2 fusion.22
  6.3 0.1 maximum_bitcast_fusion
  6.4 0.1 pad_maximum_fusion
  6.5 0.0 copy-start.5
  6.6 1.3 %convolution_convert_fusion.1 = bf16[256,1024]{1,0:T(8,128)(2,1)} fusion(bf16[512,256]{1,0:T(8,128)(2,1)S(1)} %broadcast_add_fusion, bf16[1024,512]{1,0:T(8,128)(2,1)S(1)} %bitcast.44), kind=kOutput, calls=%fused_computation.8 | convolution fusion | flops 268697600 | bytes 1835008 | tf_op jit(solution)/shard_map/dot_general | solution.py:64
  7.8 7.0 %all-to-all-start = ((bf16[16,16,1024]{2,1,0:T(8,128)(2,1)}), bf16[16,16,1024]{2,1,0:T(8,128)(2,1)S(1)}, u32[]{:S(2)}, u32[]{:S(2)}) async-start(bf16[16,16,1024]{2,1,0:T(8,128)(2,1)} %bitcast.22), calls=%async_computation | async-start | bytes 1048576 | tf_op jit(solution)/shard_map/all_to_all | solution.py:109
  14.9 0.0 copy-done.5
  14.9 0.6 %scatter_custom_fusion = s32[16]{0:T(128)S(1)} fusion(s32[16]{0:T(128)S(1)} %compare_select_fusion.1, s32[16]{0:T(128)S(1)} %iota.16, s32[]{:T(128)} %constant.45.clone.1), kind=kCustom, calls=%fused_computation.62 | custom fusion | bytes 68 | tf_op jit(solution)/shard_map/scatter | solution.py:113
  15.6 0.7 %gather_fusion = s32[32]{0:T(128)S(1)} fusion(s32[16]{0:T(128)S(1)} %scatter_custom_fusion, s32[1024]{0:T(1024)S(1)} %pad_clamp_fusion), kind=kCustom, calls=%fused_computation | custom fusion | bytes 384 | tf_op jit(solution)/shard_map/gather | solution.py:120
  16.3 0.0 copy-done
  16.3 0.7 %gather_fusion.1 = s32[32]{0:T(128)S(1)} fusion(s32[16]{0:T(128)S(1)} %copy-done, s32[1024]{0:T(1024)S(1)} %pad_clamp_fusion), kind=kCustom, calls=%fused_computation.1 | custom fusion | bytes 384 | tf_op jit(solution)/shard_map/gather | solution.py:122
  17.0 0.1 fusion.14
  17.1 12.3 %all-to-all-done = bf16[16,16,1024]{2,1,0:T(8,128)(2,1)S(1)} async-done(((bf16[16,16,1024]{2,1,0:T(8,128)(2,1)}), bf16[16,16,1024]{2,1,0:T(8,128)(2,1)S(1)}, u32[]{:S(2)}, u32[]{:S(2)}) %all-to-all-start) | async-done | bytes 524320 | tf_op jit(solution)/shard_map/all_to_all | solution.py:109
  29.3 0.1 copy.13
  29.4 0.3 %copy.11 = bf16[16,16,8,128]{3,0,2,1:T(8,128)(2,1)S(1)} copy(bf16[16,16,8,128]{3,2,1,0:T(8,128)(2,1)S(1)} %bitcast.47) | data formatting | bytes 1048576 | tf_op jit(solution)/shard_map/reshape | solution.py:117
  29.8 0.3 convolution_convert_fusion
  30.1 0.2 slice_negate_fusion
  30.3 0.4 %convolution_bitcast_fusion.1 = f32[1,64,32,32]{3,2,1,0:T(8,128)S(1)} fusion(bf16[64,32,128]{2,1,0:T(8,128)(2,1)S(1)} %convolution_convert_fusion), kind=kOutput, calls=%fused_computation.6 | convolution fusion | flops 16777216 | bytes 786432 | tf_op jit(solution)/shard_map/cak,cbk->cab/dot_general | solution.py:80
  30.7 0.5 %convolution_bitcast_fusion = f32[1,64,32,32]{3,2,1,0:T(8,128)S(1)} fusion(bf16[64,32,128]{2,1,0:T(8,128)(2,1)S(1)} %convolution_convert_fusion, bf16[64,32,64]{2,1,0:T(8,128)(2,1)S(1)} %get-tuple-element.25, bf16[64,32,64]{2,1,0:T(8,128)(2,1)S(1)} %get-tuple-element.24), kind=kOutput, calls=%fused_computation.5 | convolution fusion | flops 17825792 | bytes 1310720 | tf_op jit(solution)/shard_map/cak,cbk->cab/dot_general | solution.py:81
  31.2 0.3 fusion
  31.4 1.9 %copy.12 = bf16[2,64,32,32]{1,3,2,0:T(8,128)(2,1)} copy(bf16[2,64,32,32]{3,2,1,0:T(8,128)(2,1)S(1)} %fusion) | data formatting | bytes 524288 | tf_op jit(solution)/shard_map/layout_constraint | solution.py:128
  (12 shorter events, 0.2 us)
Async XLA Ops:
  0.0 16.3 %copy-start = (s32[16]{0:T(128)S(1)}, s32[16]{0:T(128)}, u32[]{:S(2)}) copy-start(s32[16]{0:T(128)} %param.11) | copy-start | bytes 196
  0.0 2.1 %copy-start.2 = (bf16[2,4,15360]{2,1,0:T(4,128)(2,1)S(1)}, bf16[2,4,15360]{2,1,0:T(4,128)(2,1)}, u32[]{:S(2)}) copy-start(bf16[2,4,15360]{2,1,0:T(4,128)(2,1)} %param.8) | copy-start | bytes 737284
  0.0 2.2 %copy-start.3 = (f32[16,1024]{1,0:T(8,128)S(1)}, f32[16,1024]{1,0:T(8,128)}, u32[]{:S(2)}) copy-start(f32[16,1024]{1,0:T(8,128)} %param.9) | copy-start | bytes 196612
  0.0 3.4 %copy-start.4 = (f32[4,256]{1,0:T(4,128)S(1)}, f32[4,256]{1,0:T(4,128)}, u32[]{:S(2)}) copy-start(f32[4,256]{1,0:T(4,128)} %constant.55.clone) | copy-start | bytes 12292
  0.0 3.5 %copy-start.1 = (bf16[512,256]{1,0:T(8,128)(2,1)S(1)}, bf16[512,256]{1,0:T(8,128)(2,1)}, u32[]{:S(2)}) copy-start(bf16[512,256]{1,0:T(8,128)(2,1)} %constant.56.clone) | copy-start | bytes 786436
  1.5 2.1 %collective-permute-start = (bf16[2,2,32,1024]{3,2,1,0:T(8,128)(2,1)S(1)}, bf16[2,2,32,1024]{3,2,1,0:T(8,128)(2,1)S(1)}, u32[]{:S(2)}, u32[]{:S(2)}) collective-permute-start(bf16[2,2,32,1024]{3,2,1,0:T(8,128)(2,1)S(1)} %constant_dynamic-slice_fusion), channel_id=1, source_target_pairs={{0,1},{1,0},{2,3},{3,2},{4,5},{5,4},{6,7},{7,6},{8,9},{9,8},{10,11... | collective-permute-start | bytes 786440 | tf_op jit(solution)/shard_map/ppermute | solution.py:100
  6.5 8.3 %copy-start.5 = (s32[16]{0:T(128)S(1)}, s32[16]{0:T(128)}, u32[]{:S(2)}) copy-start(s32[16]{0:T(128)} %param.10) | copy-start | bytes 196
  7.8 21.5 %all-to-all-start = ((bf16[16,16,1024]{2,1,0:T(8,128)(2,1)}), bf16[16,16,1024]{2,1,0:T(8,128)(2,1)S(1)}, u32[]{:S(2)}, u32[]{:S(2)}) async-start(bf16[16,16,1024]{2,1,0:T(8,128)(2,1)} %bitcast.22), calls=%async_computation | async-start | bytes 1048576 | tf_op jit(solution)/shard_map/all_to_all | solution.py:109

commit v15 on v14

--- a/solution.py
+++ b/solution.py
@@ -70,15 +70,20 @@
     return product.astype(jnp.bfloat16)
 
 
-def rotate_parts(ordered):
-    half_cols = ordered.shape[2] // 2
-    return jnp.concatenate([-ordered[:, :, half_cols:], ordered[:, :, :half_cols]], axis=2)
-
-
-def correlate_full(ordered, inverse_count):
-    rotated = rotate_parts(ordered)
+def correlate_full(ordered, inverse_count, half_count):
+    width = ordered.shape[2]
+    half = width // 2
+    turn = np.zeros((width, width), np.float32)
+    turn[half + np.arange(half), np.arange(half)] = -1.0
+    turn[np.arange(half), half + np.arange(half)] = 1.0
+    rotated = jnp.einsum(
+        "cak,kj->caj", ordered, jnp.asarray(turn, ordered.dtype), preferred_element_type=jnp.float32
+    ).astype(ordered.dtype)
     real_vis = jnp.einsum("cak,cbk->cab", ordered, ordered, preferred_element_type=jnp.float32)
     imag_vis = jnp.einsum("cak,cbk->cab", ordered, rotated, preferred_element_type=jnp.float32)
+    chan_count = ordered.shape[0] // half_count
+    real_vis = real_vis.reshape(half_count, chan_count, *real_vis.shape[1:]).sum(axis=0)
+    imag_vis = imag_vis.reshape(half_count, chan_count, *imag_vis.shape[1:]).sum(axis=0)
     return (jnp.stack([real_vis, imag_vis], axis=0) * inverse_count).astype(jnp.bfloat16)
 
 
@@ -93,18 +98,13 @@
     kl_count = inner // dest_count
     keep = row_count // half_count
     t = lax.axis_index("tch")
-    blocks = samples.reshape(2, row_count, -1, fft_len)
-    before = history.reshape(2, row_count, -1, fft_len)
-    own = lax.dynamic_slice_in_dim(blocks, t * keep, keep, axis=1)
-    other = lax.dynamic_slice_in_dim(blocks, (1 - t) * keep, keep, axis=1)
-    received = lax.ppermute(other, "tch", [(0, 1), (1, 0)])
-    is_first = t == 0
-    first = jnp.where(is_first, own, received)
-    second = jnp.where(is_first, received, own)
-    earlier = lax.dynamic_slice_in_dim(before, t * keep, keep, axis=1)
-    extended = jnp.concatenate([earlier, first, second], axis=2).reshape(2, keep, -1)
-    spec_total = (extended.shape[2] - (tap_count - 1) * fft_len) // fft_len
-    spectra = channelize(filter_bank(extended, coefficients, spec_total), 0.0 * coefficients[0, 0])
+    tail = samples[:, :, samples.shape[2] - (tap_count - 1) * fft_len :]
+    from_previous = lax.ppermute(tail, "tch", [(0, 1)])
+    earlier = jnp.where(t == 0, history, from_previous)
+    extended = jnp.concatenate([earlier, samples], axis=2)
+    spec_local = (extended.shape[2] - (tap_count - 1) * fft_len) // fft_len
+    spec_total = spec_local * half_count
+    spectra = channelize(filter_bank(extended, coefficients, spec_local), 0.0 * coefficients[0, 0])
     spectra = spectra.reshape(dest_count, kl_count, -1)
     turned = lax.all_to_all(spectra, ("blk", "tch"), split_axis=0, concat_axis=0, tiled=True)
     slot_index = (
@@ -114,17 +114,19 @@
     )
     chan_count = kl_count * RADIX
     input_count = station_count * POLS
-    by_source = turned.reshape(station_count, kl_count, RADIX * POLS, 2 * spec_total)
-    by_source = jnp.transpose(by_source, (1, 2, 0, 3)).reshape(chan_count, input_count, 2 * spec_total)
+    by_source = turned.reshape(block_count, half_count, kl_count, RADIX, row_count, 2 * spec_local)
+    by_source = jnp.transpose(by_source, (1, 2, 3, 0, 4, 5)).reshape(
+        half_count * chan_count, input_count, 2 * spec_local
+    )
     position = jnp.arange(input_count, dtype=jnp.int32)
-    wanted = slot_index[position // POLS] + (position % POLS) * station_count
+    wanted = slot_index[position // POLS] * POLS + position % POLS
     select = (wanted[:, None] == position[None, :]).astype(turned.dtype)
     select = select * station_ok[position // POLS].astype(turned.dtype)[:, None]
-    select = jnp.broadcast_to(select, (chan_count, input_count, input_count))
+    select = jnp.broadcast_to(select, (half_count * chan_count, input_count, input_count))
     ordered = jnp.einsum(
         "cij,cjk->cik", select, by_source, preferred_element_type=jnp.float32
     ).astype(turned.dtype)
-    vis = correlate_full(ordered, 1.0 / spec_total)
+    vis = correlate_full(ordered, 1.0 / spec_total, half_count)
     return with_layout_constraint(vis, Layout((0, 1, 2, 3)))
 
 

time: 33.6 us -> 53.4 us (1.59)
  other arithmetic: 3.53 us -> 10.8 us
  local copies, waits for them, and re-layouts: 6.6 us -> 12.7 us
  matrix products: 2.43 us -> 6.93 us
  starting transfers between devices: 7.55 us -> 9.11 us
    reduce_sum x0 -> x2, other arithmetic: none -> 3.36 us  [the longest x1 2 us: correlate_full(): imag_vis.reshape(half_count, chan_count, *imag_vis.shape[1:]).sum(axis=0)]
    dot_general x0 -> x1, local copies, waits for them, and re-layouts: none -> 3.34 us  [correlate_full(): jnp.einsum('cak,kj->caj', ordered, jnp.asarray(turn, ordered.dtype), pref...]
    dot_general x1, matrix products: 0.47 us -> 3.23 us  [correlate_full(): jnp.einsum('cak,cbk->cab', ordered, rotated, preferred_element_type=jnp.f...]
    ppermute x1, starting transfers between devices: 0.53 us -> 2.37 us  [local(): from_previous = lax.ppermute(tail, 'tch', [(0, 1)])]
    dot_general x0 -> x1, matrix products: none -> 1.33 us  [correlate_full(): jnp.einsum('cak,kj->caj', ordered, jnp.asarray(turn, ordered.dtype), pref...]
    convert_element_type x1, other arithmetic: 0.27 us -> 1.55 us  [correlate_full(): (jnp.stack([real_vis, imag_vis], axis=0) * inverse_count).astype(jnp.bflo...]
    slice x1, local copies, waits for them, and re-layouts: 0.05 us -> 1.3 us  [filter_bank(): weights[tap_index]]
    slice x0 -> x1, local copies, waits for them, and re-layouts: none -> 1.1 us  [local(): tail = samples[:, :, samples.shape[2] - (tap_count - 1) * fft_len:]]
  transfers between devices with their start and end apart: 2 -> 2, of which waited for: 1 -> 1; matrix products, arithmetic and copies ran while one was open for 9% -> 12% of each run, Pallas kernels for 0% -> 0%
where the time goes in v15:
time: 53.4 us; the launch traced here: 52.7 us
  local copies, waits for them, and re-layouts  12.7 us (24%)
  waiting for transfers between devices  12.3 us (23%)
  other arithmetic  10.8 us (20%)
  starting transfers between devices  9.11 us (17%)
  matrix products  6.93 us (13%)
  between operations  0.88 us (2%)
    all_to_all x1, waiting for transfers between devices, local(): lax.all_to_all(spectra, ('blk', 'tch'), split_axis=0, concat_axis=0, tile...  12.3 us
    all_to_all x1, starting transfers between devices, local(): lax.all_to_all(spectra, ('blk', 'tch'), split_axis=0, concat_axis=0, tile...  6.74 us
    dot_general x1, local copies, waits for them, and re-layouts, correlate_full(): jnp.einsum('cak,kj->caj', ordered, jnp.asarray(turn, ordered.dtype), pref...  3.34 us
    dot_general x1, matrix products, correlate_full(): jnp.einsum('cak,cbk->cab', ordered, rotated, preferred_element_type=jnp.f...  3.23 us
    ppermute x1, starting transfers between devices, local(): from_previous = lax.ppermute(tail, 'tch', [(0, 1)])  2.37 us
    convert_element_type x1, other arithmetic, channelize(): x = filtered.astype(jnp.float32)  2.21 us
    reduce_sum x1, other arithmetic, correlate_full(): imag_vis.reshape(half_count, chan_count, *imag_vis.shape[1:]).sum(axis=0)  2 us
    another operation x1, local copies, waits for them, and re-layouts, local(): return with_layout_constraint(vis, Layout((0, 1, 2, 3)))  1.9 us
  transfers between devices with their start and end apart: 2, of which 1 were waited for; matrix products, arithmetic and copies ran while one was open for 12% of the time, Pallas kernels for 0%

profile of v15, /device:TPU:0, one launch (start us, length us, event | category | flops | bytes accessed | tf_op | source)
XLA Modules:
  0.0 52.7 jit_solution(13615780831030851781)
XLA Ops:
  0.0 0.0 copy-start
  0.0 0.0 copy-start.1
  0.0 1.1 %slice.144 = bf16[2,4,15360]{2,1,0:T(4,128)(2,1)S(1)} slice(bf16[2,4,32768]{2,1,0:T(4,128)(2,1)} %param.8), slice={[0:2], [0:4], [17408:32768]} | slice | bytes 491520 | tf_op jit(solution)/shard_map/slice | solution.py:101
  1.1 2.4 %collective-permute-start = (bf16[2,4,15360]{2,1,0:T(4,128)(2,1)S(1)}, bf16[2,4,15360]{2,1,0:T(4,128)(2,1)S(1)}, u32[]{:S(2)}, u32[]{:S(2)}) collective-permute-start(bf16[2,4,15360]{2,1,0:T(4,128)(2,1)S(1)} %slice.144), channel_id=1, source_target_pairs={{0,1},{2,3},{4,5},{6,7},{8,9},{10,11},{12,13},{14,15},{16,17},{18,... | collective-permute-start | bytes 737288 | tf_op jit(solution)/shard_map/ppermute | solution.py:102
  3.5 1.2 %slice.142 = f32[1,1]{1,0:T(1,128)} slice(f32[16,1024]{1,0:T(8,128)} %param.10), slice={[0:1], [0:1]} | slice | bytes 8 | tf_op jit(solution)/shard_map/slice | solution.py:107
  5.3 1.0 %broadcast_add_fusion = bf16[512,256]{1,0:T(8,128)(2,1)S(1)} fusion(bf16[512,256]{1,0:T(8,128)(2,1)} %constant.57.clone, bf16[]{:T(256)S(6)} %convert_element_type.82), kind=kLoop, calls=%fused_computation.24 | loop fusion | flops 131072 | bytes 524290 | tf_op jit(solution)/shard_map/add | solution.py:55
  6.3 0.7 %fusion.16 = (f32[4,256]{1,0:T(4,128)S(1)}, f32[4,256]{1,0:T(4,128)S(1)}) fusion(f32[4,256]{1,0:T(4,128)} %constant.56.clone, f32[]{:T(128)} %bitcast.1), kind=kLoop, calls=%fused_computation.45 | loop fusion | flops 2048 | bytes 12292 | tf_op jit(solution)/shard_map/neg | solution.py:55
  7.1 1.3 %fusion.22 = (f32[1,1024]{1,0:T(1,128)S(1)}, f32[1,1024]{1,0:T(1,128)S(1)}, f32[1,1024]{1,0:T(1,128)S(1)}, f32[1,1024]{1,0:T(1,128)S(1)}, f32[1,1024]{1,0:T(1,12...) fusion(f32[16,1024]{1,0:T(8,128)} %param.10), kind=kLoop, calls=%fused_computation.59 | loop fusion | bytes 131072 | tf_op jit(solution)/shard_map/slice | solution.py:34
  8.4 0.0 collective-permute-done
  8.4 1.0 %broadcast_select_fusion = bf16[1,8,15360]{2,1,0:T(8,128)(2,1)S(1)} fusion(bf16[1,8,15360]{2,1,0:T(8,128)(2,1)} %bitcast.52, bf16[1,8,15360]{2,1,0:T(8,128)(2,1)S(1)} %bitcast.53, pred[]{:T(512)S(6)} %eq.21), kind=kLoop, calls=%fused_computation.23 | loop fusion | flops 122880 | bytes 737281 | tf_op jit(solution)/shard_map/jit(_where)/select_n | solution.py:103
  9.4 0.0 copy-done.1
  9.4 0.3 pad_maximum_fusion.1
  9.7 0.5 reshape.132
  10.2 2.2 %fusion.6 = f32[2,4,32,1024]{3,2,1,0:T(8,128)S(1)} fusion(bf16[2,4,47,1024]{3,2,1,0:T(8,128)(2,1)S(1)} %reshape.132, f32[1024]{0:T(1024)S(1)} %bitcast.68, f32[1024]{0:T(1024)S(1)} %bitcast.69, f32[1024]{0:T(1024)S(1)} %bitcast.55, f32[1024]{0:T(1024)S(1)} %bitcast.56, f32[1024]{0:T(1024)S(1)} %bitcast.57, f32[1024]{0:T(1024)S(1)} %bitcast.58, ...), kind=kLoop, calls=%fused_computation.22 | loop fusion | flops 12845056 | bytes 9502720 | tf_op jit(solution)/shard_map/convert_element_type | solution.py:44
  12.5 0.1 fusion.8
  12.5 0.1 fusion.10
  12.6 0.2 fusion.21
  12.8 0.1 maximum_bitcast_fusion
  12.9 0.1 pad_maximum_fusion
  13.0 0.0 copy-start.3
  13.1 0.1 copy.11
  13.2 1.3 %convolution_convert_fusion.1 = bf16[256,1024]{1,0:T(8,128)(2,1)} fusion(bf16[512,256]{1,0:T(8,128)(2,1)S(1)} %broadcast_add_fusion, bf16[1024,512]{1,0:T(8,128)(2,1)S(1)} %bitcast.49), kind=kOutput, calls=%fused_computation.6 | convolution fusion | flops 268697600 | bytes 1835008 | tf_op jit(solution)/shard_map/dot_general | solution.py:64
  14.5 6.7 %all-to-all-start = ((bf16[16,16,1024]{2,1,0:T(8,128)(2,1)}), bf16[16,16,1024]{2,1,0:T(8,128)(2,1)S(1)}, u32[]{:S(2)}, u32[]{:S(2)}) async-start(bf16[16,16,1024]{2,1,0:T(8,128)(2,1)} %bitcast.21), calls=%async_computation | async-start | bytes 1048576 | tf_op jit(solution)/shard_map/all_to_all | solution.py:109
  21.2 0.0 copy-done.3
  21.2 0.6 %scatter_custom_fusion = s32[16]{0:T(128)S(1)} fusion(s32[16]{0:T(128)S(1)} %compare_select_fusion.1, s32[16]{0:T(128)S(1)} %iota.16, s32[]{:T(128)} %constant.46.clone.1), kind=kCustom, calls=%fused_computation.56 | custom fusion | bytes 68 | tf_op jit(solution)/shard_map/scatter | solution.py:113
  21.9 0.7 %gather_fusion = s32[32]{0:T(128)S(1)} fusion(s32[16]{0:T(128)S(1)} %scatter_custom_fusion, s32[1024]{0:T(1024)S(1)} %pad_clamp_fusion), kind=kCustom, calls=%fused_computation | custom fusion | bytes 384 | tf_op jit(solution)/shard_map/gather | solution.py:122
  22.6 0.0 copy-done
  22.6 0.7 %gather_fusion.1 = s32[32]{0:T(128)S(1)} fusion(s32[16]{0:T(128)S(1)} %copy-done, s32[1024]{0:T(1024)S(1)} %pad_clamp_fusion), kind=kCustom, calls=%fused_computation.1 | custom fusion | bytes 384 | tf_op jit(solution)/shard_map/gather | solution.py:124
  23.3 0.1 fusion.15
  23.4 12.3 %all-to-all-done = bf16[16,16,1024]{2,1,0:T(8,128)(2,1)S(1)} async-done(((bf16[16,16,1024]{2,1,0:T(8,128)(2,1)}), bf16[16,16,1024]{2,1,0:T(8,128)(2,1)S(1)}, u32[]{:S(2)}, u32[]{:S(2)}) %all-to-all-start) | async-done | bytes 524320 | tf_op jit(solution)/shard_map/all_to_all | solution.py:109
  35.7 0.7 %reshape.134 = bf16[8,2,16,4,4,64]{5,4,3,2,1,0:T(4,128)(2,1)S(1)} reshape(bf16[16,16,1024]{2,1,0:T(8,128)(2,1)S(1)} %all-to-all-done) | data formatting | bytes 1048576 | tf_op jit(solution)/shard_map/reshape | solution.py:117
  36.3 0.5 %copy.12 = bf16[8,2,16,4,4,64]{5,4,0,3,2,1:T(4,128)(2,1)S(1)} copy(bf16[8,2,16,4,4,64]{5,4,3,2,1,0:T(4,128)(2,1)S(1)} %reshape.134) | data formatting | bytes 1048576 | tf_op jit(solution)/shard_map/reshape | solution.py:117
  36.9 0.4 convolution_convert_fusion
  37.3 0.0 copy-start.2
  37.3 0.7 %fusion.23 = f32[128,32,32]{2,1,0:T(8,128)S(1)} fusion(bf16[128,32,64]{2,1,0:T(8,128)(2,1)S(1)} %convolution_convert_fusion), kind=kOutput, calls=%fused_computation.60 | convolution fusion | flops 16777216 | bytes 1048576 | tf_op jit(solution)/shard_map/cak,cbk->cab/dot_general | solution.py:82
  38.0 0.1 copy-done.2
  38.0 1.3 %fusion.1 = bf16[128,32,64]{0,2,1:T(8,128)(2,1)} fusion(bf16[64,64,1]{1,0,2:T(8,128)(2,1)S(1)} %copy-done.2, bf16[128,32,64]{2,1,0:T(8,128)(2,1)S(1)} %convolution_convert_fusion), kind=kOutput, calls=%fused_computation.8 | convolution fusion | flops 33554432 | bytes 1056768 | tf_op jit(solution)/shard_map/cak,kj->caj/dot_general | solution.py:79
  39.4 3.3 %copy.15 = bf16[128,32,64]{2,1,0:T(8,128)(2,1)} copy(bf16[128,32,64]{0,2,1:T(8,128)(2,1)} %fusion.1) | data formatting | bytes 1048576 | tf_op jit(solution)/shard_map/cak,kj->caj/dot_general | solution.py:79
  42.7 3.2 %fusion.24 = f32[128,32,32]{2,1,0:T(8,128)} fusion(bf16[128,32,64]{2,1,0:T(8,128)(2,1)S(1)} %convolution_convert_fusion, bf16[128,32,64]{2,1,0:T(8,128)(2,1)} %copy.15), kind=kOutput, calls=%fused_computation.61 | convolution fusion | flops 16777216 | bytes 1572864 | tf_op jit(solution)/shard_map/cak,cbk->cab/dot_general | solution.py:83
  45.9 2.0 %reduce_sum.19 = f32[64,32,32]{2,1,0:T(8,128)S(1)} reduce(f32[2,64,32,32]{3,2,1,0:T(8,128)} %bitcast.46, f32[]{:T(128)} %constant.54.clone.1), dimensions={0}, to_apply=%region_2.3 | reduce | flops 65536 | bytes 786436 | tf_op jit(solution)/shard_map/reduce_sum | solution.py:86
  47.9 1.4 %reduce_sum.18 = f32[64,32,32]{2,1,0:T(8,128)} reduce(f32[2,64,32,32]{3,2,1,0:T(8,128)S(1)} %bitcast.45, f32[]{:T(128)} %constant.54.clone.1), dimensions={0}, to_apply=%region_1.2 | reduce | flops 65536 | bytes 786436 | tf_op jit(solution)/shard_map/reduce_sum | solution.py:85
  49.3 1.5 %fusion = bf16[2,64,32,32]{3,2,1,0:T(8,128)(2,1)S(1)} fusion(f32[1,64,32,32]{3,2,1,0:T(8,128)S(1)} %bitcast.47, f32[1,64,32,32]{3,2,1,0:T(8,128)} %bitcast.48), kind=kLoop, calls=%fused_computation.4 | loop fusion | flops 393216 | bytes 786432 | tf_op jit(solution)/shard_map/convert_element_type | solution.py:87
  50.8 1.9 %copy.13 = bf16[2,64,32,32]{1,3,2,0:T(8,128)(2,1)} copy(bf16[2,64,32,32]{3,2,1,0:T(8,128)(2,1)S(1)} %fusion) | data formatting | bytes 524288 | tf_op jit(solution)/shard_map/layout_constraint | solution.py:130
  (7 shorter events, 0.1 us)
Async XLA Ops:
  0.0 22.6 %copy-start = (s32[16]{0:T(128)S(1)}, s32[16]{0:T(128)}, u32[]{:S(2)}) copy-start(s32[16]{0:T(128)} %param.12) | copy-start | bytes 196
  0.0 9.4 %copy-start.1 = (bf16[2,4,32768]{2,1,0:T(4,128)(2,1)S(1)}, bf16[2,4,32768]{2,1,0:T(4,128)(2,1)}, u32[]{:S(2)}) copy-start(bf16[2,4,32768]{2,1,0:T(4,128)(2,1)} %param.8) | copy-start | bytes 1572868
  1.1 7.3 %collective-permute-start = (bf16[2,4,15360]{2,1,0:T(4,128)(2,1)S(1)}, bf16[2,4,15360]{2,1,0:T(4,128)(2,1)S(1)}, u32[]{:S(2)}, u32[]{:S(2)}) collective-permute-start(bf16[2,4,15360]{2,1,0:T(4,128)(2,1)S(1)} %slice.144), channel_id=1, source_target_pairs={{0,1},{2,3},{4,5},{6,7},{8,9},{10,11},{12,13},{14,15},{16,17},{18,... | collective-permute-start | bytes 737288 | tf_op jit(solution)/shard_map/ppermute | solution.py:102
  13.0 8.2 %copy-start.3 = (s32[16]{0:T(128)S(1)}, s32[16]{0:T(128)}, u32[]{:S(2)}) copy-start(s32[16]{0:T(128)} %param.11) | copy-start | bytes 196
  14.5 21.2 %all-to-all-start = ((bf16[16,16,1024]{2,1,0:T(8,128)(2,1)}), bf16[16,16,1024]{2,1,0:T(8,128)(2,1)S(1)}, u32[]{:S(2)}, u32[]{:S(2)}) async-start(bf16[16,16,1024]{2,1,0:T(8,128)(2,1)} %bitcast.21), calls=%async_computation | async-start | bytes 1048576 | tf_op jit(solution)/shard_map/all_to_all | solution.py:109
  37.3 0.7 %copy-start.2 = (bf16[64,64,1]{1,0,2:T(8,128)(2,1)S(1)}, bf16[64,64,1]{1,0,2:T(8,128)(2,1)}, u32[]{:S(2)}) copy-start(bf16[64,64,1]{1,0,2:T(8,128)(2,1)} %constant.61) | copy-start | bytes 24580

commit v16 on v14

--- a/solution.py
+++ b/solution.py
@@ -76,9 +76,12 @@
 
 
 def correlate_full(ordered, inverse_count):
-    rotated = rotate_parts(ordered)
+    half_cols = ordered.shape[2] // 2
     real_vis = jnp.einsum("cak,cbk->cab", ordered, ordered, preferred_element_type=jnp.float32)
-    imag_vis = jnp.einsum("cak,cbk->cab", ordered, rotated, preferred_element_type=jnp.float32)
+    cross = jnp.einsum(
+        "cak,cbk->cab", ordered[:, :, half_cols:], ordered[:, :, :half_cols], preferred_element_type=jnp.float32
+    )
+    imag_vis = cross - jnp.swapaxes(cross, 1, 2)
     return (jnp.stack([real_vis, imag_vis], axis=0) * inverse_count).astype(jnp.bfloat16)
 
 

time: 33.6 us -> 33.9 us (level)
  local copies, waits for them, and re-layouts: 6.6 us -> 6.94 us
where the time goes in v16:
time: 33.9 us; the launch traced here: 33.6 us
  waiting for transfers between devices  12.3 us (36%)
  starting transfers between devices  7.54 us (22%)
  local copies, waits for them, and re-layouts  6.94 us (20%)
  other arithmetic  3.51 us (10%)
  matrix products  2.41 us (7%)
  between operations  0.95 us (3%)
    all_to_all x1, waiting for transfers between devices, local(): lax.all_to_all(spectra, ('blk', 'tch'), split_axis=0, concat_axis=0, tile...  12.3 us
    all_to_all x1, starting transfers between devices, local(): lax.all_to_all(spectra, ('blk', 'tch'), split_axis=0, concat_axis=0, tile...  7.02 us
    convert_element_type x1, other arithmetic, channelize(): x = filtered.astype(jnp.float32)  2.12 us
    another operation x1, local copies, waits for them, and re-layouts, local(): return with_layout_constraint(vis, Layout((0, 1, 2, 3)))  1.88 us
    reshape x1, local copies, waits for them, and re-layouts, local(): blocks = samples.reshape(2, row_count, -1, fft_len)  1.48 us
    dot_general x1, matrix products, channelize(): lax.dot_general(inner_matrix, rows.astype(jnp.bfloat16), (((0,), (1,)), (...  1.28 us
    gather x1, local copies, waits for them, and re-layouts, local(): select = select * station_ok[position // POLS].astype(turned.dtype)[:, None]  0.7 us
    gather x1, local copies, waits for them, and re-layouts, local(): wanted = slot_index[position // POLS] + position % POLS * station_count  0.7 us
  transfers between devices with their start and end apart: 2, of which 1 were waited for; matrix products, arithmetic and copies ran while one was open for 9% of the time, Pallas kernels for 0%

profile of v16, /device:TPU:0, one launch (start us, length us, event | category | flops | bytes accessed | tf_op | source)
XLA Modules:
  0.0 33.6 jit_solution(10660996614203904381)
XLA Ops:
  0.0 0.0 copy-start
  0.0 0.0 copy-start.4
  0.0 0.0 copy-start.3
  0.0 0.0 copy-start.2
  0.0 0.0 copy-start.1
  0.0 1.5 %reshape.130 = bf16[2,4,32,1024]{3,2,1,0:T(8,128)(2,1)S(1)} reshape(bf16[2,4,32768]{2,1,0:T(4,128)(2,1)} %param.7) | data formatting | bytes 1048576 | tf_op jit(solution)/shard_map/reshape | solution.py:99
  1.5 0.5 %collective-permute-start = (bf16[2,2,32,1024]{3,2,1,0:T(8,128)(2,1)S(1)}, bf16[2,2,32,1024]{3,2,1,0:T(8,128)(2,1)S(1)}, u32[]{:S(2)}, u32[]{:S(2)}) collective-permute-start(bf16[2,2,32,1024]{3,2,1,0:T(8,128)(2,1)S(1)} %constant_dynamic-slice_fusion), channel_id=1, source_target_pairs={{0,1},{1,0},{2,3},{3,2},{4,5},{5,4},{6,7},{7,6},{8,9},{9,8},{10,11... | collective-permute-start | bytes 786440 | tf_op jit(solution)/shard_map/ppermute | solution.py:103
  2.1 0.0 copy-done.3
  2.1 0.5 %slice.144 = f32[1,1]{1,0:T(1,128)} slice(f32[16,1024]{1,0:T(8,128)S(1)} %copy-done.3), slice={[0:1], [0:1]} | slice | bytes 8 | tf_op jit(solution)/shard_map/slice | solution.py:110
  3.2 0.0 copy-done.4
  3.3 0.1 fusion.16
  3.3 0.0 copy-done.2
  3.3 0.1 reshape.129
  3.5 0.0 copy-done.1
  3.6 0.0 collective-permute-done
  3.7 0.2 pad_maximum_fusion.1
  3.8 2.1 %fusion.5 = f32[2,2,64,1024]{3,2,1,0:T(8,128)S(1)} fusion(bf16[2,2,32,1024]{3,2,1,0:T(8,128)(2,1)S(1)} %get-tuple-element.23, bf16[2,2,32,1024]{3,2,1,0:T(8,128)(2,1)S(1)} %get-tuple-element.22, f32[1024]{0:T(1024)S(1)} %bitcast.66, bf16[2,2,79,1024]{3,2,1,0:T(8,128)(2,1)S(1)} %pad_maximum_fusion.1, f32[1024]{0:T(1024)S(1)} %bitcast.67, ...), kind=kLoop, calls=%fused_computation.23 | loop fusion | flops 13631488 | bytes 9502720 | tf_op jit(solution)/shard_map/convert_element_type | solution.py:44
  6.0 0.1 fusion.8
  6.0 0.1 fusion.10
  6.1 0.2 fusion.22
  6.3 0.1 maximum_bitcast_fusion
  6.4 0.1 pad_maximum_fusion
  6.5 0.0 copy-start.5
  6.6 1.3 %convolution_convert_fusion.1 = bf16[256,1024]{1,0:T(8,128)(2,1)} fusion(bf16[512,256]{1,0:T(8,128)(2,1)S(1)} %broadcast_add_fusion, bf16[1024,512]{1,0:T(8,128)(2,1)S(1)} %bitcast.48), kind=kOutput, calls=%fused_computation.7 | convolution fusion | flops 268697600 | bytes 1835008 | tf_op jit(solution)/shard_map/dot_general | solution.py:64
  7.8 7.0 %all-to-all-start = ((bf16[16,16,1024]{2,1,0:T(8,128)(2,1)}), bf16[16,16,1024]{2,1,0:T(8,128)(2,1)S(1)}, u32[]{:S(2)}, u32[]{:S(2)}) async-start(bf16[16,16,1024]{2,1,0:T(8,128)(2,1)} %bitcast.22), calls=%async_computation | async-start | bytes 1048576 | tf_op jit(solution)/shard_map/all_to_all | solution.py:112
  14.9 0.0 copy-done.5
  14.9 0.6 %scatter_custom_fusion = s32[16]{0:T(128)S(1)} fusion(s32[16]{0:T(128)S(1)} %compare_select_fusion.1, s32[16]{0:T(128)S(1)} %iota.16, s32[]{:T(128)} %constant.45.clone.1), kind=kCustom, calls=%fused_computation.62 | custom fusion | bytes 68 | tf_op jit(solution)/shard_map/scatter | solution.py:116
  15.6 0.7 %gather_fusion = s32[32]{0:T(128)S(1)} fusion(s32[16]{0:T(128)S(1)} %scatter_custom_fusion, s32[1024]{0:T(1024)S(1)} %pad_clamp_fusion), kind=kCustom, calls=%fused_computation | custom fusion | bytes 384 | tf_op jit(solution)/shard_map/gather | solution.py:123
  16.3 0.0 copy-done
  16.3 0.7 %gather_fusion.1 = s32[32]{0:T(128)S(1)} fusion(s32[16]{0:T(128)S(1)} %copy-done, s32[1024]{0:T(1024)S(1)} %pad_clamp_fusion), kind=kCustom, calls=%fused_computation.1 | custom fusion | bytes 384 | tf_op jit(solution)/shard_map/gather | solution.py:125
  17.0 0.1 fusion.15
  17.1 12.3 %all-to-all-done = bf16[16,16,1024]{2,1,0:T(8,128)(2,1)S(1)} async-done(((bf16[16,16,1024]{2,1,0:T(8,128)(2,1)}), bf16[16,16,1024]{2,1,0:T(8,128)(2,1)S(1)}, u32[]{:S(2)}, u32[]{:S(2)}) %all-to-all-start) | async-done | bytes 524320 | tf_op jit(solution)/shard_map/all_to_all | solution.py:112
  29.3 0.1 copy.15
  29.4 0.3 %copy.12 = bf16[16,16,8,128]{3,0,2,1:T(8,128)(2,1)S(1)} copy(bf16[16,16,8,128]{3,2,1,0:T(8,128)(2,1)S(1)} %bitcast.51) | data formatting | bytes 1048576 | tf_op jit(solution)/shard_map/reshape | solution.py:120
  29.8 0.3 convolution_convert_fusion
  30.1 0.4 %fusion.2 = f32[64,32,32]{2,1,0:T(8,128)S(1)} fusion(bf16[64,32,128]{2,1,0:T(8,128)(2,1)S(1)} %convolution_convert_fusion), kind=kOutput, calls=%fused_computation.13 | convolution fusion | flops 8388608 | bytes 1310720 | tf_op jit(solution)/shard_map/cak,cbk->cab/dot_general | solution.py:81
  30.5 0.4 %convolution_bitcast_fusion = f32[1,64,32,32]{3,2,1,0:T(8,128)S(1)} fusion(bf16[64,32,128]{2,1,0:T(8,128)(2,1)S(1)} %convolution_convert_fusion), kind=kOutput, calls=%fused_computation.5 | convolution fusion | flops 16777216 | bytes 786432 | tf_op jit(solution)/shard_map/cak,cbk->cab/dot_general | solution.py:80
  30.9 0.3 %copy.13 = f32[64,32,32]{1,2,0:T(8,128)S(1)} copy(f32[64,32,32]{2,1,0:T(8,128)S(1)} %fusion.2) | data formatting | bytes 524288 | tf_op jit(solution)/shard_map/cak,cbk->cab/dot_general | solution.py:81
  31.3 0.2 fusion.1
  31.5 0.3 fusion
  31.8 1.9 %copy.14 = bf16[2,64,32,32]{1,3,2,0:T(8,128)(2,1)} copy(bf16[2,64,32,32]{3,2,1,0:T(8,128)(2,1)S(1)} %fusion) | data formatting | bytes 524288 | tf_op jit(solution)/shard_map/layout_constraint | solution.py:131
  (12 shorter events, 0.2 us)
Async XLA Ops:
  0.0 16.3 %copy-start = (s32[16]{0:T(128)S(1)}, s32[16]{0:T(128)}, u32[]{:S(2)}) copy-start(s32[16]{0:T(128)} %param.11) | copy-start | bytes 196
  0.0 3.2 %copy-start.4 = (f32[4,256]{1,0:T(4,128)S(1)}, f32[4,256]{1,0:T(4,128)}, u32[]{:S(2)}) copy-start(f32[4,256]{1,0:T(4,128)} %constant.55.clone) | copy-start | bytes 12292
  0.0 2.1 %copy-start.3 = (f32[16,1024]{1,0:T(8,128)S(1)}, f32[16,1024]{1,0:T(8,128)}, u32[]{:S(2)}) copy-start(f32[16,1024]{1,0:T(8,128)} %param.9) | copy-start | bytes 196612
  0.0 3.3 %copy-start.2 = (bf16[2,4,15360]{2,1,0:T(4,128)(2,1)S(1)}, bf16[2,4,15360]{2,1,0:T(4,128)(2,1)}, u32[]{:S(2)}) copy-start(bf16[2,4,15360]{2,1,0:T(4,128)(2,1)} %param.8) | copy-start | bytes 737284
  0.0 3.5 %copy-start.1 = (bf16[512,256]{1,0:T(8,128)(2,1)S(1)}, bf16[512,256]{1,0:T(8,128)(2,1)}, u32[]{:S(2)}) copy-start(bf16[512,256]{1,0:T(8,128)(2,1)} %constant.56.clone) | copy-start | bytes 786436
  1.5 2.1 %collective-permute-start = (bf16[2,2,32,1024]{3,2,1,0:T(8,128)(2,1)S(1)}, bf16[2,2,32,1024]{3,2,1,0:T(8,128)(2,1)S(1)}, u32[]{:S(2)}, u32[]{:S(2)}) collective-permute-start(bf16[2,2,32,1024]{3,2,1,0:T(8,128)(2,1)S(1)} %constant_dynamic-slice_fusion), channel_id=1, source_target_pairs={{0,1},{1,0},{2,3},{3,2},{4,5},{5,4},{6,7},{7,6},{8,9},{9,8},{10,11... | collective-permute-start | bytes 786440 | tf_op jit(solution)/shard_map/ppermute | solution.py:103
  6.5 8.3 %copy-start.5 = (s32[16]{0:T(128)S(1)}, s32[16]{0:T(128)}, u32[]{:S(2)}) copy-start(s32[16]{0:T(128)} %param.10) | copy-start | bytes 196
  7.8 21.5 %all-to-all-start = ((bf16[16,16,1024]{2,1,0:T(8,128)(2,1)}), bf16[16,16,1024]{2,1,0:T(8,128)(2,1)S(1)}, u32[]{:S(2)}, u32[]{:S(2)}) async-start(bf16[16,16,1024]{2,1,0:T(8,128)(2,1)} %bitcast.22), calls=%async_computation | async-start | bytes 1048576 | tf_op jit(solution)/shard_map/all_to_all | solution.py:112

commit v17 on v14

--- a/solution.py
+++ b/solution.py
@@ -93,8 +93,8 @@
     kl_count = inner // dest_count
     keep = row_count // half_count
     t = lax.axis_index("tch")
-    blocks = samples.reshape(2, row_count, -1, fft_len)
-    before = history.reshape(2, row_count, -1, fft_len)
+    blocks = samples.astype(jnp.float32).reshape(2, row_count, -1, fft_len)
+    before = history.astype(jnp.float32).reshape(2, row_count, -1, fft_len)
     own = lax.dynamic_slice_in_dim(blocks, t * keep, keep, axis=1)
     other = lax.dynamic_slice_in_dim(blocks, (1 - t) * keep, keep, axis=1)
     received = lax.ppermute(other, "tch", [(0, 1), (1, 0)])

time: 33.6 us -> 33.7 us (level)
  no operation moved by 1% of the time
where the time goes in v17:
time: 33.7 us; the launch traced here: 33.5 us
  waiting for transfers between devices  12.3 us (36%)
  starting transfers between devices  7.8 us (23%)
  local copies, waits for them, and re-layouts  6.49 us (19%)
  other arithmetic  3.51 us (10%)
  matrix products  2.43 us (7%)
  between operations  0.93 us (3%)
    all_to_all x1, waiting for transfers between devices, local(): lax.all_to_all(spectra, ('blk', 'tch'), split_axis=0, concat_axis=0, tile...  12.3 us
    all_to_all x1, starting transfers between devices, local(): lax.all_to_all(spectra, ('blk', 'tch'), split_axis=0, concat_axis=0, tile...  7.28 us
    convert_element_type x1, other arithmetic, channelize(): x = filtered.astype(jnp.float32)  2.02 us
    another operation x1, local copies, waits for them, and re-layouts, local(): return with_layout_constraint(vis, Layout((0, 1, 2, 3)))  1.88 us
    reshape x1, local copies, waits for them, and re-layouts, local(): blocks = samples.astype(jnp.float32).reshape(2, row_count, -1, fft_len)  1.35 us
    dot_general x1, matrix products, channelize(): lax.dot_general(inner_matrix, rows.astype(jnp.bfloat16), (((0,), (1,)), (...  1.28 us
    gather x1, local copies, waits for them, and re-layouts, local(): select = select * station_ok[position // POLS].astype(turned.dtype)[:, None]  0.7 us
    gather x1, local copies, waits for them, and re-layouts, local(): wanted = slot_index[position // POLS] + position % POLS * station_count  0.7 us
  transfers between devices with their start and end apart: 2, of which 1 were waited for; matrix products, arithmetic and copies ran while one was open for 9% of the time, Pallas kernels for 0%

profile of v17, /device:TPU:0, one launch (start us, length us, event | category | flops | bytes accessed | tf_op | source)
XLA Modules:
  0.0 33.5 jit_solution(17890026983075128815)
XLA Ops:
  0.0 0.0 copy-start
  0.0 0.0 copy-start.2
  0.0 0.0 copy-start.3
  0.0 1.4 %reshape.145 = f32[2,4,32,1024]{3,2,1,0:T(8,128)S(1)} reshape(bf16[2,4,32768]{2,1,0:T(4,128)(2,1)} %param.7) | data formatting | bytes 1572864 | tf_op jit(solution)/shard_map/reshape | solution.py:96
  1.4 0.0 copy-start.1
  1.4 0.0 copy-start.4
  1.4 0.5 %collective-permute-start = (f32[2,2,32,1024]{3,2,1,0:T(8,128)S(1)}, f32[2,2,32,1024]{3,2,1,0:T(8,128)S(1)}, u32[]{:S(2)}, u32[]{:S(2)}) collective-permute-start(f32[2,2,32,1024]{3,2,1,0:T(8,128)S(1)} %constant_dynamic-slice_fusion), channel_id=1, source_target_pairs={{0,1},{1,0},{2,3},{3,2},{4,5},{5,4},{6,7},{7,6},{8,9},{9,8},{10,11... | collective-permute-start | bytes 1572872 | tf_op jit(solution)/shard_map/ppermute | solution.py:100
  2.0 0.0 copy-done.2
  2.0 0.1 reshape.143
  2.1 0.0 copy-done.3
  2.1 0.5 %slice.144 = f32[1,1]{1,0:T(1,128)} slice(f32[16,1024]{1,0:T(8,128)S(1)} %copy-done.3), slice={[0:1], [0:1]} | slice | bytes 8 | tf_op jit(solution)/shard_map/slice | solution.py:107
  3.3 0.0 copy-done.1
  3.3 0.0 copy-done.4
  3.3 0.1 fusion.31
  3.5 0.0 collective-permute-done
  3.5 0.1 dynamic-slice_select_fusion.1
  3.6 0.2 pad_maximum_fusion
  3.8 2.0 %fusion.20 = f32[2,2,64,1024]{3,2,1,0:T(8,128)S(1)} fusion(f32[2,2,32,1024]{3,2,1,0:T(8,128)S(1)} %get-tuple-element.14, f32[2,2,32,1024]{3,2,1,0:T(8,128)S(1)} %get-tuple-element.13, f32[1024]{0:T(1024)S(1)} %bitcast.62, f32[2,2,79,1024]{3,2,1,0:T(8,128)S(1)} %pad_maximum_fusion, f32[1024]{0:T(1024)S(1)} %bitcast.63, f32[1024]{0:T(1024)S(1)} %bitcast.49, ...), kind=kLoop, calls=%fused_computation.54 | loop fusion | flops 8912896 | bytes 17891328 | tf_op jit(solution)/shard_map/convert_element_type | solution.py:44
  5.8 0.1 fusion.23
  5.9 0.1 fusion.25
  6.0 0.2 fusion.38
  6.2 0.1 maximum_bitcast_fusion
  6.3 0.1 pad_maximum_fusion.1
  6.4 0.0 copy-start.5
  6.4 1.3 %convolution_convert_fusion.1 = bf16[256,1024]{1,0:T(8,128)(2,1)} fusion(bf16[512,256]{1,0:T(8,128)(2,1)S(1)} %broadcast_add_fusion, bf16[1024,512]{1,0:T(8,128)(2,1)S(1)} %bitcast.44), kind=kOutput, calls=%fused_computation.9 | convolution fusion | flops 268697600 | bytes 1835008 | tf_op jit(solution)/shard_map/dot_general | solution.py:64
  7.7 7.3 %all-to-all-start = ((bf16[16,16,1024]{2,1,0:T(8,128)(2,1)}), bf16[16,16,1024]{2,1,0:T(8,128)(2,1)S(1)}, u32[]{:S(2)}, u32[]{:S(2)}) async-start(bf16[16,16,1024]{2,1,0:T(8,128)(2,1)} %bitcast.22), calls=%async_computation | async-start | bytes 1048576 | tf_op jit(solution)/shard_map/all_to_all | solution.py:109
  15.0 0.0 copy-done.5
  15.0 0.6 %scatter_custom_fusion = s32[16]{0:T(128)S(1)} fusion(s32[16]{0:T(128)S(1)} %compare_select_fusion.1, s32[16]{0:T(128)S(1)} %iota.16, s32[]{:T(128)} %constant.45.clone.1), kind=kCustom, calls=%fused_computation.93 | custom fusion | bytes 68 | tf_op jit(solution)/shard_map/scatter | solution.py:113
  15.7 0.7 %gather_fusion = s32[32]{0:T(128)S(1)} fusion(s32[16]{0:T(128)S(1)} %scatter_custom_fusion, s32[1024]{0:T(1024)S(1)} %pad_clamp_fusion), kind=kCustom, calls=%fused_computation | custom fusion | bytes 384 | tf_op jit(solution)/shard_map/gather | solution.py:120
  16.4 0.0 copy-done
  16.4 0.7 %gather_fusion.1 = s32[32]{0:T(128)S(1)} fusion(s32[16]{0:T(128)S(1)} %copy-done, s32[1024]{0:T(1024)S(1)} %pad_clamp_fusion), kind=kCustom, calls=%fused_computation.1 | custom fusion | bytes 384 | tf_op jit(solution)/shard_map/gather | solution.py:122
  17.1 0.1 fusion.30
  17.2 12.3 %all-to-all-done = bf16[16,16,1024]{2,1,0:T(8,128)(2,1)S(1)} async-done(((bf16[16,16,1024]{2,1,0:T(8,128)(2,1)}), bf16[16,16,1024]{2,1,0:T(8,128)(2,1)S(1)}, u32[]{:S(2)}, u32[]{:S(2)}) %all-to-all-start) | async-done | bytes 524320 | tf_op jit(solution)/shard_map/all_to_all | solution.py:109
  29.5 0.1 copy.13
  29.6 0.3 %copy.11 = bf16[16,16,8,128]{3,0,2,1:T(8,128)(2,1)S(1)} copy(bf16[16,16,8,128]{3,2,1,0:T(8,128)(2,1)S(1)} %bitcast.47) | data formatting | bytes 1048576 | tf_op jit(solution)/shard_map/reshape | solution.py:117
  29.9 0.3 convolution_convert_fusion
  30.2 0.2 slice_negate_fusion
  30.4 0.4 %convolution_bitcast_fusion.1 = f32[1,64,32,32]{3,2,1,0:T(8,128)S(1)} fusion(bf16[64,32,128]{2,1,0:T(8,128)(2,1)S(1)} %convolution_convert_fusion), kind=kOutput, calls=%fused_computation.6 | convolution fusion | flops 16777216 | bytes 786432 | tf_op jit(solution)/shard_map/cak,cbk->cab/dot_general | solution.py:80
  30.8 0.5 %convolution_bitcast_fusion = f32[1,64,32,32]{3,2,1,0:T(8,128)S(1)} fusion(bf16[64,32,128]{2,1,0:T(8,128)(2,1)S(1)} %convolution_convert_fusion, bf16[64,32,64]{2,1,0:T(8,128)(2,1)S(1)} %get-tuple-element.25, bf16[64,32,64]{2,1,0:T(8,128)(2,1)S(1)} %get-tuple-element.24), kind=kOutput, calls=%fused_computation.5 | convolution fusion | flops 17825792 | bytes 1310720 | tf_op jit(solution)/shard_map/cak,cbk->cab/dot_general | solution.py:81
  31.3 0.3 fusion
  31.6 1.9 %copy.12 = bf16[2,64,32,32]{1,3,2,0:T(8,128)(2,1)} copy(bf16[2,64,32,32]{3,2,1,0:T(8,128)(2,1)S(1)} %fusion) | data formatting | bytes 524288 | tf_op jit(solution)/shard_map/layout_constraint | solution.py:128
  (11 shorter events, 0.2 us)
Async XLA Ops:
  0.0 16.4 %copy-start = (s32[16]{0:T(128)S(1)}, s32[16]{0:T(128)}, u32[]{:S(2)}) copy-start(s32[16]{0:T(128)} %param.11) | copy-start | bytes 196
  0.0 2.0 %copy-start.2 = (bf16[2,4,15360]{2,1,0:T(4,128)(2,1)S(1)}, bf16[2,4,15360]{2,1,0:T(4,128)(2,1)}, u32[]{:S(2)}) copy-start(bf16[2,4,15360]{2,1,0:T(4,128)(2,1)} %param.8) | copy-start | bytes 737284
  0.0 2.1 %copy-start.3 = (f32[16,1024]{1,0:T(8,128)S(1)}, f32[16,1024]{1,0:T(8,128)}, u32[]{:S(2)}) copy-start(f32[16,1024]{1,0:T(8,128)} %param.9) | copy-start | bytes 196612
  1.4 1.9 %copy-start.1 = (bf16[512,256]{1,0:T(8,128)(2,1)S(1)}, bf16[512,256]{1,0:T(8,128)(2,1)}, u32[]{:S(2)}) copy-start(bf16[512,256]{1,0:T(8,128)(2,1)} %constant.56.clone) | copy-start | bytes 786436
  1.4 2.0 %copy-start.4 = (f32[4,256]{1,0:T(4,128)S(1)}, f32[4,256]{1,0:T(4,128)}, u32[]{:S(2)}) copy-start(f32[4,256]{1,0:T(4,128)} %constant.55.clone) | copy-start | bytes 12292
  1.4 2.1 %collective-permute-start = (f32[2,2,32,1024]{3,2,1,0:T(8,128)S(1)}, f32[2,2,32,1024]{3,2,1,0:T(8,128)S(1)}, u32[]{:S(2)}, u32[]{:S(2)}) collective-permute-start(f32[2,2,32,1024]{3,2,1,0:T(8,128)S(1)} %constant_dynamic-slice_fusion), channel_id=1, source_target_pairs={{0,1},{1,0},{2,3},{3,2},{4,5},{5,4},{6,7},{7,6},{8,9},{9,8},{10,11... | collective-permute-start | bytes 1572872 | tf_op jit(solution)/shard_map/ppermute | solution.py:100
  6.4 8.6 %copy-start.5 = (s32[16]{0:T(128)S(1)}, s32[16]{0:T(128)}, u32[]{:S(2)}) copy-start(s32[16]{0:T(128)} %param.10) | copy-start | bytes 196
  7.7 21.8 %all-to-all-start = ((bf16[16,16,1024]{2,1,0:T(8,128)(2,1)}), bf16[16,16,1024]{2,1,0:T(8,128)(2,1)S(1)}, u32[]{:S(2)}, u32[]{:S(2)}) async-start(bf16[16,16,1024]{2,1,0:T(8,128)(2,1)} %bitcast.22), calls=%async_computation | async-start | bytes 1048576 | tf_op jit(solution)/shard_map/all_to_all | solution.py:109

commit v18 on v17

--- a/solution.py
+++ b/solution.py
@@ -93,11 +93,12 @@
     kl_count = inner // dest_count
     keep = row_count // half_count
     t = lax.axis_index("tch")
-    blocks = samples.astype(jnp.float32).reshape(2, row_count, -1, fft_len)
+    other = lax.dynamic_slice_in_dim(samples, (1 - t) * keep, keep, axis=1)
+    other = other.astype(jnp.float32).reshape(2, keep, -1, fft_len)
+    received = lax.ppermute(other, "tch", [(0, 1), (1, 0)])
+    own = lax.dynamic_slice_in_dim(samples, t * keep, keep, axis=1)
+    own = own.astype(jnp.float32).reshape(2, keep, -1, fft_len)
     before = history.astype(jnp.float32).reshape(2, row_count, -1, fft_len)
-    own = lax.dynamic_slice_in_dim(blocks, t * keep, keep, axis=1)
-    other = lax.dynamic_slice_in_dim(blocks, (1 - t) * keep, keep, axis=1)
-    received = lax.ppermute(other, "tch", [(0, 1), (1, 0)])
     is_first = t == 0
     first = jnp.where(is_first, own, received)
     second = jnp.where(is_first, received, own)

time: 33.7 us -> 34.7 us (1.030)
  other arithmetic: 3.51 us -> 5.22 us
  local copies, waits for them, and re-layouts: 6.49 us -> 6 us
    reshape x0 -> x1, other arithmetic: none -> 1.72 us  [local(): own = own.astype(jnp.float32).reshape(2, keep, -1, fft_len)]
    reshape x1 -> x2, local copies, waits for them, and re-layouts: 1.35 us -> 0.9 us  [the longest x1 0.45 us: local(): other = other.astype(jnp.float32).reshape(2, keep, -1, fft_len)]
  transfers between devices with their start and end apart: 2 -> 2, of which waited for: 1 -> 1; matrix products, arithmetic and copies ran while one was open for 9% -> 10% of each run, Pallas kernels for 0% -> 0%
where the time goes in v18:
time: 34.7 us; the launch traced here: 34.4 us
  waiting for transfers between devices  12.3 us (35%)
  starting transfers between devices  7.54 us (22%)
  local copies, waits for them, and re-layouts  6 us (17%)
  other arithmetic  5.22 us (15%)
  matrix products  2.42 us (7%)
  between operations  0.96 us (3%)
    all_to_all x1, waiting for transfers between devices, local(): lax.all_to_all(spectra, ('blk', 'tch'), split_axis=0, concat_axis=0, tile...  12.3 us
    all_to_all x1, starting transfers between devices, local(): lax.all_to_all(spectra, ('blk', 'tch'), split_axis=0, concat_axis=0, tile...  7.02 us
    convert_element_type x1, other arithmetic, channelize(): x = filtered.astype(jnp.float32)  2.02 us
    another operation x1, local copies, waits for them, and re-layouts, local(): return with_layout_constraint(vis, Layout((0, 1, 2, 3)))  1.88 us
    reshape x1, other arithmetic, local(): own = own.astype(jnp.float32).reshape(2, keep, -1, fft_len)  1.72 us
    dot_general x1, matrix products, channelize(): lax.dot_general(inner_matrix, rows.astype(jnp.bfloat16), (((0,), (1,)), (...  1.28 us
    gather x1, local copies, waits for them, and re-layouts, local(): select = select * station_ok[position // POLS].astype(turned.dtype)[:, None]  0.7 us
    gather x1, local copies, waits for them, and re-layouts, local(): wanted = slot_index[position // POLS] + position % POLS * station_count  0.7 us
  transfers between devices with their start and end apart: 2, of which 1 were waited for; matrix products, arithmetic and copies ran while one was open for 10% of the time, Pallas kernels for 0%

profile of v18, /device:TPU:0, one launch (start us, length us, event | category | flops | bytes accessed | tf_op | source)
XLA Modules:
  0.0 34.4 jit_solution(185412246187300955)
XLA Ops:
  0.0 0.0 copy-start
  0.0 1.7 %dynamic-slice_convert_fusion.1 = (f32[2,2,32768]{2,1,0:T(2,128)S(1)}, f32[2,2,32768]{2,1,0:T(2,128)S(1)}) fusion(bf16[2,4,32768]{2,1,0:T(4,128)(2,1)} %param.7, s32[]{:T(128)S(6)} %select_n.65, s32[]{:T(128)S(6)} %select_n.67), kind=kLoop, calls=%fused_computation.56 | loop fusion | flops 262144 | bytes 1572872 | tf_op jit(solution)/shard_map/reshape | solution.py:100
  1.7 0.0 copy-start.2
  1.7 0.0 copy-start.3
  1.7 0.0 copy-start.1
  1.8 0.5 %reshape.155 = f32[2,2,32,1024]{3,2,1,0:T(8,128)S(1)} reshape(f32[2,2,32768]{2,1,0:T(2,128)S(1)} %get-tuple-element.27) | data formatting | bytes 1048576 | tf_op jit(solution)/shard_map/reshape | solution.py:97
  2.2 0.0 copy-start.4
  2.2 0.5 %collective-permute-start = (f32[2,2,32,1024]{3,2,1,0:T(8,128)S(1)}, f32[2,2,32,1024]{3,2,1,0:T(8,128)S(1)}, u32[]{:S(2)}, u32[]{:S(2)}) collective-permute-start(f32[2,2,32,1024]{3,2,1,0:T(8,128)S(1)} %reshape.155), channel_id=1, source_target_pairs={{0,1},{1,0},{2,3},{3,2},{4,5},{5,4},{6,7},{7,6},{8,9},{9,8},{10,11... | collective-permute-start | bytes 1572872 | tf_op jit(solution)/shard_map/ppermute | solution.py:98
  2.7 0.5 %reshape.153 = f32[2,2,32,1024]{3,2,1,0:T(8,128)S(1)} reshape(f32[2,2,32768]{2,1,0:T(2,128)S(1)} %get-tuple-element.26) | data formatting | bytes 1048576 | tf_op jit(solution)/shard_map/reshape | solution.py:100
  3.2 0.0 copy-done.2
  3.2 0.1 reshape.151
  3.4 0.0 copy-done.3
  3.4 0.5 %slice.144 = f32[1,1]{1,0:T(1,128)} slice(f32[16,1024]{1,0:T(8,128)S(1)} %copy-done.3), slice={[0:1], [0:1]} | slice | bytes 8 | tf_op jit(solution)/shard_map/slice | solution.py:108
  4.5 0.0 copy-done.1
  4.6 0.0 copy-done.4
  4.6 0.1 fusion.31
  4.7 0.0 collective-permute-done
  4.7 0.1 broadcast_select_fusion.1
  4.8 0.2 pad_maximum_fusion
  5.0 2.0 %fusion.20 = f32[2,2,64,1024]{3,2,1,0:T(8,128)S(1)} fusion(f32[2,2,32,1024]{3,2,1,0:T(8,128)S(1)} %get-tuple-element.23, f32[2,2,32,1024]{3,2,1,0:T(8,128)S(1)} %get-tuple-element.22, f32[1024]{0:T(1024)S(1)} %bitcast.62, f32[2,2,79,1024]{3,2,1,0:T(8,128)S(1)} %pad_maximum_fusion, f32[1024]{0:T(1024)S(1)} %bitcast.63, f32[1024]{0:T(1024)S(1)} %bitcast.49, ...), kind=kLoop, calls=%fused_computation.54 | loop fusion | flops 8912896 | bytes 17891328 | tf_op jit(solution)/shard_map/convert_element_type | solution.py:44
  7.1 0.1 fusion.23
  7.1 0.1 fusion.25
  7.2 0.2 fusion.38
  7.4 0.1 maximum_bitcast_fusion
  7.5 0.1 pad_maximum_fusion.1
  7.6 0.0 copy-start.5
  7.7 1.3 %convolution_convert_fusion.1 = bf16[256,1024]{1,0:T(8,128)(2,1)} fusion(bf16[512,256]{1,0:T(8,128)(2,1)S(1)} %broadcast_add_fusion, bf16[1024,512]{1,0:T(8,128)(2,1)S(1)} %bitcast.44), kind=kOutput, calls=%fused_computation.9 | convolution fusion | flops 268697600 | bytes 1835008 | tf_op jit(solution)/shard_map/dot_general | solution.py:64
  8.9 7.0 %all-to-all-start = ((bf16[16,16,1024]{2,1,0:T(8,128)(2,1)}), bf16[16,16,1024]{2,1,0:T(8,128)(2,1)S(1)}, u32[]{:S(2)}, u32[]{:S(2)}) async-start(bf16[16,16,1024]{2,1,0:T(8,128)(2,1)} %bitcast.22), calls=%async_computation | async-start | bytes 1048576 | tf_op jit(solution)/shard_map/all_to_all | solution.py:110
  16.0 0.0 copy-done.5
  16.0 0.6 %scatter_custom_fusion = s32[16]{0:T(128)S(1)} fusion(s32[16]{0:T(128)S(1)} %compare_select_fusion.1, s32[16]{0:T(128)S(1)} %iota.16, s32[]{:T(128)} %constant.45.clone.1), kind=kCustom, calls=%fused_computation.94 | custom fusion | bytes 68 | tf_op jit(solution)/shard_map/scatter | solution.py:114
  16.7 0.7 %gather_fusion = s32[32]{0:T(128)S(1)} fusion(s32[16]{0:T(128)S(1)} %scatter_custom_fusion, s32[1024]{0:T(1024)S(1)} %pad_clamp_fusion), kind=kCustom, calls=%fused_computation | custom fusion | bytes 384 | tf_op jit(solution)/shard_map/gather | solution.py:121
  17.4 0.0 copy-done
  17.4 0.7 %gather_fusion.1 = s32[32]{0:T(128)S(1)} fusion(s32[16]{0:T(128)S(1)} %copy-done, s32[1024]{0:T(1024)S(1)} %pad_clamp_fusion), kind=kCustom, calls=%fused_computation.1 | custom fusion | bytes 384 | tf_op jit(solution)/shard_map/gather | solution.py:123
  18.1 0.1 fusion.30
  18.1 12.3 %all-to-all-done = bf16[16,16,1024]{2,1,0:T(8,128)(2,1)S(1)} async-done(((bf16[16,16,1024]{2,1,0:T(8,128)(2,1)}), bf16[16,16,1024]{2,1,0:T(8,128)(2,1)S(1)}, u32[]{:S(2)}, u32[]{:S(2)}) %all-to-all-start) | async-done | bytes 524320 | tf_op jit(solution)/shard_map/all_to_all | solution.py:110
  30.4 0.1 copy.13
  30.5 0.3 copy.11
  30.9 0.3 convolution_convert_fusion
  31.2 0.2 slice_negate_fusion
  31.4 0.4 %convolution_bitcast_fusion.1 = f32[1,64,32,32]{3,2,1,0:T(8,128)S(1)} fusion(bf16[64,32,128]{2,1,0:T(8,128)(2,1)S(1)} %convolution_convert_fusion), kind=kOutput, calls=%fused_computation.6 | convolution fusion | flops 16777216 | bytes 786432 | tf_op jit(solution)/shard_map/cak,cbk->cab/dot_general | solution.py:80
  31.8 0.5 %convolution_bitcast_fusion = f32[1,64,32,32]{3,2,1,0:T(8,128)S(1)} fusion(bf16[64,32,128]{2,1,0:T(8,128)(2,1)S(1)} %convolution_convert_fusion, bf16[64,32,64]{2,1,0:T(8,128)(2,1)S(1)} %get-tuple-element.25, bf16[64,32,64]{2,1,0:T(8,128)(2,1)S(1)} %get-tuple-element.24), kind=kOutput, calls=%fused_computation.5 | convolution fusion | flops 17825792 | bytes 1310720 | tf_op jit(solution)/shard_map/cak,cbk->cab/dot_general | solution.py:81
  32.3 0.3 fusion
  32.5 1.9 %copy.12 = bf16[2,64,32,32]{1,3,2,0:T(8,128)(2,1)} copy(bf16[2,64,32,32]{3,2,1,0:T(8,128)(2,1)S(1)} %fusion) | data formatting | bytes 524288 | tf_op jit(solution)/shard_map/layout_constraint | solution.py:129
  (10 shorter events, 0.2 us)
Async XLA Ops:
  0.0 17.4 %copy-start = (s32[16]{0:T(128)S(1)}, s32[16]{0:T(128)}, u32[]{:S(2)}) copy-start(s32[16]{0:T(128)} %param.11) | copy-start | bytes 196
  1.7 1.5 %copy-start.2 = (bf16[2,4,15360]{2,1,0:T(4,128)(2,1)S(1)}, bf16[2,4,15360]{2,1,0:T(4,128)(2,1)}, u32[]{:S(2)}) copy-start(bf16[2,4,15360]{2,1,0:T(4,128)(2,1)} %param.8) | copy-start | bytes 737284
  1.7 1.6 %copy-start.3 = (f32[16,1024]{1,0:T(8,128)S(1)}, f32[16,1024]{1,0:T(8,128)}, u32[]{:S(2)}) copy-start(f32[16,1024]{1,0:T(8,128)} %param.9) | copy-start | bytes 196612
  1.7 2.8 %copy-start.1 = (bf16[512,256]{1,0:T(8,128)(2,1)S(1)}, bf16[512,256]{1,0:T(8,128)(2,1)}, u32[]{:S(2)}) copy-start(bf16[512,256]{1,0:T(8,128)(2,1)} %constant.56.clone) | copy-start | bytes 786436
  2.2 2.4 %copy-start.4 = (f32[4,256]{1,0:T(4,128)S(1)}, f32[4,256]{1,0:T(4,128)}, u32[]{:S(2)}) copy-start(f32[4,256]{1,0:T(4,128)} %constant.55.clone) | copy-start | bytes 12292
  2.2 2.5 %collective-permute-start = (f32[2,2,32,1024]{3,2,1,0:T(8,128)S(1)}, f32[2,2,32,1024]{3,2,1,0:T(8,128)S(1)}, u32[]{:S(2)}, u32[]{:S(2)}) collective-permute-start(f32[2,2,32,1024]{3,2,1,0:T(8,128)S(1)} %reshape.155), channel_id=1, source_target_pairs={{0,1},{1,0},{2,3},{3,2},{4,5},{5,4},{6,7},{7,6},{8,9},{9,8},{10,11... | collective-permute-start | bytes 1572872 | tf_op jit(solution)/shard_map/ppermute | solution.py:98
  7.6 8.3 %copy-start.5 = (s32[16]{0:T(128)S(1)}, s32[16]{0:T(128)}, u32[]{:S(2)}) copy-start(s32[16]{0:T(128)} %param.10) | copy-start | bytes 196
  8.9 21.5 %all-to-all-start = ((bf16[16,16,1024]{2,1,0:T(8,128)(2,1)}), bf16[16,16,1024]{2,1,0:T(8,128)(2,1)S(1)}, u32[]{:S(2)}, u32[]{:S(2)}) async-start(bf16[16,16,1024]{2,1,0:T(8,128)(2,1)} %bitcast.22), calls=%async_computation | async-start | bytes 1048576 | tf_op jit(solution)/shard_map/all_to_all | solution.py:110
